TPU v7x, 256 devices: a whole 4x4x8 slice. The times are simulated.
256 devices in a mesh: scale: 16 (over x_hi, y, core), rt: 16 (over z, x_lo).
Axes of the slice: x: 4 (x_hi: 2, x_lo: 2; x = x_hi * 2 + x_lo), y: 4, z: 8, core: 2. Of those that a mesh axis runs over, the one named last changes fastest.
Arguments:
- slab: float32 [384, 128, 896], P('rt'), may hold values from -6 to 6
- widths: int32 [16], replicated, may hold values from 1 to 8
Outputs:
- peak: bfloat16 [384, 128, 896], P('rt', 'scale')
- energy: float32 [384, 128, 896], P('rt', 'scale')
All inputs are finite; a program needn't handle non-finite values.
Results may differ from a plain program's by a relative error of at most 0.006.
Values may be sent and summed in bfloat16 or wider, within the bound.
No kernel may reach another device: no remote copies, remote signals or barrier semaphores. Data moves between devices by JAX's collectives and lax.ppermute only.
A program may use at most 128 MiB of HBM per device.

v0:
```python
import jax
import jax.numpy as jnp
from jax import lax
from jax.sharding import PartitionSpec as P

SC_DEV = 1
SCAN_RATIO = 16


def padded_2(block, sides, width):
    for axis, dim in sides:
        count = lax.axis_size(axis)
        forward = [(i, i + 1) for i in range(count - 1)]
        backward = [(target, source) for source, target in forward]
        low = lax.ppermute(
            lax.slice_in_dim(block, block.shape[dim] - width, None, axis=dim), axis, forward
        )
        high = lax.ppermute(lax.slice_in_dim(block, 0, width, axis=dim), axis, backward)
        block = jnp.concatenate([low, block, high], axis=dim)
    return block


def mexican(offsets, spread):
    ratio = offsets / spread
    return (1.0 - ratio * ratio) * jnp.exp(-0.5 * ratio * ratio) / jnp.sqrt(spread)


def scan_offsets(scan_count):
    positions = jnp.arange(scan_count, dtype=jnp.float32)
    return positions[:, None] - positions[None, :]


def frame_table(frame_rows, scale_width):
    out_pos = jnp.arange(frame_rows, dtype=jnp.float32)
    in_pos = jnp.arange(3 * frame_rows, dtype=jnp.float32)
    offsets = in_pos[None, :] - frame_rows - out_pos[:, None]
    values = jnp.where(jnp.abs(offsets) <= frame_rows, mexican(offsets, scale_width), 0.0)
    return values.astype(jnp.bfloat16)


def per_device(slab, widths):
    frame_rows, mz_bins, scan_count = slab.shape
    scan_diff = scan_offsets(scan_count)
    signal = slab.astype(jnp.bfloat16).reshape(frame_rows * mz_bins, scan_count)
    first_scale = lax.axis_index("scale") * SC_DEV
    scale_width = lax.dynamic_slice_in_dim(widths, first_scale + 0, 1)[0].astype(jnp.float32)
    scan_table = mexican(scan_diff, SCAN_RATIO * scale_width).astype(jnp.bfloat16)
    smooth = jnp.dot(signal, scan_table, preferred_element_type=jnp.float32).astype(jnp.bfloat16)
    smooth = smooth.reshape(frame_rows, mz_bins, scan_count)
    padded = padded_2(smooth, (("rt", 0),), frame_rows)
    answer = jnp.dot(
        frame_table(frame_rows, scale_width),
        padded.reshape(3 * frame_rows, -1),
        preferred_element_type=jnp.float32,
    )
    answers = [answer.astype(jnp.bfloat16).reshape(frame_rows, mz_bins, scan_count)]
    stacked = jnp.stack(answers, axis=0)
    block = lax.all_to_all(stacked, "scale", split_axis=2, concat_axis=0, tiled=True)
    peak = jnp.max(block, axis=0)
    energy = jnp.sum(jnp.square(block.astype(jnp.float32)), axis=0)
    return (peak, energy)


def solution(mesh):
    in_specs = (P("rt", None, None), P())
    out_specs = (P("rt", "scale", None), P("rt", "scale", None))
    return jax.shard_map(
        per_device, mesh=mesh, in_specs=in_specs, out_specs=out_specs, check_vma=False
    )
```

profile of v0, /device:TPU:136, one launch (start us, length us, event | category | flops | bytes accessed | tf_op | source)
XLA Modules:
  0.0 375.8 jit_solution(3813570479904891257)
XLA Ops:
  0.6 1.2 dynamic_slice.3
  2.6 5.0 %convert_element_type.32 = bf16[24,128,896]{2,1,0:T(8,128)(2,1)S(1)} convert(f32[24,128,896]{2,1,0:T(8,128)} %param.2) | non-fusion elementwise | flops 2752512 | bytes 16515072 | tf_op jit(solution)/shard_map/convert_element_type | solution.py:44
  7.6 9.1 %convert_bitcast_fusion = bf16[3072,896]{0,1:T(8,128)(2,1)} fusion(bf16[3072,896]{1,0:T(8,128)(2,1)S(1)} %bitcast.24, f32[]{:T(128)S(6)} %sqrt.7, f32[]{:T(128)S(6)} %mul_shard_map.3), kind=kOutput, calls=%fused_computation.7 | convolution fusion | flops 4942479360 | bytes 11010056 | tf_op jit(solution)/shard_map/dot_general | solution.py:48
  16.7 8.0 %copy.17 = bf16[3072,896]{1,0:T(8,128)(2,1)} copy(bf16[3072,896]{0,1:T(8,128)(2,1)} %convert_bitcast_fusion) | data formatting | bytes 11010048 | tf_op jit(solution)/shard_map/reshape | solution.py:49
  24.7 2.9 collective-permute-start.1
  27.7 3.1 collective-permute-start
  30.7 7.2 %concatenate.11 = bf16[24,114688]{1,0:T(8,128)(2,1)} reshape(bf16[3072,896]{1,0:T(8,128)(2,1)} %copy.17) | data formatting | bytes 11010048 | tf_op jit(solution)/shard_map/concatenate | solution.py:19
  38.0 227.2 %collective-permute-done.1 = bf16[24,128,896]{2,1,0:T(8,128)(2,1)} collective-permute-done((bf16[24,128,896]{2,1,0:T(8,128)(2,1)}, bf16[24,128,896]{2,1,0:T(8,128)(2,1)}, u32[]{:S(2)}, u32[]{:S(2)}) %collective-permute-start.1) | collective-permute-done | bytes 5505056 | tf_op jit(solution)/shard_map/ppermute | solution.py:18
  265.3 8.2 %copy.19 = bf16[3,8,128,896]{3,1,2,0:T(8,128)(2,1)} copy(bf16[3,8,128,896]{3,2,1,0:T(8,128)(2,1)} %bitcast.9) | data formatting | bytes 11010048
  273.4 0.0 collective-permute-done
  273.4 8.1 %copy.18 = bf16[3,8,128,896]{3,1,2,0:T(8,128)(2,1)} copy(bf16[3,8,128,896]{3,2,1,0:T(8,128)(2,1)} %bitcast.7) | data formatting | bytes 11010048
  281.5 8.8 %convolution_convert_fusion = bf16[24,114688]{1,0:T(8,128)(2,1)} fusion(bf16[24,114688]{1,0:T(8,128)(2,1)} %bitcast.21, bf16[24,114688]{1,0:T(8,128)(2,1)} %concatenate.11, bf16[24,114688]{1,0:T(8,128)(2,1)} %bitcast.22, f32[]{:T(128)S(6)} %sqrt.6, f32[]{:T(128)} %bitcast, f32[72]{0:T(128)S(1)} %iota_add_fusion), kind=kOutput, calls=%fused_computation | convolution fusion | flops 448680192 | bytes 22020392 | tf_op jit(solution)/shard_map/dot_general | solution.py:51
  290.4 3.6 copy.20
  293.9 3.2 copy.14
  297.1 70.2 %all_to_all.15 = bf16[1,24,128,896]{3,1,0,2:T(8,128)(2,1)S(1)} all-to-all(bf16[1,24,128,896]{3,1,0,2:T(8,128)(2,1)S(1)} %copy.14), channel_id=1, replica_groups=mesh['scale'=16,'rt'=16] {'scale'}, dimensions={2} | all-to-all | bytes 11010048 | tf_op jit(solution)/shard_map/all_to_all | solution.py:58
  367.3 0.0 copy-start
  367.3 2.4 copy-done
  369.7 1.1 multiply_reduce_fusion
  370.7 1.0 copy.16
  371.7 3.3 reduce_max.9
  375.0 0.8 copy.15
  (1 shorter events, 0.0 us)
Async XLA Ops:
  24.7 240.6 %collective-permute-start.1 = (bf16[24,128,896]{2,1,0:T(8,128)(2,1)}, bf16[24,128,896]{2,1,0:T(8,128)(2,1)}, u32[]{:S(2)}, u32[]{:S(2)}) collective-permute-start(bf16[24,128,896]{2,1,0:T(8,128)(2,1)} %bitcast.18), channel_id=1, source_target_pairs={{1,0},{2,1},{3,2},{4,3},{5,4},{6,5},{7,6},{8,7},{9,8},{10,9},{11,1... | collective-permute-start | bytes 16515080 | tf_op jit(solution)/shard_map/ppermute | solution.py:18
  27.7 245.8 %collective-permute-start = (bf16[24,128,896]{2,1,0:T(8,128)(2,1)}, bf16[24,128,896]{2,1,0:T(8,128)(2,1)}, u32[]{:S(2)}, u32[]{:S(2)}) collective-permute-start(bf16[24,128,896]{2,1,0:T(8,128)(2,1)} %bitcast.19), channel_id=1, source_target_pairs={{0,1},{1,2},{2,3},{3,4},{4,5},{5,6},{6,7},{7,8},{8,9},{9,10},{10,1... | collective-permute-start | bytes 16515080 | tf_op jit(solution)/shard_map/ppermute | solution.py:15
  367.3 2.4 copy-start
where the time goes:
time: 379 us; the launch traced here: 376 us
  waiting for transfers between devices  227 us (60%)
  blocking collectives  70.2 us (19%)
  local copies, waits for them, and re-layouts  43.6 us (12%)
  matrix products  17.9 us (5%)
  other arithmetic  9.47 us (2%)
  starting transfers between devices  6.01 us (2%)
    ppermute x1, waiting for transfers between devices, padded_2(): lax.ppermute(lax.slice_in_dim(block, 0, width, axis=dim), axis, backward)  227 us
    all_to_all x1, blocking collectives, per_device(): lax.all_to_all(stacked, 'scale', split_axis=2, concat_axis=0, tiled=True)  70.2 us
    unnamed x7, local copies, waits for them, and re-layouts  23.9 us
    dot_general x1, matrix products, per_device(): jnp.dot(signal, scan_table, preferred_element_type=jnp.float32)  9.06 us
    dot_general x1, matrix products, per_device(): jnp.dot(frame_table(frame_rows, scale_width), padded.reshape(3 * frame_ro...  8.84 us
    reshape x1, local copies, waits for them, and re-layouts, per_device(): smooth = smooth.reshape(frame_rows, mz_bins, scan_count)  8.02 us
  transfers between devices with their start and end apart: 2, of which 1 were waited for; matrix products, arithmetic and copies ran while one was open for 4% of the time, Pallas kernels for 0%

commit v1 on v0

v1 whole, which is shorter than its diff:
```python
import jax
import jax.numpy as jnp
from jax import lax
from jax.sharding import PartitionSpec as P

SCAN_RATIO = 16
HALO = 24


def mexican(offsets, spread):
    ratio = offsets / spread
    return (1.0 - ratio * ratio) * jnp.exp(-0.5 * ratio * ratio) / jnp.sqrt(spread)


def neighbours(block, axis):
    count = lax.axis_size(axis)
    forward = [(i, i + 1) for i in range(count - 1)]
    backward = [(i + 1, i) for i in range(count - 1)]
    frames = block.shape[0]
    low = lax.ppermute(lax.slice_in_dim(block, frames - HALO, frames, axis=0), axis, forward)
    high = lax.ppermute(lax.slice_in_dim(block, 0, HALO, axis=0), axis, backward)
    return low, high


def frame_tables(frames, scale_widths):
    out_pos = jnp.arange(frames, dtype=jnp.float32)
    in_pos = jnp.arange(frames + 2 * HALO, dtype=jnp.float32) - HALO
    offsets = (in_pos[None, :] - out_pos[:, None])[None]
    spread = scale_widths[:, None, None]
    values = jnp.where(jnp.abs(offsets) <= HALO, mexican(offsets, spread), 0.0)
    return values.astype(jnp.bfloat16)


def scan_tables(scans, scale_widths):
    positions = jnp.arange(scans, dtype=jnp.float32)
    offsets = (positions[:, None] - positions[None, :])[None]
    spread = SCAN_RATIO * scale_widths[:, None, None]
    return mexican(offsets, spread).astype(jnp.bfloat16)


def per_device(slab, widths):
    frames, mz_bins, scans = slab.shape
    strip = mz_bins // lax.axis_size("scale")
    first = lax.axis_index("scale") * strip
    signal = lax.dynamic_slice_in_dim(slab, first, strip, axis=1).astype(jnp.bfloat16)
    low, high = neighbours(signal, "rt")
    padded = jnp.concatenate([low, signal, high], axis=0).reshape(frames + 2 * HALO, strip * scans)
    scale_widths = widths.astype(jnp.float32)
    count = scale_widths.shape[0]
    framed = jnp.einsum(
        "cfj,jn->cfn", frame_tables(frames, scale_widths), padded, preferred_element_type=jnp.float32
    ).astype(jnp.bfloat16)
    framed = framed.reshape(count, frames * strip, scans)
    answer = jnp.einsum(
        "cms,cst->cmt", framed, scan_tables(scans, scale_widths), preferred_element_type=jnp.float32
    ).astype(jnp.bfloat16)
    peak = jnp.max(answer, axis=0).reshape(frames, strip, scans)
    energy = jnp.sum(jnp.square(answer.astype(jnp.float32)), axis=0).reshape(frames, strip, scans)
    return (peak, energy)


def solution(mesh):
    in_specs = (P("rt", None, None), P())
    out_specs = (P("rt", "scale", None), P("rt", "scale", None))
    return jax.shard_map(
        per_device, mesh=mesh, in_specs=in_specs, out_specs=out_specs, check_vma=False
    )
```

time: 379 us -> 60.8 us (0.16)
  the two profiles are of different devices: /device:TPU:136 before, /device:TPU:115 now
where the time goes in v1:
time: 60.8 us; the launch traced here: 60.4 us
  matrix products  25.6 us (42%)
  local copies, waits for them, and re-layouts  10.8 us (18%)
  waiting for transfers between devices  10.5 us (17%)
  starting transfers between devices  7.39 us (12%)
  other arithmetic  5.53 us (9%)
  between operations  0.68 us (1%)
    dot_general x1, matrix products, per_device(): jnp.einsum('cms,cst->cmt', framed, scan_tables(scans, scale_widths), pref...  21.5 us
    reshape x1, local copies, waits for them, and re-layouts, per_device(): framed = framed.reshape(count, frames * strip, scans)  9.14 us
    ppermute x1, waiting for transfers between devices, neighbours(): lax.ppermute(lax.slice_in_dim(block, 0, HALO, axis=0), axis, backward)  5.39 us
    ppermute x1, starting transfers between devices, neighbours(): lax.ppermute(lax.slice_in_dim(block, frames - HALO, frames, axis=0), axis...  5.23 us
    ppermute x1, waiting for transfers between devices, neighbours(): lax.ppermute(lax.slice_in_dim(block, frames - HALO, frames, axis=0), axis...  5.09 us
    dot_general x1, matrix products, per_device(): jnp.einsum('cfj,jn->cfn', frame_tables(frames, scale_widths), padded, pre...  4.12 us
    ppermute x1, starting transfers between devices, neighbours(): lax.ppermute(lax.slice_in_dim(block, 0, HALO, axis=0), axis, backward)  2.16 us
    sub x1, other arithmetic, scan_tables(): offsets = (positions[:, None] - positions[None, :])[None]  2.1 us
  transfers between devices with their start and end apart: 2, of which 2 were waited for; matrix products, arithmetic and copies ran while one was open for 6% of the time, Pallas kernels for 0%

profile of v1, /device:TPU:115, one launch (start us, length us, event | category | flops | bytes accessed | tf_op | source)
XLA Modules:
  0.0 60.4 jit_solution(2215259543414273592)
XLA Ops:
  0.6 1.1 %dynamic-slice_convert_fusion = bf16[24,8,896]{2,1,0:T(8,128)(2,1)S(1)} fusion(f32[24,128,896]{2,1,0:T(8,128)} %param.2, s32[]{:T(128)S(6)} %select_n.8), kind=kLoop, calls=%fused_computation.11 | loop fusion | bytes 688132 | tf_op jit(solution)/shard_map/convert_element_type | solution.py:45
  1.8 2.2 %collective-permute-start.1 = (bf16[24,8,896]{2,1,0:T(8,128)(2,1)S(1)}, bf16[24,8,896]{2,1,0:T(8,128)(2,1)S(1)}, u32[]{:S(2)}, u32[]{:S(2)}) collective-permute-start(bf16[24,8,896]{2,1,0:T(8,128)(2,1)S(1)} %dynamic-slice_convert_fusion), channel_id=1, source_target_pairs={{1,0},{2,1},{3,2},{4,3},{5,4},{6,5},{7,6},{8,7},{9,8},{10,9},{11,1... | collective-permute-start | bytes 1032200 | tf_op jit(solution)/shard_map/ppermute | solution.py:21
  4.0 5.2 %collective-permute-start = (bf16[24,8,896]{2,1,0:T(8,128)(2,1)S(1)}, bf16[24,8,896]{2,1,0:T(8,128)(2,1)S(1)}, u32[]{:S(2)}, u32[]{:S(2)}) collective-permute-start(bf16[24,8,896]{2,1,0:T(8,128)(2,1)S(1)} %dynamic-slice_convert_fusion), channel_id=1, source_target_pairs={{0,1},{1,2},{2,3},{3,4},{4,5},{5,6},{6,7},{7,8},{8,9},{9,10},{10,1... | collective-permute-start | bytes 1032200 | tf_op jit(solution)/shard_map/ppermute | solution.py:20
  9.2 0.7 %convert_element_type.21 = f32[16]{0:T(128)S(1)} convert(s32[16]{0:T(128)} %param.3) | non-fusion elementwise | flops 16 | bytes 128 | tf_op jit(solution)/shard_map/convert_element_type | solution.py:48
  9.9 0.7 %broadcast_multiply_fusion = (f32[16]{0:T(128)S(1)}, f32[16]{0:T(128)S(1)}, f32[16]{0:T(128)S(1)}) fusion(s32[16]{0:T(128)} %param.3), kind=kLoop, calls=%fused_computation.28 | loop fusion | flops 32 | bytes 256 | tf_op jit(solution)/shard_map/mul | solution.py:37
  10.5 2.1 %iota_subtract_fusion = f32[896,896]{1,0:T(8,128)} fusion(), kind=kLoop, calls=%fused_computation.8 | loop fusion | flops 802816 | bytes 3211264 | tf_op jit(solution)/shard_map/sub | solution.py:36
  12.7 5.4 %collective-permute-done.1 = bf16[24,8,896]{2,1,0:T(8,128)(2,1)S(1)} collective-permute-done((bf16[24,8,896]{2,1,0:T(8,128)(2,1)S(1)}, bf16[24,8,896]{2,1,0:T(8,128)(2,1)S(1)}, u32[]{:S(2)}, u32[]{:S(2)}) %collective-permute-start.1) | collective-permute-done | bytes 344096 | tf_op jit(solution)/shard_map/ppermute | solution.py:21
  18.0 5.1 %collective-permute-done = bf16[24,8,896]{2,1,0:T(8,128)(2,1)S(1)} collective-permute-done((bf16[24,8,896]{2,1,0:T(8,128)(2,1)S(1)}, bf16[24,8,896]{2,1,0:T(8,128)(2,1)S(1)}, u32[]{:S(2)}, u32[]{:S(2)}) %collective-permute-start) | collective-permute-done | bytes 344096 | tf_op jit(solution)/shard_map/ppermute | solution.py:20
  23.1 0.1 pad_maximum_fusion
  23.3 0.5 reshape.85
  23.8 4.1 %convolution_convert_fusion = bf16[16,24,7168]{2,1,0:T(8,128)(2,1)} fusion(bf16[72,7168,1]{1,0,2:T(8,128)(2,1)S(1)} %reshape.85, f32[16]{0:T(128)S(1)} %get-tuple-element.4, f32[16]{0:T(128)S(1)} %convert_element_type.21, f32[24,72]{1,0:T(8,128)S(1)} %iota_subtract_fusion.1, pred[24,72]{1,0:T(8,128)(4,1)S(1)} %abs_compare_fusion), kind=kOutput, calls=%fused_computation.7 | convolution fusion | flops 399363072 | bytes 6545984 | tf_op jit(solution)/shard_map/cfj,jn->cfn/dot_general | solution.py:50
  27.9 0.0 copy-start
  27.9 9.1 %reshape.82 = bf16[16,192,896]{2,1,0:T(8,128)(2,1)} reshape(bf16[16,24,7168]{2,1,0:T(8,128)(2,1)} %convolution_convert_fusion) | data formatting | bytes 11010048 | tf_op jit(solution)/shard_map/reshape | solution.py:53
  37.0 0.0 copy-done
  37.0 21.5 %fusion.28 = (bf16[192,896]{1,0:T(8,128)(2,1)}, bf16[16,192,896]{2,1,0:T(8,128)(2,1)S(1)}) fusion(bf16[16,192,896]{2,1,0:T(8,128)(2,1)} %reshape.82, f32[16]{0:T(128)S(1)} %get-tuple-element.3, f32[16]{0:T(128)S(1)} %get-tuple-element.2, f32[896,896]{1,0:T(8,128)S(1)} %copy-done), kind=kOutput, calls=%fused_computation.36 | convolution fusion | flops 5040594944 | bytes 14565504 | tf_op jit(solution)/shard_map/cms,cst->cmt/dot_general | solution.py:54
  58.5 1.9 %multiply_reduce_fusion = f32[192,896]{1,0:T(8,128)} fusion(bf16[16,192,896]{2,1,0:T(8,128)(2,1)S(1)} %get-tuple-element.6), kind=kLoop, calls=%fused_computation.6 | loop fusion | flops 8085504 | bytes 6193152 | tf_op jit(solution)/shard_map/reduce_sum | solution.py:58
  (3 shorter events, 0.0 us)
Async XLA Ops:
  1.8 16.3 %collective-permute-start.1 = (bf16[24,8,896]{2,1,0:T(8,128)(2,1)S(1)}, bf16[24,8,896]{2,1,0:T(8,128)(2,1)S(1)}, u32[]{:S(2)}, u32[]{:S(2)}) collective-permute-start(bf16[24,8,896]{2,1,0:T(8,128)(2,1)S(1)} %dynamic-slice_convert_fusion), channel_id=1, source_target_pairs={{1,0},{2,1},{3,2},{4,3},{5,4},{6,5},{7,6},{8,7},{9,8},{10,9},{11,1... | collective-permute-start | bytes 1032200 | tf_op jit(solution)/shard_map/ppermute | solution.py:21
  4.0 19.2 %collective-permute-start = (bf16[24,8,896]{2,1,0:T(8,128)(2,1)S(1)}, bf16[24,8,896]{2,1,0:T(8,128)(2,1)S(1)}, u32[]{:S(2)}, u32[]{:S(2)}) collective-permute-start(bf16[24,8,896]{2,1,0:T(8,128)(2,1)S(1)} %dynamic-slice_convert_fusion), channel_id=1, source_target_pairs={{0,1},{1,2},{2,3},{3,4},{4,5},{5,6},{6,7},{7,8},{8,9},{9,10},{10,1... | collective-permute-start | bytes 1032200 | tf_op jit(solution)/shard_map/ppermute | solution.py:20
  27.9 9.1 %copy-start = (f32[896,896]{1,0:T(8,128)S(1)}, f32[896,896]{1,0:T(8,128)}, u32[]{:S(2)}) copy-start(f32[896,896]{1,0:T(8,128)} %iota_subtract_fusion) | copy-start | bytes 9633796

commit v2 on v1

v2 whole, which is shorter than its diff:
```python
import jax
import jax.numpy as jnp
from jax import lax
from jax.experimental import pallas as pl
from jax.experimental.pallas import tpu as pltpu
from jax.sharding import PartitionSpec as P

SCAN_RATIO = 16
HALO = 24
TILE = 128


def mexican(offsets, spread):
    ratio = offsets / spread
    return (1.0 - ratio * ratio) * jnp.exp(-0.5 * ratio * ratio) / jnp.sqrt(spread)


def neighbours(block, axis):
    count = lax.axis_size(axis)
    forward = [(i, i + 1) for i in range(count - 1)]
    backward = [(i + 1, i) for i in range(count - 1)]
    frames = block.shape[0]
    low = lax.ppermute(lax.slice_in_dim(block, frames - HALO, frames, axis=0), axis, forward)
    high = lax.ppermute(lax.slice_in_dim(block, 0, HALO, axis=0), axis, backward)
    return low, high


def frame_tables(frames, scale_widths, depth):
    out_pos = jnp.arange(frames, dtype=jnp.float32)
    in_pos = jnp.arange(depth, dtype=jnp.float32) - HALO
    offsets = (in_pos[None, :] - out_pos[:, None])[None]
    spread = scale_widths[:, None, None]
    inside = (jnp.abs(offsets) <= HALO) & (in_pos < frames + HALO)[None, None, :]
    values = jnp.where(inside, mexican(offsets, spread), 0.0)
    return values.astype(jnp.bfloat16).reshape(-1, depth)


def scan_blocks(scans, scale_widths):
    nb = scans // TILE
    shift = (jnp.arange(2 * nb - 1, dtype=jnp.float32) - (nb - 1)) * TILE
    pos = jnp.arange(TILE, dtype=jnp.float32)
    offsets = shift[:, None, None] + (pos[:, None] - pos[None, :])[None]
    spread = SCAN_RATIO * scale_widths[:, None, None, None]
    return mexican(offsets[None], spread).astype(jnp.bfloat16)


def wavelet_kernel(f_ref, p_ref, b_ref, peak_ref, energy_ref, g_scr, s_scr):
    c = pl.program_id(0)
    count, rows, scans = g_scr.shape
    frames = f_ref.shape[0] // count
    strip = rows // frames
    nb = scans // TILE

    @pl.when(c == 0)
    def _():
        fall = f_ref[...]
        for m in range(strip):
            gm = jnp.dot(fall, p_ref[:, m * scans:(m + 1) * scans], preferred_element_type=jnp.float32)
            for cc in range(count):
                g_scr[cc, m * frames:(m + 1) * frames, :] = gm[cc * frames:(cc + 1) * frames, :]

    for i in range(nb):
        for j in range(nb):
            s_scr[i * TILE:(i + 1) * TILE, j * TILE:(j + 1) * TILE] = b_ref[0, i - j + nb - 1]
    lhs = g_scr[c].astype(jnp.bfloat16)
    answer = jnp.dot(lhs, s_scr[...], preferred_element_type=jnp.float32).astype(jnp.bfloat16)
    square = jnp.square(answer.astype(jnp.float32))

    @pl.when(c == 0)
    def _():
        peak_ref[...] = answer
        energy_ref[...] = square

    @pl.when(c > 0)
    def _():
        peak_ref[...] = jnp.maximum(peak_ref[...], answer)
        energy_ref[...] = energy_ref[...] + square


def wavelet_core(ftab, padded, blocks, frames, strip, scans, interpret=False):
    count = blocks.shape[0]
    depth = padded.shape[0]
    rows = frames * strip
    nblk = blocks.shape[1]
    return pl.pallas_call(
        wavelet_kernel,
        grid=(count,),
        in_specs=[
            pl.BlockSpec((count * frames, depth), lambda c: (0, 0)),
            pl.BlockSpec((depth, strip * scans), lambda c: (0, 0)),
            pl.BlockSpec((1, nblk, TILE, TILE), lambda c: (c, 0, 0, 0)),
        ],
        out_specs=[
            pl.BlockSpec((rows, scans), lambda c: (0, 0)),
            pl.BlockSpec((rows, scans), lambda c: (0, 0)),
        ],
        out_shape=[
            jax.ShapeDtypeStruct((rows, scans), jnp.bfloat16),
            jax.ShapeDtypeStruct((rows, scans), jnp.float32),
        ],
        scratch_shapes=[
            pltpu.VMEM((count, rows, scans), jnp.float32),
            pltpu.VMEM((scans, scans), jnp.bfloat16),
        ],
        compiler_params=pltpu.CompilerParams(
            dimension_semantics=("arbitrary",), vmem_limit_bytes=56 * 1024 * 1024
        ),
        interpret=interpret,
    )(ftab, padded, blocks)


def compute(signal, low, high, widths, interpret=False):
    frames, strip, scans = signal.shape
    depth = -(-(frames + 2 * HALO) // TILE) * TILE
    pad = jnp.zeros((depth - frames - 2 * HALO, strip, scans), signal.dtype)
    padded = jnp.concatenate([low, signal, high, pad], axis=0).reshape(depth, strip * scans)
    scale_widths = widths.astype(jnp.float32)
    ftab = frame_tables(frames, scale_widths, depth)
    blocks = scan_blocks(scans, scale_widths)
    peak, energy = wavelet_core(ftab, padded, blocks, frames, strip, scans, interpret)
    peak = peak.reshape(strip, frames, scans).transpose(1, 0, 2)
    energy = energy.reshape(strip, frames, scans).transpose(1, 0, 2)
    return peak, energy


def per_device(slab, widths):
    frames, mz_bins, scans = slab.shape
    strip = mz_bins // lax.axis_size("scale")
    first = lax.axis_index("scale") * strip
    signal = lax.dynamic_slice_in_dim(slab, first, strip, axis=1).astype(jnp.bfloat16)
    low, high = neighbours(signal, "rt")
    return compute(signal, low, high, widths)


def solution(mesh):
    in_specs = (P("rt", None, None), P())
    out_specs = (P("rt", "scale", None), P("rt", "scale", None))
    return jax.shard_map(
        per_device, mesh=mesh, in_specs=in_specs, out_specs=out_specs, check_vma=False
    )
```

time: 60.8 us -> 47.9 us (0.79)
  the two profiles are of different devices: /device:TPU:115 before, /device:TPU:111 now
where the time goes in v2:
time: 47.9 us; the launch traced here: 47.3 us
  Pallas kernels  18.5 us (39%)
  other arithmetic  8.67 us (18%)
  starting transfers between devices  7.39 us (15%)
  local copies, waits for them, and re-layouts  6.98 us (15%)
  waiting for transfers between devices  5.09 us (11%)
  between operations  0.72 us (2%)
    pallas_call x1, Pallas kernels, wavelet_core(): pl.pallas_call(wavelet_kernel, grid=(count,), in_specs=[pl.BlockSpec((cou...  18.5 us
    convert_element_type x1, other arithmetic, scan_blocks(): return mexican(offsets[None], spread).astype(jnp.bfloat16)  6.07 us
    ppermute x1, starting transfers between devices, neighbours(): lax.ppermute(lax.slice_in_dim(block, frames - HALO, frames, axis=0), axis...  4.94 us
    ppermute x1, waiting for transfers between devices, neighbours(): lax.ppermute(lax.slice_in_dim(block, frames - HALO, frames, axis=0), axis...  4.8 us
    ppermute x1, starting transfers between devices, neighbours(): lax.ppermute(lax.slice_in_dim(block, 0, HALO, axis=0), axis, backward)  2.46 us
    reshape x1, local copies, waits for them, and re-layouts, compute(): energy = energy.reshape(strip, frames, scans).transpose(1, 0, 2)  2.08 us
    reshape x1, local copies, waits for them, and re-layouts, compute(): peak = peak.reshape(strip, frames, scans).transpose(1, 0, 2)  1.74 us
    unnamed x1, local copies, waits for them, and re-layouts  1.61 us
  transfers between devices with their start and end apart: 2, of which 2 were waited for; matrix products, arithmetic and copies ran while one was open for 19% of the time, Pallas kernels for 0%

profile of v2, /device:TPU:111, one launch (start us, length us, event | category | flops | bytes accessed | tf_op | source)
XLA Modules:
  0.0 47.3 jit_solution(3235007092953004480)
XLA Ops:
  0.6 1.1 %dynamic-slice_convert_fusion = bf16[24,8,896]{2,1,0:T(8,128)(2,1)S(1)} fusion(f32[24,128,896]{2,1,0:T(8,128)} %param.2, s32[]{:T(128)S(6)} %select_n.9), kind=kLoop, calls=%fused_computation.7 | loop fusion | bytes 688132 | tf_op jit(solution)/shard_map/convert_element_type | solution.py:130
  1.8 2.5 %collective-permute-start.1 = (bf16[24,8,896]{2,1,0:T(8,128)(2,1)S(1)}, bf16[24,8,896]{2,1,0:T(8,128)(2,1)S(1)}, u32[]{:S(2)}, u32[]{:S(2)}) collective-permute-start(bf16[24,8,896]{2,1,0:T(8,128)(2,1)S(1)} %dynamic-slice_convert_fusion), channel_id=1, source_target_pairs={{1,0},{2,1},{3,2},{4,3},{5,4},{6,5},{7,6},{8,7},{9,8},{10,9},{11,1... | collective-permute-start | bytes 1032200 | tf_op jit(solution)/shard_map/ppermute | solution.py:24
  4.2 4.9 %collective-permute-start = (bf16[24,8,896]{2,1,0:T(8,128)(2,1)S(1)}, bf16[24,8,896]{2,1,0:T(8,128)(2,1)S(1)}, u32[]{:S(2)}, u32[]{:S(2)}) collective-permute-start(bf16[24,8,896]{2,1,0:T(8,128)(2,1)S(1)} %dynamic-slice_convert_fusion), channel_id=1, source_target_pairs={{0,1},{1,2},{2,3},{3,4},{4,5},{5,6},{6,7},{7,8},{8,9},{9,10},{10,1... | collective-permute-start | bytes 1032200 | tf_op jit(solution)/shard_map/ppermute | solution.py:23
  9.2 0.7 %convert_element_type.13 = f32[16]{0:T(128)S(1)} convert(s32[16]{0:T(128)} %param.3) | non-fusion elementwise | flops 16 | bytes 128 | tf_op jit(solution)/shard_map/convert_element_type | solution.py:117
  9.9 0.7 %broadcast_multiply_fusion = (f32[16]{0:T(128)S(1)}, f32[16]{0:T(128)S(1)}, f32[16]{0:T(128)S(1)}) fusion(s32[16]{0:T(128)} %param.3), kind=kLoop, calls=%fused_computation.23 | loop fusion | flops 32 | bytes 256 | tf_op jit(solution)/shard_map/mul | solution.py:43
  10.6 0.1 div.56
  10.7 0.1 div.57
  10.7 0.1 div.60
  10.8 0.1 div.61
  10.9 0.1 pad.3.clone
  11.0 0.1 broadcast_add_fusion
  11.1 6.1 %fusion.3.b_ref = bf16[16,13,128,128]{3,2,1,0:T(8,128)(2,1)} fusion(f32[16]{0:T(128)S(1)} %get-tuple-element.7, f32[16]{0:T(128)S(1)} %get-tuple-element.6, f32[13,128,128]{2,1,0:T(8,128)S(1)} %broadcast_add_fusion), kind=kLoop, calls=%fused_computation.4 | loop fusion | flops 27262976 | bytes 7667840 | tf_op jit(solution)/shard_map/convert_element_type | solution.py:44
  17.2 0.8 %fusion.8.f_ref = bf16[384,128]{1,0:T(8,128)(2,1)} fusion(f32[384]{0:T(512)S(1)} %div.61, f32[384]{0:T(512)S(1)} %div.57, f32[24,128]{1,0:T(8,128)S(1)} %iota_subtract_fusion.1, pred[24,128]{1,0:T(8,128)(4,1)S(1)} %fusion.9), kind=kLoop, calls=%fused_computation.16 | loop fusion | flops 442368 | bytes 116736 | tf_op jit(solution)/shard_map/convert_element_type | solution.py:35
  18.0 0.3 collective-permute-done.1
  18.3 4.8 %collective-permute-done = bf16[24,8,896]{2,1,0:T(8,128)(2,1)S(1)} collective-permute-done((bf16[24,8,896]{2,1,0:T(8,128)(2,1)S(1)}, bf16[24,8,896]{2,1,0:T(8,128)(2,1)S(1)}, u32[]{:S(2)}, u32[]{:S(2)}) %collective-permute-start) | collective-permute-done | bytes 344096 | tf_op jit(solution)/shard_map/ppermute | solution.py:23
  23.1 0.3 maximum_maximum_fusion
  23.4 1.6 %copy.6 = bf16[16,8,8,896]{3,1,2,0:T(8,128)(2,1)} copy(bf16[16,8,8,896]{3,2,1,0:T(8,128)(2,1)S(1)} %bitcast.19) | data formatting | bytes 3670016
  25.0 18.5 %shard_map.41 = (bf16[192,896]{1,0:T(8,128)(2,1)}, f32[192,896]{1,0:T(8,128)}) custom-call(bf16[384,128]{1,0:T(8,128)(2,1)} %fusion.8.f_ref, bf16[128,7168]{1,0:T(8,128)(2,1)} %bitcast.18, bf16[16,13,128,128]{3,2,1,0:T(8,128)(2,1)} %fusion.3.b_ref), custom_call_target="tpu_custom_call" | custom-call | tf_op jit(solution)/shard_map/pallas_call | solution.py:85
  43.5 1.7 %copy.10 = bf16[8,24,896]{2,0,1:T(8,128)(2,1)} copy(bf16[8,24,896]{2,1,0:T(8,128)(2,1)} %bitcast.23) | data formatting | bytes 688128 | tf_op jit(solution)/shard_map/reshape | solution.py:121
  45.3 2.1 %copy.9 = f32[8,24,896]{2,0,1:T(8,128)} copy(f32[8,24,896]{2,1,0:T(8,128)} %bitcast.20) | data formatting | bytes 1376256 | tf_op jit(solution)/shard_map/reshape | solution.py:122
  (7 shorter events, 0.1 us)
Async XLA Ops:
  1.8 16.6 %collective-permute-start.1 = (bf16[24,8,896]{2,1,0:T(8,128)(2,1)S(1)}, bf16[24,8,896]{2,1,0:T(8,128)(2,1)S(1)}, u32[]{:S(2)}, u32[]{:S(2)}) collective-permute-start(bf16[24,8,896]{2,1,0:T(8,128)(2,1)S(1)} %dynamic-slice_convert_fusion), channel_id=1, source_target_pairs={{1,0},{2,1},{3,2},{4,3},{5,4},{6,5},{7,6},{8,7},{9,8},{10,9},{11,1... | collective-permute-start | bytes 1032200 | tf_op jit(solution)/shard_map/ppermute | solution.py:24
  4.2 18.9 %collective-permute-start = (bf16[24,8,896]{2,1,0:T(8,128)(2,1)S(1)}, bf16[24,8,896]{2,1,0:T(8,128)(2,1)S(1)}, u32[]{:S(2)}, u32[]{:S(2)}) collective-permute-start(bf16[24,8,896]{2,1,0:T(8,128)(2,1)S(1)} %dynamic-slice_convert_fusion), channel_id=1, source_target_pairs={{0,1},{1,2},{2,3},{3,4},{4,5},{5,6},{6,7},{7,8},{8,9},{9,10},{10,1... | collective-permute-start | bytes 1032200 | tf_op jit(solution)/shard_map/ppermute | solution.py:23

commit v3 on v2

v3 whole, which is shorter than its diff:
```python
import jax
import jax.numpy as jnp
from jax import lax
from jax.experimental import pallas as pl
from jax.experimental.pallas import tpu as pltpu
from jax.sharding import PartitionSpec as P

SCAN_RATIO = 16
HALO = 24
TILE = 128


def mexican(offsets, spread):
    ratio = offsets / spread
    return (1.0 - ratio * ratio) * jnp.exp(-0.5 * ratio * ratio) / jnp.sqrt(spread)


def halos(slab, strip):
    n_scale, n_rt = lax.axis_size("scale"), lax.axis_size("rt")
    half = n_scale // 2
    s, r = lax.axis_index("scale"), lax.axis_index("rt")
    other = (s + half) % n_scale
    forward, backward = [], []
    for ss in range(n_scale):
        for rr in range(n_rt):
            flip = (ss + half) % n_scale
            if rr + 1 < n_rt:
                forward.append((ss * n_rt + rr, (ss if rr % 2 == 0 else flip) * n_rt + rr + 1))
            if rr > 0:
                backward.append((ss * n_rt + rr, (ss if rr % 2 == 1 else flip) * n_rt + rr - 1))
    frames = slab.shape[0]

    def piece(index, start):
        part = lax.dynamic_slice_in_dim(slab, index * strip, strip, axis=1)
        part = lax.slice_in_dim(part, start, start + HALO, axis=0)
        return part.astype(jnp.bfloat16)

    send_fwd = piece(jnp.where(r % 2 == 0, s, other), frames - HALO)
    send_bwd = piece(jnp.where(r % 2 == 1, s, other), 0)
    low = lax.ppermute(send_fwd, ("scale", "rt"), forward)
    high = lax.ppermute(send_bwd, ("scale", "rt"), backward)
    return low, high


def frame_tables(frames, scale_widths, depth):
    out_pos = jnp.arange(frames, dtype=jnp.float32)
    in_pos = jnp.arange(depth, dtype=jnp.float32) - HALO
    offsets = (in_pos[None, :] - out_pos[:, None])[None]
    spread = scale_widths[:, None, None]
    inside = (jnp.abs(offsets) <= HALO) & (in_pos < frames + HALO)[None, None, :]
    values = jnp.where(inside, mexican(offsets, spread), 0.0)
    return values.astype(jnp.bfloat16).reshape(-1, depth)


def scan_blocks(scans, scale_widths):
    nb = scans // TILE
    shift = (jnp.arange(2 * nb - 1, dtype=jnp.float32) - (nb - 1)) * TILE
    pos = jnp.arange(TILE, dtype=jnp.float32)
    offsets = shift[:, None, None] + (pos[:, None] - pos[None, :])[None]
    spread = SCAN_RATIO * scale_widths[:, None, None, None]
    return mexican(offsets[None], spread).astype(jnp.bfloat16)


def wavelet_kernel(f_ref, lo_ref, own_ref, hi_ref, b_ref, peak_ref, energy_ref, p_scr, g_scr, s_scr):
    c = pl.program_id(0)
    count, frames, strip, scans = g_scr.shape
    rows = frames * strip
    nb = scans // TILE

    @pl.when(c == 0)
    def _():
        p_scr[...] = jnp.zeros(p_scr.shape, p_scr.dtype)
        for m in range(strip):
            cols = slice(m * scans, (m + 1) * scans)
            p_scr[0:HALO, cols] = lo_ref[:, m, :].astype(jnp.float32)
            p_scr[HALO:HALO + frames, cols] = own_ref[:, m, :].astype(jnp.float32)
            p_scr[HALO + frames:2 * HALO + frames, cols] = hi_ref[:, m, :].astype(jnp.float32)
        fall = f_ref[...]
        for m in range(strip):
            part = p_scr[:, m * scans:(m + 1) * scans].astype(jnp.bfloat16)
            gm = jnp.dot(fall, part, preferred_element_type=jnp.float32)
            for cc in range(count):
                g_scr[cc, :, m, :] = gm[cc * frames:(cc + 1) * frames, :]

    for i in range(nb):
        for j in range(nb):
            s_scr[i * TILE:(i + 1) * TILE, j * TILE:(j + 1) * TILE] = b_ref[0, i - j + nb - 1]
    lhs = g_scr[c].reshape(rows, scans).astype(jnp.bfloat16)
    answer = jnp.dot(lhs, s_scr[...], preferred_element_type=jnp.float32).astype(jnp.bfloat16)
    square = jnp.square(answer.astype(jnp.float32))

    @pl.when(c == 0)
    def _():
        peak_ref[...] = answer
        energy_ref[...] = square

    @pl.when(c > 0)
    def _():
        peak_ref[...] = jnp.maximum(peak_ref[...], answer)
        energy_ref[...] = energy_ref[...] + square


def wavelet_core(ftab, low, own, high, blocks, frames, strip, scans, interpret=False):
    count = blocks.shape[0]
    depth = ftab.shape[1]
    rows = frames * strip
    nblk = blocks.shape[1]
    whole = lambda c: (0, 0)
    whole3 = lambda c: (0, 0, 0)
    return pl.pallas_call(
        wavelet_kernel,
        grid=(count,),
        in_specs=[
            pl.BlockSpec((count * frames, depth), whole),
            pl.BlockSpec((HALO, strip, scans), whole3),
            pl.BlockSpec((frames, strip, scans), whole3),
            pl.BlockSpec((HALO, strip, scans), whole3),
            pl.BlockSpec((1, nblk, TILE, TILE), lambda c: (c, 0, 0, 0)),
        ],
        out_specs=[
            pl.BlockSpec((rows, scans), whole),
            pl.BlockSpec((rows, scans), whole),
        ],
        out_shape=[
            jax.ShapeDtypeStruct((rows, scans), jnp.bfloat16),
            jax.ShapeDtypeStruct((rows, scans), jnp.float32),
        ],
        scratch_shapes=[
            pltpu.VMEM((depth, strip * scans), jnp.float32),
            pltpu.VMEM((count, frames, strip, scans), jnp.float32),
            pltpu.VMEM((scans, scans), jnp.bfloat16),
        ],
        compiler_params=pltpu.CompilerParams(
            dimension_semantics=("arbitrary",), vmem_limit_bytes=56 * 1024 * 1024
        ),
        interpret=interpret,
    )(ftab, low, own, high, blocks)


def compute(own, low, high, widths, interpret=False):
    frames, strip, scans = own.shape
    depth = -(-(frames + 2 * HALO) // TILE) * TILE
    scale_widths = widths.astype(jnp.float32)
    ftab = frame_tables(frames, scale_widths, depth)
    blocks = scan_blocks(scans, scale_widths)
    peak, energy = wavelet_core(ftab, low, own, high, blocks, frames, strip, scans, interpret)
    return peak.reshape(frames, strip, scans), energy.reshape(frames, strip, scans)


def per_device(slab, widths):
    frames, mz_bins, scans = slab.shape
    strip = mz_bins // lax.axis_size("scale")
    first = lax.axis_index("scale") * strip
    own = lax.dynamic_slice_in_dim(slab, first, strip, axis=1).astype(jnp.bfloat16)
    low, high = halos(slab, strip)
    return compute(own, low, high, widths)


def solution(mesh):
    in_specs = (P("rt", None, None), P())
    out_specs = (P("rt", "scale", None), P("rt", "scale", None))
    return jax.shard_map(
        per_device, mesh=mesh, in_specs=in_specs, out_specs=out_specs, check_vma=False
    )
```

time: 47.9 us -> 46 us (0.960)
  the two profiles are of different devices: /device:TPU:111 before, /device:TPU:136 now
where the time goes in v3:
time: 46 us; the launch traced here: 45.5 us
  Pallas kernels  22.7 us (49%)
  other arithmetic  8.41 us (18%)
  starting transfers between devices  5.92 us (13%)
  waiting for transfers between devices  4.17 us (9%)
  local copies, waits for them, and re-layouts  3.63 us (8%)
  between operations  0.73 us (2%)
    pallas_call x1, Pallas kernels, wavelet_core(): pl.pallas_call(wavelet_kernel, grid=(count,), in_specs=[pl.BlockSpec((cou...  22.7 us
    convert_element_type x1, other arithmetic, scan_blocks(): return mexican(offsets[None], spread).astype(jnp.bfloat16)  6.07 us
    ppermute x1, waiting for transfers between devices, halos(): low = lax.ppermute(send_fwd, ('scale', 'rt'), forward)  4.16 us
    ppermute x1, starting transfers between devices, halos(): high = lax.ppermute(send_bwd, ('scale', 'rt'), backward)  4 us
    convert_element_type x1, local copies, waits for them, and re-layouts, piece(): return part.astype(jnp.bfloat16)  2.57 us
    ppermute x1, starting transfers between devices, halos(): low = lax.ppermute(send_fwd, ('scale', 'rt'), forward)  1.92 us
  transfers between devices with their start and end apart: 2, of which 1 were waited for; matrix products, arithmetic and copies ran while one was open for 19% of the time, Pallas kernels for 0%

profile of v3, /device:TPU:136, one launch (start us, length us, event | category | flops | bytes accessed | tf_op | source)
XLA Modules:
  0.0 45.5 jit_solution(11672587771551693539)
XLA Ops:
  0.7 2.6 %dynamic-slice_convert_fusion = (bf16[24,8,896]{2,1,0:T(8,128)(2,1)S(1)}, bf16[24,8,896]{2,1,0:T(8,128)(2,1)S(1)}, bf16[24,8,896]{2,1,0:T(8,128)(2,1)}) fusion(f32[24,128,896]{2,1,0:T(8,128)} %param.2, s32[]{:T(128)S(6)} %select_n.40, s32[]{:T(128)S(6)} %select_n.37, s32[]{:T(128)S(6)} %select_n.38), kind=kLoop, calls=%fused_computation.5 | loop fusion | bytes 2064396 | tf_op jit(solution)/shard_map/convert_element_type | solution.py:36
  3.2 4.0 %collective-permute-start.1 = (bf16[24,8,896]{2,1,0:T(8,128)(2,1)S(1)}, bf16[24,8,896]{2,1,0:T(8,128)(2,1)S(1)}, u32[]{:S(2)}, u32[]{:S(2)}) collective-permute-start(bf16[24,8,896]{2,1,0:T(8,128)(2,1)S(1)} %get-tuple-element.6), channel_id=1, source_target_pairs={{1,0},{2,129},{3,2},{4,131},{5,4},{6,133},{7,6},{8,135},{9,8},{10,... | collective-permute-start | bytes 1032200 | tf_op jit(solution)/shard_map/ppermute | solution.py:41
  7.2 1.9 %collective-permute-start = (bf16[24,8,896]{2,1,0:T(8,128)(2,1)S(1)}, bf16[24,8,896]{2,1,0:T(8,128)(2,1)S(1)}, u32[]{:S(2)}, u32[]{:S(2)}) collective-permute-start(bf16[24,8,896]{2,1,0:T(8,128)(2,1)S(1)} %get-tuple-element.7), channel_id=1, source_target_pairs={{0,1},{1,130},{2,3},{3,132},{4,5},{5,134},{6,7},{7,136},{8,9},{9,1... | collective-permute-start | bytes 1032200 | tf_op jit(solution)/shard_map/ppermute | solution.py:40
  9.2 0.7 %convert_element_type.19 = f32[16]{0:T(128)S(1)} convert(s32[16]{0:T(128)} %param.3) | non-fusion elementwise | flops 16 | bytes 128 | tf_op jit(solution)/shard_map/convert_element_type | solution.py:143
  9.9 0.7 %broadcast_multiply_fusion = (f32[16]{0:T(128)S(1)}, f32[16]{0:T(128)S(1)}, f32[16]{0:T(128)S(1)}) fusion(s32[16]{0:T(128)} %param.3), kind=kLoop, calls=%fused_computation.22 | loop fusion | flops 32 | bytes 256 | tf_op jit(solution)/shard_map/mul | solution.py:60
  10.6 0.1 div.56
  10.6 0.1 div.57
  10.7 0.1 div.60
  10.8 0.1 div.61
  10.9 0.1 broadcast_add_fusion
  11.0 6.1 %fusion.3.b_ref = bf16[16,13,128,128]{3,2,1,0:T(8,128)(2,1)} fusion(f32[16]{0:T(128)S(1)} %get-tuple-element.10, f32[16]{0:T(128)S(1)} %get-tuple-element.9, f32[13,128,128]{2,1,0:T(8,128)S(1)} %broadcast_add_fusion), kind=kLoop, calls=%fused_computation.4 | loop fusion | flops 27262976 | bytes 7667840 | tf_op jit(solution)/shard_map/convert_element_type | solution.py:61
  17.1 0.8 %fusion.8.f_ref = bf16[384,128]{1,0:T(8,128)(2,1)} fusion(f32[384]{0:T(512)S(1)} %div.61, f32[384]{0:T(512)S(1)} %div.57, f32[24,128]{1,0:T(8,128)S(1)} %iota_subtract_fusion.1, pred[24,128]{1,0:T(8,128)(4,1)S(1)} %fusion.9), kind=kLoop, calls=%fused_computation.15 | loop fusion | flops 442368 | bytes 116736 | tf_op jit(solution)/shard_map/convert_element_type | solution.py:52
  18.0 0.0 collective-permute-done.1.hi_ref
  18.0 0.0 copy-start
  18.0 4.2 %collective-permute-done.lo_ref = bf16[24,8,896]{2,1,0:T(8,128)(2,1)S(1)} collective-permute-done((bf16[24,8,896]{2,1,0:T(8,128)(2,1)S(1)}, bf16[24,8,896]{2,1,0:T(8,128)(2,1)S(1)}, u32[]{:S(2)}, u32[]{:S(2)}) %collective-permute-start) | collective-permute-done | bytes 344096 | tf_op jit(solution)/shard_map/ppermute | solution.py:40
  22.1 0.0 copy-start.1
  22.1 0.0 copy-done
  22.1 0.7 %copy-done.1 = bf16[24,8,896]{2,1,0:T(8,128)(2,1)} copy-done((bf16[24,8,896]{2,1,0:T(8,128)(2,1)}, bf16[24,8,896]{2,1,0:T(8,128)(2,1)S(1)}, u32[]{:S(2)}) %copy-start.1) | copy-done | bytes 344088
  22.9 22.7 %shard_map.41 = (bf16[192,896]{1,0:T(8,128)(2,1)}, f32[192,896]{1,0:T(8,128)}) custom-call(bf16[384,128]{1,0:T(8,128)(2,1)} %fusion.8.f_ref, bf16[24,8,896]{2,1,0:T(8,128)(2,1)} %copy-done.1, bf16[24,8,896]{2,1,0:T(8,128)(2,1)} %get-tuple-element.8.own_ref, bf16[24,8,896]{2,1,0:T(8,128)(2,1)} %copy-done, bf16[16,13,128,128]{3,2,1,0:T(8,128)(2,1)} %fusion.3.b_ref), custom_call_target="tpu_custom_call" | custom-call | tf_op jit(solution)/shard_map/pallas_call | solution.py:110
  (6 shorter events, 0.1 us)
Async XLA Ops:
  3.2 14.7 %collective-permute-start.1 = (bf16[24,8,896]{2,1,0:T(8,128)(2,1)S(1)}, bf16[24,8,896]{2,1,0:T(8,128)(2,1)S(1)}, u32[]{:S(2)}, u32[]{:S(2)}) collective-permute-start(bf16[24,8,896]{2,1,0:T(8,128)(2,1)S(1)} %get-tuple-element.6), channel_id=1, source_target_pairs={{1,0},{2,129},{3,2},{4,131},{5,4},{6,133},{7,6},{8,135},{9,8},{10,... | collective-permute-start | bytes 1032200 | tf_op jit(solution)/shard_map/ppermute | solution.py:41
  7.2 14.9 %collective-permute-start = (bf16[24,8,896]{2,1,0:T(8,128)(2,1)S(1)}, bf16[24,8,896]{2,1,0:T(8,128)(2,1)S(1)}, u32[]{:S(2)}, u32[]{:S(2)}) collective-permute-start(bf16[24,8,896]{2,1,0:T(8,128)(2,1)S(1)} %get-tuple-element.7), channel_id=1, source_target_pairs={{0,1},{1,130},{2,3},{3,132},{4,5},{5,134},{6,7},{7,136},{8,9},{9,1... | collective-permute-start | bytes 1032200 | tf_op jit(solution)/shard_map/ppermute | solution.py:40
  18.0 4.2 %copy-start = (bf16[24,8,896]{2,1,0:T(8,128)(2,1)}, bf16[24,8,896]{2,1,0:T(8,128)(2,1)S(1)}, u32[]{:S(2)}) copy-start(bf16[24,8,896]{2,1,0:T(8,128)(2,1)S(1)} %collective-permute-done.1.hi_ref) | copy-start | bytes 1032196
  22.1 0.7 %copy-start.1 = (bf16[24,8,896]{2,1,0:T(8,128)(2,1)}, bf16[24,8,896]{2,1,0:T(8,128)(2,1)S(1)}, u32[]{:S(2)}) copy-start(bf16[24,8,896]{2,1,0:T(8,128)(2,1)S(1)} %collective-permute-done.lo_ref) | copy-start | bytes 1032196

commit v4 on v3

--- a/solution.py
+++ b/solution.py
@@ -61,43 +61,52 @@
     return mexican(offsets[None], spread).astype(jnp.bfloat16)
 
 
-def wavelet_kernel(f_ref, lo_ref, own_ref, hi_ref, b_ref, peak_ref, energy_ref, p_scr, g_scr, s_scr):
+def wavelet_kernel(f_ref, lo_ref, own_ref, hi_ref, b_ref, peak_ref, energy_ref,
+                   p_scr, g_scr, s_scr, best_scr, total_scr):
     c = pl.program_id(0)
-    count, frames, strip, scans = g_scr.shape
-    rows = frames * strip
+    count, rows, scans = g_scr.shape
+    frames, strip, _ = own_ref.shape
     nb = scans // TILE
+    used = 2 * HALO + frames
 
     @pl.when(c == 0)
     def _():
-        p_scr[...] = jnp.zeros(p_scr.shape, p_scr.dtype)
+        p_scr[used:, :] = jnp.zeros((p_scr.shape[0] - used, p_scr.shape[1]), p_scr.dtype)
         for m in range(strip):
             cols = slice(m * scans, (m + 1) * scans)
             p_scr[0:HALO, cols] = lo_ref[:, m, :].astype(jnp.float32)
             p_scr[HALO:HALO + frames, cols] = own_ref[:, m, :].astype(jnp.float32)
-            p_scr[HALO + frames:2 * HALO + frames, cols] = hi_ref[:, m, :].astype(jnp.float32)
+            p_scr[HALO + frames:used, cols] = hi_ref[:, m, :].astype(jnp.float32)
         fall = f_ref[...]
         for m in range(strip):
             part = p_scr[:, m * scans:(m + 1) * scans].astype(jnp.bfloat16)
             gm = jnp.dot(fall, part, preferred_element_type=jnp.float32)
             for cc in range(count):
-                g_scr[cc, :, m, :] = gm[cc * frames:(cc + 1) * frames, :]
+                g_scr[cc, m * frames:(m + 1) * frames, :] = gm[cc * frames:(cc + 1) * frames, :]
 
     for i in range(nb):
         for j in range(nb):
             s_scr[i * TILE:(i + 1) * TILE, j * TILE:(j + 1) * TILE] = b_ref[0, i - j + nb - 1]
-    lhs = g_scr[c].reshape(rows, scans).astype(jnp.bfloat16)
+    lhs = g_scr[c].astype(jnp.bfloat16)
     answer = jnp.dot(lhs, s_scr[...], preferred_element_type=jnp.float32).astype(jnp.bfloat16)
-    square = jnp.square(answer.astype(jnp.float32))
+    answer = answer.astype(jnp.float32)
+    square = answer * answer
 
     @pl.when(c == 0)
     def _():
-        peak_ref[...] = answer
-        energy_ref[...] = square
+        best_scr[...] = answer
+        total_scr[...] = square
 
     @pl.when(c > 0)
     def _():
-        peak_ref[...] = jnp.maximum(peak_ref[...], answer)
-        energy_ref[...] = energy_ref[...] + square
+        best_scr[...] = jnp.maximum(best_scr[...], answer)
+        total_scr[...] = total_scr[...] + square
+
+    @pl.when(c == count - 1)
+    def _():
+        for m in range(strip):
+            peak_ref[:, m, :] = best_scr[m * frames:(m + 1) * frames, :].astype(peak_ref.dtype)
+            energy_ref[:, m, :] = total_scr[m * frames:(m + 1) * frames, :]
 
 
 def wavelet_core(ftab, low, own, high, blocks, frames, strip, scans, interpret=False):
@@ -118,17 +127,19 @@
             pl.BlockSpec((1, nblk, TILE, TILE), lambda c: (c, 0, 0, 0)),
         ],
         out_specs=[
-            pl.BlockSpec((rows, scans), whole),
-            pl.BlockSpec((rows, scans), whole),
+            pl.BlockSpec((frames, strip, scans), whole3),
+            pl.BlockSpec((frames, strip, scans), whole3),
         ],
         out_shape=[
-            jax.ShapeDtypeStruct((rows, scans), jnp.bfloat16),
-            jax.ShapeDtypeStruct((rows, scans), jnp.float32),
+            jax.ShapeDtypeStruct((frames, strip, scans), jnp.bfloat16),
+            jax.ShapeDtypeStruct((frames, strip, scans), jnp.float32),
         ],
         scratch_shapes=[
             pltpu.VMEM((depth, strip * scans), jnp.float32),
-            pltpu.VMEM((count, frames, strip, scans), jnp.float32),
+            pltpu.VMEM((count, rows, scans), jnp.float32),
             pltpu.VMEM((scans, scans), jnp.bfloat16),
+            pltpu.VMEM((rows, scans), jnp.float32),
+            pltpu.VMEM((rows, scans), jnp.float32),
         ],
         compiler_params=pltpu.CompilerParams(
             dimension_semantics=("arbitrary",), vmem_limit_bytes=56 * 1024 * 1024
@@ -143,8 +154,7 @@
     scale_widths = widths.astype(jnp.float32)
     ftab = frame_tables(frames, scale_widths, depth)
     blocks = scan_blocks(scans, scale_widths)
-    peak, energy = wavelet_core(ftab, low, own, high, blocks, frames, strip, scans, interpret)
-    return peak.reshape(frames, strip, scans), energy.reshape(frames, strip, scans)
+    return wavelet_core(ftab, low, own, high, blocks, frames, strip, scans, interpret)
 
 
 def per_device(slab, widths):

time: 46 us -> 42.3 us (0.920)
  Pallas kernels: 22.7 us -> 19 us
    pallas_call x1, Pallas kernels: 22.7 us -> 19 us  [wavelet_core(): pl.pallas_call(wavelet_kernel, grid=(count,), in_specs=[pl.BlockSpec((cou...]
  transfers between devices with their start and end apart: 2 -> 2, of which waited for: 1 -> 1; matrix products, arithmetic and copies ran while one was open for 19% -> 21% of each run, Pallas kernels for 0% -> 0%
where the time goes in v4:
time: 42.3 us; the launch traced here: 41.9 us
  Pallas kernels  19 us (45%)
  other arithmetic  8.39 us (20%)
  starting transfers between devices  5.92 us (14%)
  waiting for transfers between devices  4.18 us (10%)
  local copies, waits for them, and re-layouts  3.62 us (9%)
  between operations  0.73 us (2%)
    pallas_call x1, Pallas kernels, wavelet_core(): pl.pallas_call(wavelet_kernel, grid=(count,), in_specs=[pl.BlockSpec((cou...  19 us
    convert_element_type x1, other arithmetic, scan_blocks(): return mexican(offsets[None], spread).astype(jnp.bfloat16)  6.05 us
    ppermute x1, waiting for transfers between devices, halos(): low = lax.ppermute(send_fwd, ('scale', 'rt'), forward)  4.18 us
    ppermute x1, starting transfers between devices, halos(): high = lax.ppermute(send_bwd, ('scale', 'rt'), backward)  4 us
    convert_element_type x1, local copies, waits for them, and re-layouts, piece(): return part.astype(jnp.bfloat16)  2.56 us
    ppermute x1, starting transfers between devices, halos(): low = lax.ppermute(send_fwd, ('scale', 'rt'), forward)  1.92 us
  transfers between devices with their start and end apart: 2, of which 1 were waited for; matrix products, arithmetic and copies ran while one was open for 21% of the time, Pallas kernels for 0%

profile of v4, /device:TPU:136, one launch (start us, length us, event | category | flops | bytes accessed | tf_op | source)
XLA Modules:
  0.0 41.9 jit_solution(1710480167816458264)
XLA Ops:
  0.7 2.6 %dynamic-slice_convert_fusion = (bf16[24,8,896]{2,1,0:T(8,128)(2,1)S(1)}, bf16[24,8,896]{2,1,0:T(8,128)(2,1)S(1)}, bf16[24,8,896]{2,1,0:T(8,128)(2,1)}) fusion(f32[24,128,896]{2,1,0:T(8,128)} %param.2, s32[]{:T(128)S(6)} %select_n.40, s32[]{:T(128)S(6)} %select_n.37, s32[]{:T(128)S(6)} %select_n.38), kind=kLoop, calls=%fused_computation.5 | loop fusion | bytes 2064396 | tf_op jit(solution)/shard_map/convert_element_type | solution.py:36
  3.2 4.0 %collective-permute-start.1 = (bf16[24,8,896]{2,1,0:T(8,128)(2,1)S(1)}, bf16[24,8,896]{2,1,0:T(8,128)(2,1)S(1)}, u32[]{:S(2)}, u32[]{:S(2)}) collective-permute-start(bf16[24,8,896]{2,1,0:T(8,128)(2,1)S(1)} %get-tuple-element.2), channel_id=1, source_target_pairs={{1,0},{2,129},{3,2},{4,131},{5,4},{6,133},{7,6},{8,135},{9,8},{10,... | collective-permute-start | bytes 1032200 | tf_op jit(solution)/shard_map/ppermute | solution.py:41
  7.2 1.9 %collective-permute-start = (bf16[24,8,896]{2,1,0:T(8,128)(2,1)S(1)}, bf16[24,8,896]{2,1,0:T(8,128)(2,1)S(1)}, u32[]{:S(2)}, u32[]{:S(2)}) collective-permute-start(bf16[24,8,896]{2,1,0:T(8,128)(2,1)S(1)} %get-tuple-element.3), channel_id=1, source_target_pairs={{0,1},{1,130},{2,3},{3,132},{4,5},{5,134},{6,7},{7,136},{8,9},{9,1... | collective-permute-start | bytes 1032200 | tf_op jit(solution)/shard_map/ppermute | solution.py:40
  9.2 0.7 %convert_element_type.19 = f32[16]{0:T(128)S(1)} convert(s32[16]{0:T(128)} %param.3) | non-fusion elementwise | flops 16 | bytes 128 | tf_op jit(solution)/shard_map/convert_element_type | solution.py:154
  9.9 0.7 %broadcast_multiply_fusion = (f32[16]{0:T(128)S(1)}, f32[16]{0:T(128)S(1)}, f32[16]{0:T(128)S(1)}) fusion(s32[16]{0:T(128)} %param.3), kind=kLoop, calls=%fused_computation.22 | loop fusion | flops 32 | bytes 256 | tf_op jit(solution)/shard_map/mul | solution.py:60
  10.6 0.1 div.56
  10.6 0.1 div.57
  10.7 0.1 div.60
  10.8 0.1 div.61
  10.9 0.1 broadcast_add_fusion
  11.0 6.0 %fusion.3.b_ref = bf16[16,13,128,128]{3,2,1,0:T(8,128)(2,1)} fusion(f32[16]{0:T(128)S(1)} %get-tuple-element.6, f32[16]{0:T(128)S(1)} %get-tuple-element.5, f32[13,128,128]{2,1,0:T(8,128)S(1)} %broadcast_add_fusion), kind=kLoop, calls=%fused_computation.4 | loop fusion | flops 27262976 | bytes 7667840 | tf_op jit(solution)/shard_map/convert_element_type | solution.py:61
  17.1 0.8 %fusion.8.f_ref = bf16[384,128]{1,0:T(8,128)(2,1)} fusion(f32[384]{0:T(512)S(1)} %div.61, f32[384]{0:T(512)S(1)} %div.57, f32[24,128]{1,0:T(8,128)S(1)} %iota_subtract_fusion.1, pred[24,128]{1,0:T(8,128)(4,1)S(1)} %fusion.9), kind=kLoop, calls=%fused_computation.15 | loop fusion | flops 442368 | bytes 116736 | tf_op jit(solution)/shard_map/convert_element_type | solution.py:52
  17.9 0.0 collective-permute-done.1.hi_ref
  17.9 0.0 copy-start
  17.9 4.2 %collective-permute-done.lo_ref = bf16[24,8,896]{2,1,0:T(8,128)(2,1)S(1)} collective-permute-done((bf16[24,8,896]{2,1,0:T(8,128)(2,1)S(1)}, bf16[24,8,896]{2,1,0:T(8,128)(2,1)S(1)}, u32[]{:S(2)}, u32[]{:S(2)}) %collective-permute-start) | collective-permute-done | bytes 344096 | tf_op jit(solution)/shard_map/ppermute | solution.py:40
  22.1 0.0 copy-start.1
  22.1 0.0 copy-done
  22.1 0.7 %copy-done.1 = bf16[24,8,896]{2,1,0:T(8,128)(2,1)} copy-done((bf16[24,8,896]{2,1,0:T(8,128)(2,1)}, bf16[24,8,896]{2,1,0:T(8,128)(2,1)S(1)}, u32[]{:S(2)}) %copy-start.1) | copy-done | bytes 344088
  22.8 19.0 %shard_map.41 = (bf16[24,8,896]{2,1,0:T(8,128)(2,1)}, f32[24,8,896]{2,1,0:T(8,128)}) custom-call(bf16[384,128]{1,0:T(8,128)(2,1)} %fusion.8.f_ref, bf16[24,8,896]{2,1,0:T(8,128)(2,1)} %copy-done.1, bf16[24,8,896]{2,1,0:T(8,128)(2,1)} %get-tuple-element.4.own_ref, bf16[24,8,896]{2,1,0:T(8,128)(2,1)} %copy-done, bf16[16,13,128,128]{3,2,1,0:T(8,128)(2,1)} %fusion.3.b_ref), custom_call_target="tpu_custom_call" | custom-call | tf_op jit(solution)/shard_map/pallas_call | solution.py:119
  (6 shorter events, 0.1 us)
Async XLA Ops:
  3.2 14.7 %collective-permute-start.1 = (bf16[24,8,896]{2,1,0:T(8,128)(2,1)S(1)}, bf16[24,8,896]{2,1,0:T(8,128)(2,1)S(1)}, u32[]{:S(2)}, u32[]{:S(2)}) collective-permute-start(bf16[24,8,896]{2,1,0:T(8,128)(2,1)S(1)} %get-tuple-element.2), channel_id=1, source_target_pairs={{1,0},{2,129},{3,2},{4,131},{5,4},{6,133},{7,6},{8,135},{9,8},{10,... | collective-permute-start | bytes 1032200 | tf_op jit(solution)/shard_map/ppermute | solution.py:41
  7.2 14.9 %collective-permute-start = (bf16[24,8,896]{2,1,0:T(8,128)(2,1)S(1)}, bf16[24,8,896]{2,1,0:T(8,128)(2,1)S(1)}, u32[]{:S(2)}, u32[]{:S(2)}) collective-permute-start(bf16[24,8,896]{2,1,0:T(8,128)(2,1)S(1)} %get-tuple-element.3), channel_id=1, source_target_pairs={{0,1},{1,130},{2,3},{3,132},{4,5},{5,134},{6,7},{7,136},{8,9},{9,1... | collective-permute-start | bytes 1032200 | tf_op jit(solution)/shard_map/ppermute | solution.py:40
  17.9 4.2 %copy-start = (bf16[24,8,896]{2,1,0:T(8,128)(2,1)}, bf16[24,8,896]{2,1,0:T(8,128)(2,1)S(1)}, u32[]{:S(2)}) copy-start(bf16[24,8,896]{2,1,0:T(8,128)(2,1)S(1)} %collective-permute-done.1.hi_ref) | copy-start | bytes 1032196
  22.1 0.7 %copy-start.1 = (bf16[24,8,896]{2,1,0:T(8,128)(2,1)}, bf16[24,8,896]{2,1,0:T(8,128)(2,1)S(1)}, u32[]{:S(2)}) copy-start(bf16[24,8,896]{2,1,0:T(8,128)(2,1)S(1)} %collective-permute-done.lo_ref) | copy-start | bytes 1032196

commit v5 on v4

--- a/solution.py
+++ b/solution.py
@@ -61,7 +61,7 @@
     return mexican(offsets[None], spread).astype(jnp.bfloat16)
 
 
-def wavelet_kernel(f_ref, lo_ref, own_ref, hi_ref, b_ref, peak_ref, energy_ref,
+def wavelet_kernel(strip_ref, f_ref, lo_ref, own_ref, hi_ref, b_ref, peak_ref, energy_ref,
                    p_scr, g_scr, s_scr, best_scr, total_scr):
     c = pl.program_id(0)
     count, rows, scans = g_scr.shape
@@ -75,7 +75,7 @@
         for m in range(strip):
             cols = slice(m * scans, (m + 1) * scans)
             p_scr[0:HALO, cols] = lo_ref[:, m, :].astype(jnp.float32)
-            p_scr[HALO:HALO + frames, cols] = own_ref[:, m, :].astype(jnp.float32)
+            p_scr[HALO:HALO + frames, cols] = own_ref[:, m, :]
             p_scr[HALO + frames:used, cols] = hi_ref[:, m, :].astype(jnp.float32)
         fall = f_ref[...]
         for m in range(strip):
@@ -109,30 +109,27 @@
             energy_ref[:, m, :] = total_scr[m * frames:(m + 1) * frames, :]
 
 
-def wavelet_core(ftab, low, own, high, blocks, frames, strip, scans, interpret=False):
+def wavelet_core(first, ftab, low, slab, high, blocks, interpret=False):
     count = blocks.shape[0]
     depth = ftab.shape[1]
+    frames, strip, scans = low.shape
     rows = frames * strip
     nblk = blocks.shape[1]
-    whole = lambda c: (0, 0)
-    whole3 = lambda c: (0, 0, 0)
-    return pl.pallas_call(
-        wavelet_kernel,
+    whole = lambda c, i: (0, 0)
+    whole3 = lambda c, i: (0, 0, 0)
+    grid_spec = pltpu.PrefetchScalarGridSpec(
+        num_scalar_prefetch=1,
         grid=(count,),
         in_specs=[
             pl.BlockSpec((count * frames, depth), whole),
             pl.BlockSpec((HALO, strip, scans), whole3),
-            pl.BlockSpec((frames, strip, scans), whole3),
+            pl.BlockSpec((frames, strip, scans), lambda c, i: (0, i[0], 0)),
             pl.BlockSpec((HALO, strip, scans), whole3),
-            pl.BlockSpec((1, nblk, TILE, TILE), lambda c: (c, 0, 0, 0)),
+            pl.BlockSpec((1, nblk, TILE, TILE), lambda c, i: (c, 0, 0, 0)),
         ],
         out_specs=[
             pl.BlockSpec((frames, strip, scans), whole3),
             pl.BlockSpec((frames, strip, scans), whole3),
-        ],
-        out_shape=[
-            jax.ShapeDtypeStruct((frames, strip, scans), jnp.bfloat16),
-            jax.ShapeDtypeStruct((frames, strip, scans), jnp.float32),
         ],
         scratch_shapes=[
             pltpu.VMEM((depth, strip * scans), jnp.float32),
@@ -141,29 +138,35 @@
             pltpu.VMEM((rows, scans), jnp.float32),
             pltpu.VMEM((rows, scans), jnp.float32),
         ],
+    )
+    return pl.pallas_call(
+        wavelet_kernel,
+        grid_spec=grid_spec,
+        out_shape=[
+            jax.ShapeDtypeStruct((frames, strip, scans), jnp.bfloat16),
+            jax.ShapeDtypeStruct((frames, strip, scans), jnp.float32),
+        ],
         compiler_params=pltpu.CompilerParams(
             dimension_semantics=("arbitrary",), vmem_limit_bytes=56 * 1024 * 1024
         ),
         interpret=interpret,
-    )(ftab, low, own, high, blocks)
+    )(first, ftab, low, slab, high, blocks)
 
 
-def compute(own, low, high, widths, interpret=False):
-    frames, strip, scans = own.shape
+def compute(slab, block_index, low, high, widths, interpret=False):
+    frames, strip, scans = low.shape
     depth = -(-(frames + 2 * HALO) // TILE) * TILE
     scale_widths = widths.astype(jnp.float32)
     ftab = frame_tables(frames, scale_widths, depth)
     blocks = scan_blocks(scans, scale_widths)
-    return wavelet_core(ftab, low, own, high, blocks, frames, strip, scans, interpret)
+    first = jnp.reshape(block_index, (1,)).astype(jnp.int32)
+    return wavelet_core(first, ftab, low, slab, high, blocks, interpret)
 
 
 def per_device(slab, widths):
-    frames, mz_bins, scans = slab.shape
-    strip = mz_bins // lax.axis_size("scale")
-    first = lax.axis_index("scale") * strip
-    own = lax.dynamic_slice_in_dim(slab, first, strip, axis=1).astype(jnp.bfloat16)
+    strip = slab.shape[1] // lax.axis_size("scale")
     low, high = halos(slab, strip)
-    return compute(own, low, high, widths)
+    return compute(slab, lax.axis_index("scale"), low, high, widths)
 
 
 def solution(mesh):

time: 42.3 us -> 41.3 us (0.976)
  local copies, waits for them, and re-layouts: 3.62 us -> 2.44 us
    convert_element_type x1, local copies, waits for them, and re-layouts: 2.56 us -> 1.39 us  [piece(): return part.astype(jnp.bfloat16)]
where the time goes in v5:
time: 41.3 us; the launch traced here: 40.8 us
  Pallas kernels  19.1 us (46%)
  other arithmetic  8.38 us (20%)
  starting transfers between devices  6.13 us (15%)
  waiting for transfers between devices  4.06 us (10%)
  local copies, waits for them, and re-layouts  2.44 us (6%)
  between operations  0.73 us (2%)
    pallas_call x1, Pallas kernels, wavelet_core(): pl.pallas_call(wavelet_kernel, grid_spec=grid_spec, out_shape=[jax.ShapeD...  19.1 us
    convert_element_type x1, other arithmetic, scan_blocks(): return mexican(offsets[None], spread).astype(jnp.bfloat16)  6.05 us
    ppermute x1, starting transfers between devices, halos(): high = lax.ppermute(send_bwd, ('scale', 'rt'), backward)  4.21 us
    ppermute x1, waiting for transfers between devices, halos(): low = lax.ppermute(send_fwd, ('scale', 'rt'), forward)  4.05 us
    ppermute x1, starting transfers between devices, halos(): low = lax.ppermute(send_fwd, ('scale', 'rt'), forward)  1.92 us
    convert_element_type x1, local copies, waits for them, and re-layouts, piece(): return part.astype(jnp.bfloat16)  1.39 us
  transfers between devices with their start and end apart: 2, of which 1 were waited for; matrix products, arithmetic and copies ran while one was open for 21% of the time, Pallas kernels for 0%

profile of v5, /device:TPU:136, one launch (start us, length us, event | category | flops | bytes accessed | tf_op | source)
XLA Modules:
  0.0 40.8 jit_solution(13579787378366512570)
XLA Ops:
  0.7 1.4 %dynamic-slice_convert_fusion = (bf16[24,8,896]{2,1,0:T(8,128)(2,1)S(1)}, bf16[24,8,896]{2,1,0:T(8,128)(2,1)S(1)}) fusion(f32[24,128,896]{2,1,0:T(8,128)} %own_ref.1, s32[]{:T(128)S(6)} %select_n.36, s32[]{:T(128)S(6)} %select_n.34), kind=kLoop, calls=%fused_computation.5 | loop fusion | bytes 1376264 | tf_op jit(solution)/shard_map/convert_element_type | solution.py:36
  2.1 4.2 %collective-permute-start.1 = (bf16[24,8,896]{2,1,0:T(8,128)(2,1)S(1)}, bf16[24,8,896]{2,1,0:T(8,128)(2,1)S(1)}, u32[]{:S(2)}, u32[]{:S(2)}) collective-permute-start(bf16[24,8,896]{2,1,0:T(8,128)(2,1)S(1)} %get-tuple-element.2), channel_id=1, source_target_pairs={{1,0},{2,129},{3,2},{4,131},{5,4},{6,133},{7,6},{8,135},{9,8},{10,... | collective-permute-start | bytes 1032200 | tf_op jit(solution)/shard_map/ppermute | solution.py:41
  6.3 1.9 %collective-permute-start = (bf16[24,8,896]{2,1,0:T(8,128)(2,1)S(1)}, bf16[24,8,896]{2,1,0:T(8,128)(2,1)S(1)}, u32[]{:S(2)}, u32[]{:S(2)}) collective-permute-start(bf16[24,8,896]{2,1,0:T(8,128)(2,1)S(1)} %get-tuple-element.3), channel_id=1, source_target_pairs={{0,1},{1,130},{2,3},{3,132},{4,5},{5,134},{6,7},{7,136},{8,9},{9,1... | collective-permute-start | bytes 1032200 | tf_op jit(solution)/shard_map/ppermute | solution.py:40
  8.2 0.7 %convert_element_type.16 = f32[16]{0:T(128)S(1)} convert(s32[16]{0:T(128)} %param.3) | non-fusion elementwise | flops 16 | bytes 128 | tf_op jit(solution)/shard_map/convert_element_type | solution.py:159
  8.9 0.7 %broadcast_multiply_fusion = (f32[16]{0:T(128)S(1)}, f32[16]{0:T(128)S(1)}, f32[16]{0:T(128)S(1)}) fusion(s32[16]{0:T(128)} %param.3), kind=kLoop, calls=%fused_computation.21 | loop fusion | flops 32 | bytes 256 | tf_op jit(solution)/shard_map/mul | solution.py:60
  9.6 0.1 div.56
  9.7 0.1 div.57
  9.8 0.1 div.60
  9.8 0.1 div.61
  9.9 0.1 broadcast_add_fusion
  10.1 6.0 %fusion.3.b_ref = bf16[16,13,128,128]{3,2,1,0:T(8,128)(2,1)} fusion(f32[16]{0:T(128)S(1)} %get-tuple-element.5, f32[16]{0:T(128)S(1)} %get-tuple-element.4, f32[13,128,128]{2,1,0:T(8,128)S(1)} %broadcast_add_fusion), kind=kLoop, calls=%fused_computation.4 | loop fusion | flops 27262976 | bytes 7667840 | tf_op jit(solution)/shard_map/convert_element_type | solution.py:61
  16.1 0.8 %fusion.8.f_ref = bf16[384,128]{1,0:T(8,128)(2,1)} fusion(f32[384]{0:T(512)S(1)} %div.61, f32[384]{0:T(512)S(1)} %div.57, f32[24,128]{1,0:T(8,128)S(1)} %iota_subtract_fusion.1, pred[24,128]{1,0:T(8,128)(4,1)S(1)} %fusion.9), kind=kLoop, calls=%fused_computation.14 | loop fusion | flops 442368 | bytes 116736 | tf_op jit(solution)/shard_map/convert_element_type | solution.py:52
  17.0 0.0 collective-permute-done.1.hi_ref
  17.0 0.0 copy-start
  17.0 4.1 %collective-permute-done.lo_ref = bf16[24,8,896]{2,1,0:T(8,128)(2,1)S(1)} collective-permute-done((bf16[24,8,896]{2,1,0:T(8,128)(2,1)S(1)}, bf16[24,8,896]{2,1,0:T(8,128)(2,1)S(1)}, u32[]{:S(2)}, u32[]{:S(2)}) %collective-permute-start) | collective-permute-done | bytes 344096 | tf_op jit(solution)/shard_map/ppermute | solution.py:40
  21.0 0.0 copy-start.1
  21.0 0.0 copy-done
  21.0 0.7 %copy-done.1 = bf16[24,8,896]{2,1,0:T(8,128)(2,1)} copy-done((bf16[24,8,896]{2,1,0:T(8,128)(2,1)}, bf16[24,8,896]{2,1,0:T(8,128)(2,1)S(1)}, u32[]{:S(2)}) %copy-start.1) | copy-done | bytes 344088
  21.7 19.1 %shard_map.41 = (bf16[24,8,896]{2,1,0:T(8,128)(2,1)}, f32[24,8,896]{2,1,0:T(8,128)}) custom-call(s32[1]{0:T(128)} %bitcast.strip_ref, bf16[384,128]{1,0:T(8,128)(2,1)} %fusion.8.f_ref, bf16[24,8,896]{2,1,0:T(8,128)(2,1)} %copy-done.1, f32[24,128,896]{2,1,0:T(8,128)} %own_ref.1, bf16[24,8,896]{2,1,0:T(8,128)(2,1)} %copy-done, ...), custom_call_target="tpu_custom_call" | custom-call | tf_op jit(solution)/shard_map/pallas_call | solution.py:142
  (6 shorter events, 0.1 us)
Async XLA Ops:
  2.1 14.9 %collective-permute-start.1 = (bf16[24,8,896]{2,1,0:T(8,128)(2,1)S(1)}, bf16[24,8,896]{2,1,0:T(8,128)(2,1)S(1)}, u32[]{:S(2)}, u32[]{:S(2)}) collective-permute-start(bf16[24,8,896]{2,1,0:T(8,128)(2,1)S(1)} %get-tuple-element.2), channel_id=1, source_target_pairs={{1,0},{2,129},{3,2},{4,131},{5,4},{6,133},{7,6},{8,135},{9,8},{10,... | collective-permute-start | bytes 1032200 | tf_op jit(solution)/shard_map/ppermute | solution.py:41
  6.3 14.7 %collective-permute-start = (bf16[24,8,896]{2,1,0:T(8,128)(2,1)S(1)}, bf16[24,8,896]{2,1,0:T(8,128)(2,1)S(1)}, u32[]{:S(2)}, u32[]{:S(2)}) collective-permute-start(bf16[24,8,896]{2,1,0:T(8,128)(2,1)S(1)} %get-tuple-element.3), channel_id=1, source_target_pairs={{0,1},{1,130},{2,3},{3,132},{4,5},{5,134},{6,7},{7,136},{8,9},{9,1... | collective-permute-start | bytes 1032200 | tf_op jit(solution)/shard_map/ppermute | solution.py:40
  17.0 4.1 %copy-start = (bf16[24,8,896]{2,1,0:T(8,128)(2,1)}, bf16[24,8,896]{2,1,0:T(8,128)(2,1)S(1)}, u32[]{:S(2)}) copy-start(bf16[24,8,896]{2,1,0:T(8,128)(2,1)S(1)} %collective-permute-done.1.hi_ref) | copy-start | bytes 1032196
  21.0 0.7 %copy-start.1 = (bf16[24,8,896]{2,1,0:T(8,128)(2,1)}, bf16[24,8,896]{2,1,0:T(8,128)(2,1)S(1)}, u32[]{:S(2)}) copy-start(bf16[24,8,896]{2,1,0:T(8,128)(2,1)S(1)} %collective-permute-done.lo_ref) | copy-start | bytes 1032196

commit v6 on v5

--- a/solution.py
+++ b/solution.py
@@ -63,50 +63,42 @@
 
 def wavelet_kernel(strip_ref, f_ref, lo_ref, own_ref, hi_ref, b_ref, peak_ref, energy_ref,
                    p_scr, g_scr, s_scr, best_scr, total_scr):
-    c = pl.program_id(0)
     count, rows, scans = g_scr.shape
     frames, strip, _ = own_ref.shape
     nb = scans // TILE
     used = 2 * HALO + frames
 
-    @pl.when(c == 0)
-    def _():
-        p_scr[used:, :] = jnp.zeros((p_scr.shape[0] - used, p_scr.shape[1]), p_scr.dtype)
-        for m in range(strip):
-            cols = slice(m * scans, (m + 1) * scans)
-            p_scr[0:HALO, cols] = lo_ref[:, m, :].astype(jnp.float32)
-            p_scr[HALO:HALO + frames, cols] = own_ref[:, m, :]
-            p_scr[HALO + frames:used, cols] = hi_ref[:, m, :].astype(jnp.float32)
-        fall = f_ref[...]
-        for m in range(strip):
-            part = p_scr[:, m * scans:(m + 1) * scans].astype(jnp.bfloat16)
-            gm = jnp.dot(fall, part, preferred_element_type=jnp.float32)
-            for cc in range(count):
-                g_scr[cc, m * frames:(m + 1) * frames, :] = gm[cc * frames:(cc + 1) * frames, :]
+    p_scr[used:, :] = jnp.zeros((p_scr.shape[0] - used, p_scr.shape[1]), p_scr.dtype)
+    for m in range(strip):
+        cols = slice(m * scans, (m + 1) * scans)
+        p_scr[0:HALO, cols] = lo_ref[:, m, :].astype(jnp.float32)
+        p_scr[HALO:HALO + frames, cols] = own_ref[:, m, :]
+        p_scr[HALO + frames:used, cols] = hi_ref[:, m, :].astype(jnp.float32)
+    fall = f_ref[...]
+    for m in range(strip):
+        part = p_scr[:, m * scans:(m + 1) * scans].astype(jnp.bfloat16)
+        gm = jnp.dot(fall, part, preferred_element_type=jnp.float32)
+        for cc in range(count):
+            g_scr[cc, m * frames:(m + 1) * frames, :] = gm[cc * frames:(cc + 1) * frames, :]
 
-    for i in range(nb):
-        for j in range(nb):
-            s_scr[i * TILE:(i + 1) * TILE, j * TILE:(j + 1) * TILE] = b_ref[0, i - j + nb - 1]
-    lhs = g_scr[c].astype(jnp.bfloat16)
-    answer = jnp.dot(lhs, s_scr[...], preferred_element_type=jnp.float32).astype(jnp.bfloat16)
-    answer = answer.astype(jnp.float32)
-    square = answer * answer
+    for c in range(count):
+        table = s_scr.at[c % 2]
+        for i in range(nb):
+            for j in range(nb):
+                table[i * TILE:(i + 1) * TILE, j * TILE:(j + 1) * TILE] = b_ref[c, i - j + nb - 1]
+        lhs = g_scr[c].astype(jnp.bfloat16)
+        answer = jnp.dot(lhs, table[...], preferred_element_type=jnp.float32).astype(jnp.bfloat16)
+        answer = answer.astype(jnp.float32)
+        if c == 0:
+            best_scr[...] = answer
+            total_scr[...] = answer * answer
+        else:
+            best_scr[...] = jnp.maximum(best_scr[...], answer)
+            total_scr[...] = total_scr[...] + answer * answer
 
-    @pl.when(c == 0)
-    def _():
-        best_scr[...] = answer
-        total_scr[...] = square
-
-    @pl.when(c > 0)
-    def _():
-        best_scr[...] = jnp.maximum(best_scr[...], answer)
-        total_scr[...] = total_scr[...] + square
-
-    @pl.when(c == count - 1)
-    def _():
-        for m in range(strip):
-            peak_ref[:, m, :] = best_scr[m * frames:(m + 1) * frames, :].astype(peak_ref.dtype)
-            energy_ref[:, m, :] = total_scr[m * frames:(m + 1) * frames, :]
+    for m in range(strip):
+        peak_ref[:, m, :] = best_scr[m * frames:(m + 1) * frames, :].astype(peak_ref.dtype)
+        energy_ref[:, m, :] = total_scr[m * frames:(m + 1) * frames, :]
 
 
 def wavelet_core(first, ftab, low, slab, high, blocks, interpret=False):
@@ -119,13 +111,13 @@
     whole3 = lambda c, i: (0, 0, 0)
     grid_spec = pltpu.PrefetchScalarGridSpec(
         num_scalar_prefetch=1,
-        grid=(count,),
+        grid=(1,),
         in_specs=[
             pl.BlockSpec((count * frames, depth), whole),
             pl.BlockSpec((HALO, strip, scans), whole3),
             pl.BlockSpec((frames, strip, scans), lambda c, i: (0, i[0], 0)),
             pl.BlockSpec((HALO, strip, scans), whole3),
-            pl.BlockSpec((1, nblk, TILE, TILE), lambda c, i: (c, 0, 0, 0)),
+            pl.BlockSpec((count, nblk, TILE, TILE), lambda c, i: (0, 0, 0, 0)),
         ],
         out_specs=[
             pl.BlockSpec((frames, strip, scans), whole3),
@@ -134,7 +126,7 @@
         scratch_shapes=[
             pltpu.VMEM((depth, strip * scans), jnp.float32),
             pltpu.VMEM((count, rows, scans), jnp.float32),
-            pltpu.VMEM((scans, scans), jnp.bfloat16),
+            pltpu.VMEM((2, scans, scans), jnp.bfloat16),
             pltpu.VMEM((rows, scans), jnp.float32),
             pltpu.VMEM((rows, scans), jnp.float32),
         ],

time: 41.3 us -> 37.2 us (0.901)
  Pallas kernels: 19.1 us -> 15.3 us
    pallas_call x1, Pallas kernels: 19.1 us -> 15.3 us  [wavelet_core(): pl.pallas_call(wavelet_kernel, grid_spec=grid_spec, out_shape=[jax.ShapeD...]
  transfers between devices with their start and end apart: 2 -> 2, of which waited for: 1 -> 1; matrix products, arithmetic and copies ran while one was open for 21% -> 23% of each run, Pallas kernels for 0% -> 0%
where the time goes in v6:
time: 37.2 us; the launch traced here: 37.1 us
  Pallas kernels  15.3 us (41%)
  other arithmetic  8.38 us (23%)
  starting transfers between devices  6.13 us (16%)
  waiting for transfers between devices  4.06 us (11%)
  local copies, waits for them, and re-layouts  2.44 us (7%)
  between operations  0.73 us (2%)
    pallas_call x1, Pallas kernels, wavelet_core(): pl.pallas_call(wavelet_kernel, grid_spec=grid_spec, out_shape=[jax.ShapeD...  15.3 us
    convert_element_type x1, other arithmetic, scan_blocks(): return mexican(offsets[None], spread).astype(jnp.bfloat16)  6.05 us
    ppermute x1, starting transfers between devices, halos(): high = lax.ppermute(send_bwd, ('scale', 'rt'), backward)  4.21 us
    ppermute x1, waiting for transfers between devices, halos(): low = lax.ppermute(send_fwd, ('scale', 'rt'), forward)  4.05 us
    ppermute x1, starting transfers between devices, halos(): low = lax.ppermute(send_fwd, ('scale', 'rt'), forward)  1.92 us
    convert_element_type x1, local copies, waits for them, and re-layouts, piece(): return part.astype(jnp.bfloat16)  1.39 us
    convert_element_type x1, other arithmetic, frame_tables(): return values.astype(jnp.bfloat16).reshape(-1, depth)  0.81 us
  transfers between devices with their start and end apart: 2, of which 1 were waited for; matrix products, arithmetic and copies ran while one was open for 23% of the time, Pallas kernels for 0%

profile of v6, /device:TPU:136, one launch (start us, length us, event | category | flops | bytes accessed | tf_op | source)
XLA Modules:
  0.0 37.1 jit_solution(12525916180497590336)
XLA Ops:
  0.7 1.4 %dynamic-slice_convert_fusion = (bf16[24,8,896]{2,1,0:T(8,128)(2,1)S(1)}, bf16[24,8,896]{2,1,0:T(8,128)(2,1)S(1)}) fusion(f32[24,128,896]{2,1,0:T(8,128)} %own_ref.1, s32[]{:T(128)S(6)} %select_n.36, s32[]{:T(128)S(6)} %select_n.34), kind=kLoop, calls=%fused_computation.5 | loop fusion | bytes 1376264 | tf_op jit(solution)/shard_map/convert_element_type | solution.py:36
  2.1 4.2 %collective-permute-start.1 = (bf16[24,8,896]{2,1,0:T(8,128)(2,1)S(1)}, bf16[24,8,896]{2,1,0:T(8,128)(2,1)S(1)}, u32[]{:S(2)}, u32[]{:S(2)}) collective-permute-start(bf16[24,8,896]{2,1,0:T(8,128)(2,1)S(1)} %get-tuple-element.2), channel_id=1, source_target_pairs={{1,0},{2,129},{3,2},{4,131},{5,4},{6,133},{7,6},{8,135},{9,8},{10,... | collective-permute-start | bytes 1032200 | tf_op jit(solution)/shard_map/ppermute | solution.py:41
  6.3 1.9 %collective-permute-start = (bf16[24,8,896]{2,1,0:T(8,128)(2,1)S(1)}, bf16[24,8,896]{2,1,0:T(8,128)(2,1)S(1)}, u32[]{:S(2)}, u32[]{:S(2)}) collective-permute-start(bf16[24,8,896]{2,1,0:T(8,128)(2,1)S(1)} %get-tuple-element.3), channel_id=1, source_target_pairs={{0,1},{1,130},{2,3},{3,132},{4,5},{5,134},{6,7},{7,136},{8,9},{9,1... | collective-permute-start | bytes 1032200 | tf_op jit(solution)/shard_map/ppermute | solution.py:40
  8.2 0.7 %convert_element_type.16 = f32[16]{0:T(128)S(1)} convert(s32[16]{0:T(128)} %param.3) | non-fusion elementwise | flops 16 | bytes 128 | tf_op jit(solution)/shard_map/convert_element_type | solution.py:151
  8.9 0.7 %broadcast_multiply_fusion = (f32[16]{0:T(128)S(1)}, f32[16]{0:T(128)S(1)}, f32[16]{0:T(128)S(1)}) fusion(s32[16]{0:T(128)} %param.3), kind=kLoop, calls=%fused_computation.21 | loop fusion | flops 32 | bytes 256 | tf_op jit(solution)/shard_map/mul | solution.py:60
  9.6 0.1 div.56
  9.7 0.1 div.57
  9.8 0.1 div.60
  9.8 0.1 div.61
  9.9 0.1 broadcast_add_fusion
  10.1 6.0 %fusion.3.b_ref = bf16[16,13,128,128]{3,2,1,0:T(8,128)(2,1)} fusion(f32[16]{0:T(128)S(1)} %get-tuple-element.5, f32[16]{0:T(128)S(1)} %get-tuple-element.4, f32[13,128,128]{2,1,0:T(8,128)S(1)} %broadcast_add_fusion), kind=kLoop, calls=%fused_computation.4 | loop fusion | flops 27262976 | bytes 7667840 | tf_op jit(solution)/shard_map/convert_element_type | solution.py:61
  16.1 0.8 %fusion.8.f_ref = bf16[384,128]{1,0:T(8,128)(2,1)} fusion(f32[384]{0:T(512)S(1)} %div.61, f32[384]{0:T(512)S(1)} %div.57, f32[24,128]{1,0:T(8,128)S(1)} %iota_subtract_fusion.1, pred[24,128]{1,0:T(8,128)(4,1)S(1)} %fusion.9), kind=kLoop, calls=%fused_computation.14 | loop fusion | flops 442368 | bytes 116736 | tf_op jit(solution)/shard_map/convert_element_type | solution.py:52
  17.0 0.0 collective-permute-done.1.hi_ref
  17.0 0.0 copy-start
  17.0 4.1 %collective-permute-done.lo_ref = bf16[24,8,896]{2,1,0:T(8,128)(2,1)S(1)} collective-permute-done((bf16[24,8,896]{2,1,0:T(8,128)(2,1)S(1)}, bf16[24,8,896]{2,1,0:T(8,128)(2,1)S(1)}, u32[]{:S(2)}, u32[]{:S(2)}) %collective-permute-start) | collective-permute-done | bytes 344096 | tf_op jit(solution)/shard_map/ppermute | solution.py:40
  21.0 0.0 copy-start.1
  21.0 0.0 copy-done
  21.0 0.7 %copy-done.1 = bf16[24,8,896]{2,1,0:T(8,128)(2,1)} copy-done((bf16[24,8,896]{2,1,0:T(8,128)(2,1)}, bf16[24,8,896]{2,1,0:T(8,128)(2,1)S(1)}, u32[]{:S(2)}) %copy-start.1) | copy-done | bytes 344088
  21.7 15.3 %shard_map.41 = (bf16[24,8,896]{2,1,0:T(8,128)(2,1)}, f32[24,8,896]{2,1,0:T(8,128)}) custom-call(s32[1]{0:T(128)} %bitcast.strip_ref, bf16[384,128]{1,0:T(8,128)(2,1)} %fusion.8.f_ref, bf16[24,8,896]{2,1,0:T(8,128)(2,1)} %copy-done.1, f32[24,128,896]{2,1,0:T(8,128)} %own_ref.1, bf16[24,8,896]{2,1,0:T(8,128)(2,1)} %copy-done, ...), custom_call_target="tpu_custom_call" | custom-call | tf_op jit(solution)/shard_map/pallas_call | solution.py:134
  (6 shorter events, 0.1 us)
Async XLA Ops:
  2.1 14.9 %collective-permute-start.1 = (bf16[24,8,896]{2,1,0:T(8,128)(2,1)S(1)}, bf16[24,8,896]{2,1,0:T(8,128)(2,1)S(1)}, u32[]{:S(2)}, u32[]{:S(2)}) collective-permute-start(bf16[24,8,896]{2,1,0:T(8,128)(2,1)S(1)} %get-tuple-element.2), channel_id=1, source_target_pairs={{1,0},{2,129},{3,2},{4,131},{5,4},{6,133},{7,6},{8,135},{9,8},{10,... | collective-permute-start | bytes 1032200 | tf_op jit(solution)/shard_map/ppermute | solution.py:41
  6.3 14.7 %collective-permute-start = (bf16[24,8,896]{2,1,0:T(8,128)(2,1)S(1)}, bf16[24,8,896]{2,1,0:T(8,128)(2,1)S(1)}, u32[]{:S(2)}, u32[]{:S(2)}) collective-permute-start(bf16[24,8,896]{2,1,0:T(8,128)(2,1)S(1)} %get-tuple-element.3), channel_id=1, source_target_pairs={{0,1},{1,130},{2,3},{3,132},{4,5},{5,134},{6,7},{7,136},{8,9},{9,1... | collective-permute-start | bytes 1032200 | tf_op jit(solution)/shard_map/ppermute | solution.py:40
  17.0 4.1 %copy-start = (bf16[24,8,896]{2,1,0:T(8,128)(2,1)}, bf16[24,8,896]{2,1,0:T(8,128)(2,1)S(1)}, u32[]{:S(2)}) copy-start(bf16[24,8,896]{2,1,0:T(8,128)(2,1)S(1)} %collective-permute-done.1.hi_ref) | copy-start | bytes 1032196
  21.0 0.7 %copy-start.1 = (bf16[24,8,896]{2,1,0:T(8,128)(2,1)}, bf16[24,8,896]{2,1,0:T(8,128)(2,1)S(1)}, u32[]{:S(2)}) copy-start(bf16[24,8,896]{2,1,0:T(8,128)(2,1)S(1)} %collective-permute-done.lo_ref) | copy-start | bytes 1032196

commit v7 on v6

--- a/solution.py
+++ b/solution.py
@@ -61,19 +61,33 @@
     return mexican(offsets[None], spread).astype(jnp.bfloat16)
 
 
-def wavelet_kernel(strip_ref, f_ref, lo_ref, own_ref, hi_ref, b_ref, peak_ref, energy_ref,
-                   p_scr, g_scr, s_scr, best_scr, total_scr):
+def wavelet_kernel(strip_ref, f_ref, lo_hbm, own_ref, hi_hbm, b_hbm, peak_ref, energy_ref,
+                   lo_buf, hi_buf, b_buf, sem, p_scr, g_scr, s_scr, best_scr, total_scr):
     count, rows, scans = g_scr.shape
     frames, strip, _ = own_ref.shape
     nb = scans // TILE
     used = 2 * HALO + frames
 
+    def table_copy(c):
+        return pltpu.make_async_copy(b_hbm.at[c], b_buf.at[c % 2], sem.at[c % 2])
+
+    lo_copy = pltpu.make_async_copy(lo_hbm, lo_buf, sem.at[2])
+    hi_copy = pltpu.make_async_copy(hi_hbm, hi_buf, sem.at[3])
+    lo_copy.start()
+    hi_copy.start()
+    table_copy(0).start()
+    table_copy(1).start()
+
     p_scr[used:, :] = jnp.zeros((p_scr.shape[0] - used, p_scr.shape[1]), p_scr.dtype)
     for m in range(strip):
         cols = slice(m * scans, (m + 1) * scans)
-        p_scr[0:HALO, cols] = lo_ref[:, m, :].astype(jnp.float32)
         p_scr[HALO:HALO + frames, cols] = own_ref[:, m, :]
-        p_scr[HALO + frames:used, cols] = hi_ref[:, m, :].astype(jnp.float32)
+    lo_copy.wait()
+    hi_copy.wait()
+    for m in range(strip):
+        cols = slice(m * scans, (m + 1) * scans)
+        p_scr[0:HALO, cols] = lo_buf[:, m, :].astype(jnp.float32)
+        p_scr[HALO + frames:used, cols] = hi_buf[:, m, :].astype(jnp.float32)
     fall = f_ref[...]
     for m in range(strip):
         part = p_scr[:, m * scans:(m + 1) * scans].astype(jnp.bfloat16)
@@ -83,9 +97,13 @@
 
     for c in range(count):
         table = s_scr.at[c % 2]
+        blocks = b_buf.at[c % 2]
+        table_copy(c).wait()
         for i in range(nb):
             for j in range(nb):
-                table[i * TILE:(i + 1) * TILE, j * TILE:(j + 1) * TILE] = b_ref[c, i - j + nb - 1]
+                table[i * TILE:(i + 1) * TILE, j * TILE:(j + 1) * TILE] = blocks[i - j + nb - 1]
+        if c + 2 < count:
+            table_copy(c + 2).start()
         lhs = g_scr[c].astype(jnp.bfloat16)
         answer = jnp.dot(lhs, table[...], preferred_element_type=jnp.float32).astype(jnp.bfloat16)
         answer = answer.astype(jnp.float32)
@@ -114,16 +132,20 @@
         grid=(1,),
         in_specs=[
             pl.BlockSpec((count * frames, depth), whole),
-            pl.BlockSpec((HALO, strip, scans), whole3),
+            pl.BlockSpec(memory_space=pl.ANY),
             pl.BlockSpec((frames, strip, scans), lambda c, i: (0, i[0], 0)),
-            pl.BlockSpec((HALO, strip, scans), whole3),
-            pl.BlockSpec((count, nblk, TILE, TILE), lambda c, i: (0, 0, 0, 0)),
+            pl.BlockSpec(memory_space=pl.ANY),
+            pl.BlockSpec(memory_space=pl.ANY),
         ],
         out_specs=[
             pl.BlockSpec((frames, strip, scans), whole3),
             pl.BlockSpec((frames, strip, scans), whole3),
         ],
         scratch_shapes=[
+            pltpu.VMEM((HALO, strip, scans), low.dtype),
+            pltpu.VMEM((HALO, strip, scans), high.dtype),
+            pltpu.VMEM((2, nblk, TILE, TILE), blocks.dtype),
+            pltpu.SemaphoreType.DMA((4,)),
             pltpu.VMEM((depth, strip * scans), jnp.float32),
             pltpu.VMEM((count, rows, scans), jnp.float32),
             pltpu.VMEM((2, scans, scans), jnp.bfloat16),

time: 37.2 us -> 39.1 us (1.051)
  Pallas kernels: 15.3 us -> 17 us
    pallas_call x1, Pallas kernels: 15.3 us -> 17 us  [wavelet_core(): pl.pallas_call(wavelet_kernel, grid_spec=grid_spec, out_shape=[jax.ShapeD...]
  transfers between devices with their start and end apart: 2 -> 2, of which waited for: 1 -> 1; matrix products, arithmetic and copies ran while one was open for 23% -> 22% of each run, Pallas kernels for 0% -> 0%
where the time goes in v7:
time: 39.1 us; the launch traced here: 38.7 us
  Pallas kernels  17 us (43%)
  other arithmetic  8.38 us (21%)
  starting transfers between devices  6.13 us (16%)
  waiting for transfers between devices  4.06 us (10%)
  local copies, waits for them, and re-layouts  2.44 us (6%)
  between operations  0.73 us (2%)
    pallas_call x1, Pallas kernels, wavelet_core(): pl.pallas_call(wavelet_kernel, grid_spec=grid_spec, out_shape=[jax.ShapeD...  17 us
    convert_element_type x1, other arithmetic, scan_blocks(): return mexican(offsets[None], spread).astype(jnp.bfloat16)  6.05 us
    ppermute x1, starting transfers between devices, halos(): high = lax.ppermute(send_bwd, ('scale', 'rt'), backward)  4.21 us
    ppermute x1, waiting for transfers between devices, halos(): low = lax.ppermute(send_fwd, ('scale', 'rt'), forward)  4.05 us
    ppermute x1, starting transfers between devices, halos(): low = lax.ppermute(send_fwd, ('scale', 'rt'), forward)  1.92 us
    convert_element_type x1, local copies, waits for them, and re-layouts, piece(): return part.astype(jnp.bfloat16)  1.39 us
    convert_element_type x1, other arithmetic, frame_tables(): return values.astype(jnp.bfloat16).reshape(-1, depth)  0.81 us
  transfers between devices with their start and end apart: 2, of which 1 were waited for; matrix products, arithmetic and copies ran while one was open for 22% of the time, Pallas kernels for 0%

profile of v7, /device:TPU:136, one launch (start us, length us, event | category | flops | bytes accessed | tf_op | source)
XLA Modules:
  0.0 38.7 jit_solution(648786906996743844)
XLA Ops:
  0.7 1.4 %dynamic-slice_convert_fusion = (bf16[24,8,896]{2,1,0:T(8,128)(2,1)S(1)}, bf16[24,8,896]{2,1,0:T(8,128)(2,1)S(1)}) fusion(f32[24,128,896]{2,1,0:T(8,128)} %own_ref.1, s32[]{:T(128)S(6)} %select_n.36, s32[]{:T(128)S(6)} %select_n.34), kind=kLoop, calls=%fused_computation.5 | loop fusion | bytes 1376264 | tf_op jit(solution)/shard_map/convert_element_type | solution.py:36
  2.1 4.2 %collective-permute-start.1 = (bf16[24,8,896]{2,1,0:T(8,128)(2,1)S(1)}, bf16[24,8,896]{2,1,0:T(8,128)(2,1)S(1)}, u32[]{:S(2)}, u32[]{:S(2)}) collective-permute-start(bf16[24,8,896]{2,1,0:T(8,128)(2,1)S(1)} %get-tuple-element.2), channel_id=1, source_target_pairs={{1,0},{2,129},{3,2},{4,131},{5,4},{6,133},{7,6},{8,135},{9,8},{10,... | collective-permute-start | bytes 1032200 | tf_op jit(solution)/shard_map/ppermute | solution.py:41
  6.3 1.9 %collective-permute-start = (bf16[24,8,896]{2,1,0:T(8,128)(2,1)S(1)}, bf16[24,8,896]{2,1,0:T(8,128)(2,1)S(1)}, u32[]{:S(2)}, u32[]{:S(2)}) collective-permute-start(bf16[24,8,896]{2,1,0:T(8,128)(2,1)S(1)} %get-tuple-element.3), channel_id=1, source_target_pairs={{0,1},{1,130},{2,3},{3,132},{4,5},{5,134},{6,7},{7,136},{8,9},{9,1... | collective-permute-start | bytes 1032200 | tf_op jit(solution)/shard_map/ppermute | solution.py:40
  8.2 0.7 %convert_element_type.16 = f32[16]{0:T(128)S(1)} convert(s32[16]{0:T(128)} %param.3) | non-fusion elementwise | flops 16 | bytes 128 | tf_op jit(solution)/shard_map/convert_element_type | solution.py:173
  8.9 0.7 %broadcast_multiply_fusion = (f32[16]{0:T(128)S(1)}, f32[16]{0:T(128)S(1)}, f32[16]{0:T(128)S(1)}) fusion(s32[16]{0:T(128)} %param.3), kind=kLoop, calls=%fused_computation.21 | loop fusion | flops 32 | bytes 256 | tf_op jit(solution)/shard_map/mul | solution.py:60
  9.6 0.1 div.56
  9.7 0.1 div.57
  9.8 0.1 div.60
  9.8 0.1 div.61
  9.9 0.1 broadcast_add_fusion
  10.1 6.0 %fusion.3.b_hbm = bf16[16,13,128,128]{3,2,1,0:T(8,128)(2,1)} fusion(f32[16]{0:T(128)S(1)} %get-tuple-element.5, f32[16]{0:T(128)S(1)} %get-tuple-element.4, f32[13,128,128]{2,1,0:T(8,128)S(1)} %broadcast_add_fusion), kind=kLoop, calls=%fused_computation.4 | loop fusion | flops 27262976 | bytes 7667840 | tf_op jit(solution)/shard_map/convert_element_type | solution.py:61
  16.1 0.8 %fusion.8.f_ref = bf16[384,128]{1,0:T(8,128)(2,1)} fusion(f32[384]{0:T(512)S(1)} %div.61, f32[384]{0:T(512)S(1)} %div.57, f32[24,128]{1,0:T(8,128)S(1)} %iota_subtract_fusion.1, pred[24,128]{1,0:T(8,128)(4,1)S(1)} %fusion.9), kind=kLoop, calls=%fused_computation.14 | loop fusion | flops 442368 | bytes 116736 | tf_op jit(solution)/shard_map/convert_element_type | solution.py:52
  17.0 0.0 collective-permute-done.1.hi_hbm
  17.0 0.0 copy-start
  17.0 4.1 %collective-permute-done.lo_hbm = bf16[24,8,896]{2,1,0:T(8,128)(2,1)S(1)} collective-permute-done((bf16[24,8,896]{2,1,0:T(8,128)(2,1)S(1)}, bf16[24,8,896]{2,1,0:T(8,128)(2,1)S(1)}, u32[]{:S(2)}, u32[]{:S(2)}) %collective-permute-start) | collective-permute-done | bytes 344096 | tf_op jit(solution)/shard_map/ppermute | solution.py:40
  21.0 0.0 copy-start.1
  21.0 0.0 copy-done
  21.0 0.7 %copy-done.1 = bf16[24,8,896]{2,1,0:T(8,128)(2,1)} copy-done((bf16[24,8,896]{2,1,0:T(8,128)(2,1)}, bf16[24,8,896]{2,1,0:T(8,128)(2,1)S(1)}, u32[]{:S(2)}) %copy-start.1) | copy-done | bytes 344088
  21.7 17.0 %shard_map.41 = (bf16[24,8,896]{2,1,0:T(8,128)(2,1)}, f32[24,8,896]{2,1,0:T(8,128)}) custom-call(s32[1]{0:T(128)} %bitcast.strip_ref, bf16[384,128]{1,0:T(8,128)(2,1)} %fusion.8.f_ref, bf16[24,8,896]{2,1,0:T(8,128)(2,1)} %copy-done.1, f32[24,128,896]{2,1,0:T(8,128)} %own_ref.1, bf16[24,8,896]{2,1,0:T(8,128)(2,1)} %copy-done, ...), custom_call_target="tpu_custom_call" | custom-call | tf_op jit(solution)/shard_map/pallas_call | solution.py:156
  (6 shorter events, 0.1 us)
Async XLA Ops:
  2.1 14.9 %collective-permute-start.1 = (bf16[24,8,896]{2,1,0:T(8,128)(2,1)S(1)}, bf16[24,8,896]{2,1,0:T(8,128)(2,1)S(1)}, u32[]{:S(2)}, u32[]{:S(2)}) collective-permute-start(bf16[24,8,896]{2,1,0:T(8,128)(2,1)S(1)} %get-tuple-element.2), channel_id=1, source_target_pairs={{1,0},{2,129},{3,2},{4,131},{5,4},{6,133},{7,6},{8,135},{9,8},{10,... | collective-permute-start | bytes 1032200 | tf_op jit(solution)/shard_map/ppermute | solution.py:41
  6.3 14.7 %collective-permute-start = (bf16[24,8,896]{2,1,0:T(8,128)(2,1)S(1)}, bf16[24,8,896]{2,1,0:T(8,128)(2,1)S(1)}, u32[]{:S(2)}, u32[]{:S(2)}) collective-permute-start(bf16[24,8,896]{2,1,0:T(8,128)(2,1)S(1)} %get-tuple-element.3), channel_id=1, source_target_pairs={{0,1},{1,130},{2,3},{3,132},{4,5},{5,134},{6,7},{7,136},{8,9},{9,1... | collective-permute-start | bytes 1032200 | tf_op jit(solution)/shard_map/ppermute | solution.py:40
  17.0 4.1 %copy-start = (bf16[24,8,896]{2,1,0:T(8,128)(2,1)}, bf16[24,8,896]{2,1,0:T(8,128)(2,1)S(1)}, u32[]{:S(2)}) copy-start(bf16[24,8,896]{2,1,0:T(8,128)(2,1)S(1)} %collective-permute-done.1.hi_hbm) | copy-start | bytes 1032196
  21.0 0.7 %copy-start.1 = (bf16[24,8,896]{2,1,0:T(8,128)(2,1)}, bf16[24,8,896]{2,1,0:T(8,128)(2,1)S(1)}, u32[]{:S(2)}) copy-start(bf16[24,8,896]{2,1,0:T(8,128)(2,1)S(1)} %collective-permute-done.lo_hbm) | copy-start | bytes 1032196

commit v8 on v5

--- a/solution.py
+++ b/solution.py
@@ -8,6 +8,7 @@
 SCAN_RATIO = 16
 HALO = 24
 TILE = 128
+STEPS = 2
 
 
 def mexican(offsets, spread):
@@ -63,13 +64,14 @@
 
 def wavelet_kernel(strip_ref, f_ref, lo_ref, own_ref, hi_ref, b_ref, peak_ref, energy_ref,
                    p_scr, g_scr, s_scr, best_scr, total_scr):
-    c = pl.program_id(0)
+    step = pl.program_id(0)
     count, rows, scans = g_scr.shape
+    per = b_ref.shape[0]
     frames, strip, _ = own_ref.shape
     nb = scans // TILE
     used = 2 * HALO + frames
 
-    @pl.when(c == 0)
+    @pl.when(step == 0)
     def _():
         p_scr[used:, :] = jnp.zeros((p_scr.shape[0] - used, p_scr.shape[1]), p_scr.dtype)
         for m in range(strip):
@@ -83,26 +85,21 @@
             gm = jnp.dot(fall, part, preferred_element_type=jnp.float32)
             for cc in range(count):
                 g_scr[cc, m * frames:(m + 1) * frames, :] = gm[cc * frames:(cc + 1) * frames, :]
+        best_scr[...] = jnp.full(best_scr.shape, -jnp.inf, best_scr.dtype)
+        total_scr[...] = jnp.zeros(total_scr.shape, total_scr.dtype)
 
-    for i in range(nb):
-        for j in range(nb):
-            s_scr[i * TILE:(i + 1) * TILE, j * TILE:(j + 1) * TILE] = b_ref[0, i - j + nb - 1]
-    lhs = g_scr[c].astype(jnp.bfloat16)
-    answer = jnp.dot(lhs, s_scr[...], preferred_element_type=jnp.float32).astype(jnp.bfloat16)
-    answer = answer.astype(jnp.float32)
-    square = answer * answer
+    for k in range(per):
+        table = s_scr.at[k % 2]
+        for i in range(nb):
+            for j in range(nb):
+                table[i * TILE:(i + 1) * TILE, j * TILE:(j + 1) * TILE] = b_ref[k, i - j + nb - 1]
+        lhs = g_scr[step * per + k].astype(jnp.bfloat16)
+        answer = jnp.dot(lhs, table[...], preferred_element_type=jnp.float32).astype(jnp.bfloat16)
+        answer = answer.astype(jnp.float32)
+        best_scr[...] = jnp.maximum(best_scr[...], answer)
+        total_scr[...] = total_scr[...] + answer * answer
 
-    @pl.when(c == 0)
-    def _():
-        best_scr[...] = answer
-        total_scr[...] = square
-
-    @pl.when(c > 0)
-    def _():
-        best_scr[...] = jnp.maximum(best_scr[...], answer)
-        total_scr[...] = total_scr[...] + square
-
-    @pl.when(c == count - 1)
+    @pl.when(step == pl.num_programs(0) - 1)
     def _():
         for m in range(strip):
             peak_ref[:, m, :] = best_scr[m * frames:(m + 1) * frames, :].astype(peak_ref.dtype)
@@ -119,13 +116,13 @@
     whole3 = lambda c, i: (0, 0, 0)
     grid_spec = pltpu.PrefetchScalarGridSpec(
         num_scalar_prefetch=1,
-        grid=(count,),
+        grid=(STEPS,),
         in_specs=[
             pl.BlockSpec((count * frames, depth), whole),
             pl.BlockSpec((HALO, strip, scans), whole3),
             pl.BlockSpec((frames, strip, scans), lambda c, i: (0, i[0], 0)),
             pl.BlockSpec((HALO, strip, scans), whole3),
-            pl.BlockSpec((1, nblk, TILE, TILE), lambda c, i: (c, 0, 0, 0)),
+            pl.BlockSpec((count // STEPS, nblk, TILE, TILE), lambda c, i: (c, 0, 0, 0)),
         ],
         out_specs=[
             pl.BlockSpec((frames, strip, scans), whole3),
@@ -134,7 +131,7 @@
         scratch_shapes=[
             pltpu.VMEM((depth, strip * scans), jnp.float32),
             pltpu.VMEM((count, rows, scans), jnp.float32),
-            pltpu.VMEM((scans, scans), jnp.bfloat16),
+            pltpu.VMEM((2, scans, scans), jnp.bfloat16),
             pltpu.VMEM((rows, scans), jnp.float32),
             pltpu.VMEM((rows, scans), jnp.float32),
         ],

time: 41.3 us -> 37.6 us (0.910)
  Pallas kernels: 19.1 us -> 15.7 us
    pallas_call x1, Pallas kernels: 19.1 us -> 15.7 us  [wavelet_core(): pl.pallas_call(wavelet_kernel, grid_spec=grid_spec, out_shape=[jax.ShapeD...]
  transfers between devices with their start and end apart: 2 -> 2, of which waited for: 1 -> 1; matrix products, arithmetic and copies ran while one was open for 21% -> 23% of each run, Pallas kernels for 0% -> 0%
where the time goes in v8:
time: 37.6 us; the launch traced here: 37.4 us
  Pallas kernels  15.7 us (42%)
  other arithmetic  8.38 us (22%)
  starting transfers between devices  6.13 us (16%)
  waiting for transfers between devices  4.06 us (11%)
  local copies, waits for them, and re-layouts  2.44 us (6%)
  between operations  0.73 us (2%)
    pallas_call x1, Pallas kernels, wavelet_core(): pl.pallas_call(wavelet_kernel, grid_spec=grid_spec, out_shape=[jax.ShapeD...  15.7 us
    convert_element_type x1, other arithmetic, scan_blocks(): return mexican(offsets[None], spread).astype(jnp.bfloat16)  6.05 us
    ppermute x1, starting transfers between devices, halos(): high = lax.ppermute(send_bwd, ('scale', 'rt'), backward)  4.21 us
    ppermute x1, waiting for transfers between devices, halos(): low = lax.ppermute(send_fwd, ('scale', 'rt'), forward)  4.05 us
    ppermute x1, starting transfers between devices, halos(): low = lax.ppermute(send_fwd, ('scale', 'rt'), forward)  1.92 us
    convert_element_type x1, local copies, waits for them, and re-layouts, piece(): return part.astype(jnp.bfloat16)  1.39 us
    convert_element_type x1, other arithmetic, frame_tables(): return values.astype(jnp.bfloat16).reshape(-1, depth)  0.81 us
  transfers between devices with their start and end apart: 2, of which 1 were waited for; matrix products, arithmetic and copies ran while one was open for 23% of the time, Pallas kernels for 0%

profile of v8, /device:TPU:136, one launch (start us, length us, event | category | flops | bytes accessed | tf_op | source)
XLA Modules:
  0.0 37.4 jit_solution(12763644198247023074)
XLA Ops:
  0.7 1.4 %dynamic-slice_convert_fusion = (bf16[24,8,896]{2,1,0:T(8,128)(2,1)S(1)}, bf16[24,8,896]{2,1,0:T(8,128)(2,1)S(1)}) fusion(f32[24,128,896]{2,1,0:T(8,128)} %own_ref.1, s32[]{:T(128)S(6)} %select_n.36, s32[]{:T(128)S(6)} %select_n.34), kind=kLoop, calls=%fused_computation.5 | loop fusion | bytes 1376264 | tf_op jit(solution)/shard_map/convert_element_type | solution.py:37
  2.1 4.2 %collective-permute-start.1 = (bf16[24,8,896]{2,1,0:T(8,128)(2,1)S(1)}, bf16[24,8,896]{2,1,0:T(8,128)(2,1)S(1)}, u32[]{:S(2)}, u32[]{:S(2)}) collective-permute-start(bf16[24,8,896]{2,1,0:T(8,128)(2,1)S(1)} %get-tuple-element.2), channel_id=1, source_target_pairs={{1,0},{2,129},{3,2},{4,131},{5,4},{6,133},{7,6},{8,135},{9,8},{10,... | collective-permute-start | bytes 1032200 | tf_op jit(solution)/shard_map/ppermute | solution.py:42
  6.3 1.9 %collective-permute-start = (bf16[24,8,896]{2,1,0:T(8,128)(2,1)S(1)}, bf16[24,8,896]{2,1,0:T(8,128)(2,1)S(1)}, u32[]{:S(2)}, u32[]{:S(2)}) collective-permute-start(bf16[24,8,896]{2,1,0:T(8,128)(2,1)S(1)} %get-tuple-element.3), channel_id=1, source_target_pairs={{0,1},{1,130},{2,3},{3,132},{4,5},{5,134},{6,7},{7,136},{8,9},{9,1... | collective-permute-start | bytes 1032200 | tf_op jit(solution)/shard_map/ppermute | solution.py:41
  8.2 0.7 %convert_element_type.16 = f32[16]{0:T(128)S(1)} convert(s32[16]{0:T(128)} %param.3) | non-fusion elementwise | flops 16 | bytes 128 | tf_op jit(solution)/shard_map/convert_element_type | solution.py:156
  8.9 0.7 %broadcast_multiply_fusion = (f32[16]{0:T(128)S(1)}, f32[16]{0:T(128)S(1)}, f32[16]{0:T(128)S(1)}) fusion(s32[16]{0:T(128)} %param.3), kind=kLoop, calls=%fused_computation.21 | loop fusion | flops 32 | bytes 256 | tf_op jit(solution)/shard_map/mul | solution.py:61
  9.6 0.1 div.56
  9.7 0.1 div.57
  9.8 0.1 div.60
  9.8 0.1 div.61
  9.9 0.1 broadcast_add_fusion
  10.1 6.0 %fusion.3.b_ref = bf16[16,13,128,128]{3,2,1,0:T(8,128)(2,1)} fusion(f32[16]{0:T(128)S(1)} %get-tuple-element.5, f32[16]{0:T(128)S(1)} %get-tuple-element.4, f32[13,128,128]{2,1,0:T(8,128)S(1)} %broadcast_add_fusion), kind=kLoop, calls=%fused_computation.4 | loop fusion | flops 27262976 | bytes 7667840 | tf_op jit(solution)/shard_map/convert_element_type | solution.py:62
  16.1 0.8 %fusion.8.f_ref = bf16[384,128]{1,0:T(8,128)(2,1)} fusion(f32[384]{0:T(512)S(1)} %div.61, f32[384]{0:T(512)S(1)} %div.57, f32[24,128]{1,0:T(8,128)S(1)} %iota_subtract_fusion.1, pred[24,128]{1,0:T(8,128)(4,1)S(1)} %fusion.9), kind=kLoop, calls=%fused_computation.14 | loop fusion | flops 442368 | bytes 116736 | tf_op jit(solution)/shard_map/convert_element_type | solution.py:53
  17.0 0.0 collective-permute-done.1.hi_ref
  17.0 0.0 copy-start
  17.0 4.1 %collective-permute-done.lo_ref = bf16[24,8,896]{2,1,0:T(8,128)(2,1)S(1)} collective-permute-done((bf16[24,8,896]{2,1,0:T(8,128)(2,1)S(1)}, bf16[24,8,896]{2,1,0:T(8,128)(2,1)S(1)}, u32[]{:S(2)}, u32[]{:S(2)}) %collective-permute-start) | collective-permute-done | bytes 344096 | tf_op jit(solution)/shard_map/ppermute | solution.py:41
  21.0 0.0 copy-start.1
  21.0 0.0 copy-done
  21.0 0.7 %copy-done.1 = bf16[24,8,896]{2,1,0:T(8,128)(2,1)} copy-done((bf16[24,8,896]{2,1,0:T(8,128)(2,1)}, bf16[24,8,896]{2,1,0:T(8,128)(2,1)S(1)}, u32[]{:S(2)}) %copy-start.1) | copy-done | bytes 344088
  21.7 15.7 %shard_map.41 = (bf16[24,8,896]{2,1,0:T(8,128)(2,1)}, f32[24,8,896]{2,1,0:T(8,128)}) custom-call(s32[1]{0:T(128)} %bitcast.strip_ref, bf16[384,128]{1,0:T(8,128)(2,1)} %fusion.8.f_ref, bf16[24,8,896]{2,1,0:T(8,128)(2,1)} %copy-done.1, f32[24,128,896]{2,1,0:T(8,128)} %own_ref.1, bf16[24,8,896]{2,1,0:T(8,128)(2,1)} %copy-done, ...), custom_call_target="tpu_custom_call" | custom-call | tf_op jit(solution)/shard_map/pallas_call | solution.py:139
  (6 shorter events, 0.1 us)
Async XLA Ops:
  2.1 14.9 %collective-permute-start.1 = (bf16[24,8,896]{2,1,0:T(8,128)(2,1)S(1)}, bf16[24,8,896]{2,1,0:T(8,128)(2,1)S(1)}, u32[]{:S(2)}, u32[]{:S(2)}) collective-permute-start(bf16[24,8,896]{2,1,0:T(8,128)(2,1)S(1)} %get-tuple-element.2), channel_id=1, source_target_pairs={{1,0},{2,129},{3,2},{4,131},{5,4},{6,133},{7,6},{8,135},{9,8},{10,... | collective-permute-start | bytes 1032200 | tf_op jit(solution)/shard_map/ppermute | solution.py:42
  6.3 14.7 %collective-permute-start = (bf16[24,8,896]{2,1,0:T(8,128)(2,1)S(1)}, bf16[24,8,896]{2,1,0:T(8,128)(2,1)S(1)}, u32[]{:S(2)}, u32[]{:S(2)}) collective-permute-start(bf16[24,8,896]{2,1,0:T(8,128)(2,1)S(1)} %get-tuple-element.3), channel_id=1, source_target_pairs={{0,1},{1,130},{2,3},{3,132},{4,5},{5,134},{6,7},{7,136},{8,9},{9,1... | collective-permute-start | bytes 1032200 | tf_op jit(solution)/shard_map/ppermute | solution.py:41
  17.0 4.1 %copy-start = (bf16[24,8,896]{2,1,0:T(8,128)(2,1)}, bf16[24,8,896]{2,1,0:T(8,128)(2,1)S(1)}, u32[]{:S(2)}) copy-start(bf16[24,8,896]{2,1,0:T(8,128)(2,1)S(1)} %collective-permute-done.1.hi_ref) | copy-start | bytes 1032196
  21.0 0.7 %copy-start.1 = (bf16[24,8,896]{2,1,0:T(8,128)(2,1)}, bf16[24,8,896]{2,1,0:T(8,128)(2,1)S(1)}, u32[]{:S(2)}) copy-start(bf16[24,8,896]{2,1,0:T(8,128)(2,1)S(1)} %collective-permute-done.lo_ref) | copy-start | bytes 1032196

commit v9 on v6

--- a/solution.py
+++ b/solution.py
@@ -61,12 +61,15 @@
     return mexican(offsets[None], spread).astype(jnp.bfloat16)
 
 
-def wavelet_kernel(strip_ref, f_ref, lo_ref, own_ref, hi_ref, b_ref, peak_ref, energy_ref,
-                   p_scr, g_scr, s_scr, best_scr, total_scr):
+def wavelet_kernel(strip_ref, f_ref, lo_ref, own_ref, hi_ref, b_ref, late_hbm, peak_ref, energy_ref,
+                   late_buf, sem, p_scr, g_scr, s_scr, best_scr, total_scr):
     count, rows, scans = g_scr.shape
     frames, strip, _ = own_ref.shape
     nb = scans // TILE
     used = 2 * HALO + frames
+    early = b_ref.shape[0]
+    late_copy = pltpu.make_async_copy(late_hbm, late_buf, sem.at[0])
+    late_copy.start()
 
     p_scr[used:, :] = jnp.zeros((p_scr.shape[0] - used, p_scr.shape[1]), p_scr.dtype)
     for m in range(strip):
@@ -83,9 +86,12 @@
 
     for c in range(count):
         table = s_scr.at[c % 2]
+        if c == early:
+            late_copy.wait()
+        blocks = b_ref.at[c] if c < early else late_buf.at[c - early]
         for i in range(nb):
             for j in range(nb):
-                table[i * TILE:(i + 1) * TILE, j * TILE:(j + 1) * TILE] = b_ref[c, i - j + nb - 1]
+                table[i * TILE:(i + 1) * TILE, j * TILE:(j + 1) * TILE] = blocks[i - j + nb - 1]
         lhs = g_scr[c].astype(jnp.bfloat16)
         answer = jnp.dot(lhs, table[...], preferred_element_type=jnp.float32).astype(jnp.bfloat16)
         answer = answer.astype(jnp.float32)
@@ -117,13 +123,16 @@
             pl.BlockSpec((HALO, strip, scans), whole3),
             pl.BlockSpec((frames, strip, scans), lambda c, i: (0, i[0], 0)),
             pl.BlockSpec((HALO, strip, scans), whole3),
-            pl.BlockSpec((count, nblk, TILE, TILE), lambda c, i: (0, 0, 0, 0)),
+            pl.BlockSpec((count // 2, nblk, TILE, TILE), lambda c, i: (0, 0, 0, 0)),
+            pl.BlockSpec(memory_space=pl.ANY),
         ],
         out_specs=[
             pl.BlockSpec((frames, strip, scans), whole3),
             pl.BlockSpec((frames, strip, scans), whole3),
         ],
         scratch_shapes=[
+            pltpu.VMEM((count - count // 2, nblk, TILE, TILE), blocks.dtype),
+            pltpu.SemaphoreType.DMA((1,)),
             pltpu.VMEM((depth, strip * scans), jnp.float32),
             pltpu.VMEM((count, rows, scans), jnp.float32),
             pltpu.VMEM((2, scans, scans), jnp.bfloat16),
@@ -142,7 +151,7 @@
             dimension_semantics=("arbitrary",), vmem_limit_bytes=56 * 1024 * 1024
         ),
         interpret=interpret,
-    )(first, ftab, low, slab, high, blocks)
+    )(first, ftab, low, slab, high, blocks[:count // 2], blocks[count // 2:])
 
 
 def compute(slab, block_index, low, high, widths, interpret=False):

time: 37.2 us -> 39.3 us (1.056)
  local copies, waits for them, and re-layouts: 2.44 us -> 6.82 us
  waiting for transfers between devices: 4.06 us -> 0.01 us
  starting transfers between devices: 6.13 us -> 9.16 us
  other arithmetic: 8.38 us -> 7.12 us
    slice x0 -> x1, local copies, waits for them, and re-layouts: none -> 4.28 us  [wavelet_core(): blocks[count // 2:]]
    ppermute x1, waiting for transfers between devices: 4.05 us -> 0.01 us  [halos(): low = lax.ppermute(send_fwd, ('scale', 'rt'), forward)]
    ppermute x1, starting transfers between devices: 4.21 us -> 5.76 us  [halos(): high = lax.ppermute(send_bwd, ('scale', 'rt'), backward)]
    ppermute x1, starting transfers between devices: 1.92 us -> 3.4 us  [halos(): low = lax.ppermute(send_fwd, ('scale', 'rt'), forward)]
    convert_element_type x1, other arithmetic: 6.05 us -> 4.77 us  [scan_blocks(): return mexican(offsets[None], spread).astype(jnp.bfloat16)]
  transfers between devices with their start and end apart: 2 -> 2, of which waited for: 1 -> 0; matrix products, arithmetic and copies ran while one was open for 23% -> 30% of each run, Pallas kernels for 0% -> 0%
where the time goes in v9:
time: 39.3 us; the launch traced here: 39.1 us
  Pallas kernels  15.3 us (39%)
  starting transfers between devices  9.16 us (23%)
  other arithmetic  7.12 us (18%)
  local copies, waits for them, and re-layouts  6.82 us (17%)
  between operations  0.76 us (2%)
    pallas_call x1, Pallas kernels, wavelet_core(): pl.pallas_call(wavelet_kernel, grid_spec=grid_spec, out_shape=[jax.ShapeD...  15.3 us
    ppermute x1, starting transfers between devices, halos(): high = lax.ppermute(send_bwd, ('scale', 'rt'), backward)  5.76 us
    convert_element_type x1, other arithmetic, scan_blocks(): return mexican(offsets[None], spread).astype(jnp.bfloat16)  4.77 us
    slice x1, local copies, waits for them, and re-layouts, wavelet_core(): blocks[count // 2:]  4.28 us
    ppermute x1, starting transfers between devices, halos(): low = lax.ppermute(send_fwd, ('scale', 'rt'), forward)  3.4 us
    convert_element_type x1, local copies, waits for them, and re-layouts, piece(): return part.astype(jnp.bfloat16)  1.39 us
    unnamed x4, local copies, waits for them, and re-layouts  0.84 us
    convert_element_type x1, other arithmetic, frame_tables(): return values.astype(jnp.bfloat16).reshape(-1, depth)  0.82 us
  transfers between devices with their start and end apart: 2, of which 0 were waited for; matrix products, arithmetic and copies ran while one was open for 30% of the time, Pallas kernels for 0%

profile of v9, /device:TPU:136, one launch (start us, length us, event | category | flops | bytes accessed | tf_op | source)
XLA Modules:
  0.0 39.1 jit_solution(16794169037374667594)
XLA Ops:
  0.7 1.4 %dynamic-slice_convert_fusion = (bf16[24,8,896]{2,1,0:T(8,128)(2,1)S(1)}, bf16[24,8,896]{2,1,0:T(8,128)(2,1)S(1)}) fusion(f32[24,128,896]{2,1,0:T(8,128)} %own_ref.1, s32[]{:T(128)S(6)} %select_n.36, s32[]{:T(128)S(6)} %select_n.34), kind=kLoop, calls=%fused_computation.5 | loop fusion | bytes 1376264 | tf_op jit(solution)/shard_map/convert_element_type | solution.py:36
  2.1 3.4 %collective-permute-start = (bf16[24,8,896]{2,1,0:T(8,128)(2,1)S(1)}, bf16[24,8,896]{2,1,0:T(8,128)(2,1)S(1)}, u32[]{:S(2)}, u32[]{:S(2)}) collective-permute-start(bf16[24,8,896]{2,1,0:T(8,128)(2,1)S(1)} %get-tuple-element.3), channel_id=1, source_target_pairs={{0,1},{1,130},{2,3},{3,132},{4,5},{5,134},{6,7},{7,136},{8,9},{9,1... | collective-permute-start | bytes 1032200 | tf_op jit(solution)/shard_map/ppermute | solution.py:40
  5.5 5.8 %collective-permute-start.1 = (bf16[24,8,896]{2,1,0:T(8,128)(2,1)S(1)}, bf16[24,8,896]{2,1,0:T(8,128)(2,1)S(1)}, u32[]{:S(2)}, u32[]{:S(2)}) collective-permute-start(bf16[24,8,896]{2,1,0:T(8,128)(2,1)S(1)} %get-tuple-element.2), channel_id=1, source_target_pairs={{1,0},{2,129},{3,2},{4,131},{5,4},{6,133},{7,6},{8,135},{9,8},{10,... | collective-permute-start | bytes 1032200 | tf_op jit(solution)/shard_map/ppermute | solution.py:41
  11.3 0.7 %broadcast_multiply_fusion = (f32[16]{0:T(128)S(1)}, f32[16]{0:T(128)S(1)}, f32[16]{0:T(128)S(1)}) fusion(s32[16]{0:T(128)} %param.3), kind=kLoop, calls=%fused_computation.21 | loop fusion | flops 32 | bytes 256 | tf_op jit(solution)/shard_map/mul | solution.py:60
  12.0 0.7 %convert_element_type.16 = f32[16]{0:T(128)S(1)} convert(s32[16]{0:T(128)} %param.3) | non-fusion elementwise | flops 16 | bytes 128 | tf_op jit(solution)/shard_map/convert_element_type | solution.py:160
  12.6 0.1 div.60
  12.7 0.1 div.61
  12.8 0.1 div.56
  12.9 0.1 div.57
  13.0 0.1 broadcast_add_fusion
  13.1 4.8 %fusion.3 = bf16[16,13,128,128]{3,2,1,0:T(8,128)(2,1)S(1)} fusion(f32[16]{0:T(128)S(1)} %get-tuple-element.7, f32[16]{0:T(128)S(1)} %get-tuple-element.6, f32[13,128,128]{2,1,0:T(8,128)S(1)} %broadcast_add_fusion), kind=kLoop, calls=%fused_computation.4 | loop fusion | flops 27262976 | bytes 7667840 | tf_op jit(solution)/shard_map/convert_element_type | solution.py:61
  17.9 0.8 %fusion.8.f_ref = bf16[384,128]{1,0:T(8,128)(2,1)} fusion(f32[384]{0:T(512)S(1)} %div.61, f32[384]{0:T(512)S(1)} %div.57, f32[24,128]{1,0:T(8,128)S(1)} %iota_subtract_fusion.1, pred[24,128]{1,0:T(8,128)(4,1)S(1)} %fusion.9), kind=kLoop, calls=%fused_computation.14 | loop fusion | flops 442368 | bytes 116736 | tf_op jit(solution)/shard_map/convert_element_type | solution.py:52
  18.7 4.3 %fusion.11 = (bf16[8,13,128,128]{3,2,1,0:T(8,128)(2,1)}, bf16[8,13,128,128]{3,2,1,0:T(8,128)(2,1)}) fusion(bf16[16,13,128,128]{3,2,1,0:T(8,128)(2,1)S(1)} %fusion.3), kind=kLoop, calls=%fused_computation.25 | loop fusion | bytes 13631488 | tf_op jit(solution)/shard_map/slice | solution.py:154
  23.0 0.0 collective-permute-done.lo_ref
  23.0 0.0 copy-start
  23.0 0.0 collective-permute-done.1.hi_ref
  23.0 0.0 copy-start.1
  23.0 0.7 %copy-done = bf16[24,8,896]{2,1,0:T(8,128)(2,1)} copy-done((bf16[24,8,896]{2,1,0:T(8,128)(2,1)}, bf16[24,8,896]{2,1,0:T(8,128)(2,1)S(1)}, u32[]{:S(2)}) %copy-start) | copy-done | bytes 344088
  23.8 0.1 copy-done.1
  23.9 15.3 %shard_map.41 = (bf16[24,8,896]{2,1,0:T(8,128)(2,1)}, f32[24,8,896]{2,1,0:T(8,128)}) custom-call(s32[1]{0:T(128)} %bitcast.strip_ref, bf16[384,128]{1,0:T(8,128)(2,1)} %fusion.8.f_ref, bf16[24,8,896]{2,1,0:T(8,128)(2,1)} %copy-done, f32[24,128,896]{2,1,0:T(8,128)} %own_ref.1, bf16[24,8,896]{2,1,0:T(8,128)(2,1)} %copy-done.1, ...), custom_call_target="tpu_custom_call" | custom-call | tf_op jit(solution)/shard_map/pallas_call | solution.py:143
  (6 shorter events, 0.1 us)
Async XLA Ops:
  2.1 21.0 %collective-permute-start = (bf16[24,8,896]{2,1,0:T(8,128)(2,1)S(1)}, bf16[24,8,896]{2,1,0:T(8,128)(2,1)S(1)}, u32[]{:S(2)}, u32[]{:S(2)}) collective-permute-start(bf16[24,8,896]{2,1,0:T(8,128)(2,1)S(1)} %get-tuple-element.3), channel_id=1, source_target_pairs={{0,1},{1,130},{2,3},{3,132},{4,5},{5,134},{6,7},{7,136},{8,9},{9,1... | collective-permute-start | bytes 1032200 | tf_op jit(solution)/shard_map/ppermute | solution.py:40
  5.5 17.6 %collective-permute-start.1 = (bf16[24,8,896]{2,1,0:T(8,128)(2,1)S(1)}, bf16[24,8,896]{2,1,0:T(8,128)(2,1)S(1)}, u32[]{:S(2)}, u32[]{:S(2)}) collective-permute-start(bf16[24,8,896]{2,1,0:T(8,128)(2,1)S(1)} %get-tuple-element.2), channel_id=1, source_target_pairs={{1,0},{2,129},{3,2},{4,131},{5,4},{6,133},{7,6},{8,135},{9,8},{10,... | collective-permute-start | bytes 1032200 | tf_op jit(solution)/shard_map/ppermute | solution.py:41
  23.0 0.7 %copy-start = (bf16[24,8,896]{2,1,0:T(8,128)(2,1)}, bf16[24,8,896]{2,1,0:T(8,128)(2,1)S(1)}, u32[]{:S(2)}) copy-start(bf16[24,8,896]{2,1,0:T(8,128)(2,1)S(1)} %collective-permute-done.lo_ref) | copy-start | bytes 1032196
  23.0 0.8 %copy-start.1 = (bf16[24,8,896]{2,1,0:T(8,128)(2,1)}, bf16[24,8,896]{2,1,0:T(8,128)(2,1)S(1)}, u32[]{:S(2)}) copy-start(bf16[24,8,896]{2,1,0:T(8,128)(2,1)S(1)} %collective-permute-done.1.hi_ref) | copy-start | bytes 1032196

commit v10 on v6

--- a/solution.py
+++ b/solution.py
@@ -8,6 +8,7 @@
 SCAN_RATIO = 16
 HALO = 24
 TILE = 128
+SLOT = 32
 
 
 def mexican(offsets, spread):
@@ -42,12 +43,16 @@
     return low, high
 
 
-def frame_tables(frames, scale_widths, depth):
+def frame_tables(frames, scale_widths, depth, slot):
     out_pos = jnp.arange(frames, dtype=jnp.float32)
-    in_pos = jnp.arange(depth, dtype=jnp.float32) - HALO
+    k = jnp.arange(depth)
+    piece, rest = k // slot, k % slot
+    size = jnp.where(piece == 1, frames, HALO)
+    valid = (piece < 3) & (rest < size)
+    in_pos = jnp.where(piece == 0, rest - HALO, jnp.where(piece == 1, rest, frames + rest)).astype(jnp.float32)
     offsets = (in_pos[None, :] - out_pos[:, None])[None]
     spread = scale_widths[:, None, None]
-    inside = (jnp.abs(offsets) <= HALO) & (in_pos < frames + HALO)[None, None, :]
+    inside = (jnp.abs(offsets) <= HALO) & valid[None, None, :]
     values = jnp.where(inside, mexican(offsets, spread), 0.0)
     return values.astype(jnp.bfloat16).reshape(-1, depth)
 
@@ -66,17 +71,17 @@
     count, rows, scans = g_scr.shape
     frames, strip, _ = own_ref.shape
     nb = scans // TILE
-    used = 2 * HALO + frames
+    slot = SLOT
 
-    p_scr[used:, :] = jnp.zeros((p_scr.shape[0] - used, p_scr.shape[1]), p_scr.dtype)
+    p_scr[...] = jnp.zeros(p_scr.shape, p_scr.dtype)
     for m in range(strip):
         cols = slice(m * scans, (m + 1) * scans)
-        p_scr[0:HALO, cols] = lo_ref[:, m, :].astype(jnp.float32)
-        p_scr[HALO:HALO + frames, cols] = own_ref[:, m, :]
-        p_scr[HALO + frames:used, cols] = hi_ref[:, m, :].astype(jnp.float32)
+        p_scr[0:HALO, cols] = lo_ref[:, m, :]
+        p_scr[slot:slot + frames, cols] = own_ref[:, m, :].astype(p_scr.dtype)
+        p_scr[2 * slot:2 * slot + HALO, cols] = hi_ref[:, m, :]
     fall = f_ref[...]
     for m in range(strip):
-        part = p_scr[:, m * scans:(m + 1) * scans].astype(jnp.bfloat16)
+        part = p_scr[:, m * scans:(m + 1) * scans]
         gm = jnp.dot(fall, part, preferred_element_type=jnp.float32)
         for cc in range(count):
             g_scr[cc, m * frames:(m + 1) * frames, :] = gm[cc * frames:(cc + 1) * frames, :]
@@ -124,7 +129,7 @@
             pl.BlockSpec((frames, strip, scans), whole3),
         ],
         scratch_shapes=[
-            pltpu.VMEM((depth, strip * scans), jnp.float32),
+            pltpu.VMEM((depth, strip * scans), jnp.bfloat16),
             pltpu.VMEM((count, rows, scans), jnp.float32),
             pltpu.VMEM((2, scans, scans), jnp.bfloat16),
             pltpu.VMEM((rows, scans), jnp.float32),
@@ -147,9 +152,10 @@
 
 def compute(slab, block_index, low, high, widths, interpret=False):
     frames, strip, scans = low.shape
-    depth = -(-(frames + 2 * HALO) // TILE) * TILE
+    assert max(HALO, frames) <= SLOT
+    depth = -(-(3 * SLOT) // TILE) * TILE
     scale_widths = widths.astype(jnp.float32)
-    ftab = frame_tables(frames, scale_widths, depth)
+    ftab = frame_tables(frames, scale_widths, depth, SLOT)
     blocks = scan_blocks(scans, scale_widths)
     first = jnp.reshape(block_index, (1,)).astype(jnp.int32)
     return wavelet_core(first, ftab, low, slab, high, blocks, interpret)

time: 37.2 us -> 38.1 us (1.024)
  Pallas kernels: 15.3 us -> 16.2 us
    pallas_call x1, Pallas kernels: 15.3 us -> 16.2 us  [wavelet_core(): pl.pallas_call(wavelet_kernel, grid_spec=grid_spec, out_shape=[jax.ShapeD...]
where the time goes in v10:
time: 38.1 us; the launch traced here: 37.9 us
  Pallas kernels  16.2 us (43%)
  other arithmetic  8.38 us (22%)
  starting transfers between devices  6.13 us (16%)
  waiting for transfers between devices  4.06 us (11%)
  local copies, waits for them, and re-layouts  2.44 us (6%)
  between operations  0.74 us (2%)
    pallas_call x1, Pallas kernels, wavelet_core(): pl.pallas_call(wavelet_kernel, grid_spec=grid_spec, out_shape=[jax.ShapeD...  16.2 us
    convert_element_type x1, other arithmetic, scan_blocks(): return mexican(offsets[None], spread).astype(jnp.bfloat16)  6.05 us
    ppermute x1, starting transfers between devices, halos(): high = lax.ppermute(send_bwd, ('scale', 'rt'), backward)  4.21 us
    ppermute x1, waiting for transfers between devices, halos(): low = lax.ppermute(send_fwd, ('scale', 'rt'), forward)  4.05 us
    ppermute x1, starting transfers between devices, halos(): low = lax.ppermute(send_fwd, ('scale', 'rt'), forward)  1.92 us
    convert_element_type x1, local copies, waits for them, and re-layouts, piece(): return part.astype(jnp.bfloat16)  1.39 us
    convert_element_type x1, other arithmetic, frame_tables(): return values.astype(jnp.bfloat16).reshape(-1, depth)  0.81 us
  transfers between devices with their start and end apart: 2, of which 1 were waited for; matrix products, arithmetic and copies ran while one was open for 23% of the time, Pallas kernels for 0%

profile of v10, /device:TPU:136, one launch (start us, length us, event | category | flops | bytes accessed | tf_op | source)
XLA Modules:
  0.0 37.9 jit_solution(832953763436674572)
XLA Ops:
  0.7 1.4 %dynamic-slice_convert_fusion = (bf16[24,8,896]{2,1,0:T(8,128)(2,1)S(1)}, bf16[24,8,896]{2,1,0:T(8,128)(2,1)S(1)}) fusion(f32[24,128,896]{2,1,0:T(8,128)} %own_ref.1, s32[]{:T(128)S(6)} %select_n.94, s32[]{:T(128)S(6)} %select_n.92), kind=kLoop, calls=%fused_computation.5 | loop fusion | bytes 1376264 | tf_op jit(solution)/shard_map/convert_element_type | solution.py:37
  2.1 4.2 %collective-permute-start.1 = (bf16[24,8,896]{2,1,0:T(8,128)(2,1)S(1)}, bf16[24,8,896]{2,1,0:T(8,128)(2,1)S(1)}, u32[]{:S(2)}, u32[]{:S(2)}) collective-permute-start(bf16[24,8,896]{2,1,0:T(8,128)(2,1)S(1)} %get-tuple-element.2), channel_id=1, source_target_pairs={{1,0},{2,129},{3,2},{4,131},{5,4},{6,133},{7,6},{8,135},{9,8},{10,... | collective-permute-start | bytes 1032200 | tf_op jit(solution)/shard_map/ppermute | solution.py:42
  6.3 1.9 %collective-permute-start = (bf16[24,8,896]{2,1,0:T(8,128)(2,1)S(1)}, bf16[24,8,896]{2,1,0:T(8,128)(2,1)S(1)}, u32[]{:S(2)}, u32[]{:S(2)}) collective-permute-start(bf16[24,8,896]{2,1,0:T(8,128)(2,1)S(1)} %get-tuple-element.3), channel_id=1, source_target_pairs={{0,1},{1,130},{2,3},{3,132},{4,5},{5,134},{6,7},{7,136},{8,9},{9,1... | collective-permute-start | bytes 1032200 | tf_op jit(solution)/shard_map/ppermute | solution.py:41
  8.2 0.7 %convert_element_type.26 = f32[16]{0:T(128)S(1)} convert(s32[16]{0:T(128)} %param.3) | non-fusion elementwise | flops 16 | bytes 128 | tf_op jit(solution)/shard_map/convert_element_type | solution.py:157
  8.9 0.7 %broadcast_multiply_fusion = (f32[16]{0:T(128)S(1)}, f32[16]{0:T(128)S(1)}, f32[16]{0:T(128)S(1)}) fusion(s32[16]{0:T(128)} %param.3), kind=kLoop, calls=%fused_computation.29 | loop fusion | flops 32 | bytes 256 | tf_op jit(solution)/shard_map/mul | solution.py:65
  9.6 0.1 div.68
  9.7 0.1 div.69
  9.8 0.1 div.72
  9.8 0.1 div.73
  9.9 0.1 broadcast_add_fusion
  10.1 6.0 %fusion.3.b_ref = bf16[16,13,128,128]{3,2,1,0:T(8,128)(2,1)} fusion(f32[16]{0:T(128)S(1)} %get-tuple-element.5, f32[16]{0:T(128)S(1)} %get-tuple-element.4, f32[13,128,128]{2,1,0:T(8,128)S(1)} %broadcast_add_fusion), kind=kLoop, calls=%fused_computation.4 | loop fusion | flops 27262976 | bytes 7667840 | tf_op jit(solution)/shard_map/convert_element_type | solution.py:66
  16.1 0.8 %fusion.8.f_ref = bf16[384,128]{1,0:T(8,128)(2,1)} fusion(f32[384]{0:T(512)S(1)} %div.73, f32[384]{0:T(512)S(1)} %div.69, f32[24,128]{1,0:T(8,128)S(1)} %iota_subtract_fusion.1, pred[24,128]{1,0:T(8,128)(4,1)S(1)} %fusion.9), kind=kLoop, calls=%fused_computation.14 | loop fusion | flops 442368 | bytes 116736 | tf_op jit(solution)/shard_map/convert_element_type | solution.py:57
  17.0 0.0 collective-permute-done.1.hi_ref
  17.0 0.0 copy-start
  17.0 4.1 %collective-permute-done.lo_ref = bf16[24,8,896]{2,1,0:T(8,128)(2,1)S(1)} collective-permute-done((bf16[24,8,896]{2,1,0:T(8,128)(2,1)S(1)}, bf16[24,8,896]{2,1,0:T(8,128)(2,1)S(1)}, u32[]{:S(2)}, u32[]{:S(2)}) %collective-permute-start) | collective-permute-done | bytes 344096 | tf_op jit(solution)/shard_map/ppermute | solution.py:41
  21.0 0.0 copy-start.1
  21.0 0.0 copy-done
  21.0 0.7 %copy-done.1 = bf16[24,8,896]{2,1,0:T(8,128)(2,1)} copy-done((bf16[24,8,896]{2,1,0:T(8,128)(2,1)}, bf16[24,8,896]{2,1,0:T(8,128)(2,1)S(1)}, u32[]{:S(2)}) %copy-start.1) | copy-done | bytes 344088
  21.7 16.2 %shard_map.41 = (bf16[24,8,896]{2,1,0:T(8,128)(2,1)}, f32[24,8,896]{2,1,0:T(8,128)}) custom-call(s32[1]{0:T(128)} %bitcast.strip_ref, bf16[384,128]{1,0:T(8,128)(2,1)} %fusion.8.f_ref, bf16[24,8,896]{2,1,0:T(8,128)(2,1)} %copy-done.1, f32[24,128,896]{2,1,0:T(8,128)} %own_ref.1, bf16[24,8,896]{2,1,0:T(8,128)(2,1)} %copy-done, ...), custom_call_target="tpu_custom_call" | custom-call | tf_op jit(solution)/shard_map/pallas_call | solution.py:139
  (6 shorter events, 0.1 us)
Async XLA Ops:
  2.1 14.9 %collective-permute-start.1 = (bf16[24,8,896]{2,1,0:T(8,128)(2,1)S(1)}, bf16[24,8,896]{2,1,0:T(8,128)(2,1)S(1)}, u32[]{:S(2)}, u32[]{:S(2)}) collective-permute-start(bf16[24,8,896]{2,1,0:T(8,128)(2,1)S(1)} %get-tuple-element.2), channel_id=1, source_target_pairs={{1,0},{2,129},{3,2},{4,131},{5,4},{6,133},{7,6},{8,135},{9,8},{10,... | collective-permute-start | bytes 1032200 | tf_op jit(solution)/shard_map/ppermute | solution.py:42
  6.3 14.7 %collective-permute-start = (bf16[24,8,896]{2,1,0:T(8,128)(2,1)S(1)}, bf16[24,8,896]{2,1,0:T(8,128)(2,1)S(1)}, u32[]{:S(2)}, u32[]{:S(2)}) collective-permute-start(bf16[24,8,896]{2,1,0:T(8,128)(2,1)S(1)} %get-tuple-element.3), channel_id=1, source_target_pairs={{0,1},{1,130},{2,3},{3,132},{4,5},{5,134},{6,7},{7,136},{8,9},{9,1... | collective-permute-start | bytes 1032200 | tf_op jit(solution)/shard_map/ppermute | solution.py:41
  17.0 4.1 %copy-start = (bf16[24,8,896]{2,1,0:T(8,128)(2,1)}, bf16[24,8,896]{2,1,0:T(8,128)(2,1)S(1)}, u32[]{:S(2)}) copy-start(bf16[24,8,896]{2,1,0:T(8,128)(2,1)S(1)} %collective-permute-done.1.hi_ref) | copy-start | bytes 1032196
  21.0 0.7 %copy-start.1 = (bf16[24,8,896]{2,1,0:T(8,128)(2,1)}, bf16[24,8,896]{2,1,0:T(8,128)(2,1)S(1)}, u32[]{:S(2)}) copy-start(bf16[24,8,896]{2,1,0:T(8,128)(2,1)S(1)} %collective-permute-done.lo_ref) | copy-start | bytes 1032196

commit v11 on v6

--- a/solution.py
+++ b/solution.py
@@ -54,7 +54,7 @@
 
 def scan_blocks(scans, scale_widths):
     nb = scans // TILE
-    shift = (jnp.arange(2 * nb - 1, dtype=jnp.float32) - (nb - 1)) * TILE
+    shift = jnp.arange(nb, dtype=jnp.float32) * TILE
     pos = jnp.arange(TILE, dtype=jnp.float32)
     offsets = shift[:, None, None] + (pos[:, None] - pos[None, :])[None]
     spread = SCAN_RATIO * scale_widths[:, None, None, None]
@@ -83,9 +83,11 @@
 
     for c in range(count):
         table = s_scr.at[c % 2]
+        flipped = {d: b_ref[c, d].T for d in range(1, nb)}
         for i in range(nb):
             for j in range(nb):
-                table[i * TILE:(i + 1) * TILE, j * TILE:(j + 1) * TILE] = b_ref[c, i - j + nb - 1]
+                block = b_ref[c, i - j] if i >= j else flipped[j - i]
+                table[i * TILE:(i + 1) * TILE, j * TILE:(j + 1) * TILE] = block
         lhs = g_scr[c].astype(jnp.bfloat16)
         answer = jnp.dot(lhs, table[...], preferred_element_type=jnp.float32).astype(jnp.bfloat16)
         answer = answer.astype(jnp.float32)

time: 37.2 us -> 36.8 us (0.989)
  other arithmetic: 8.38 us -> 6.1 us
  waiting for transfers between devices: 4.06 us -> 6.34 us
  Pallas kernels: 15.3 us -> 14.9 us
    ppermute x1, waiting for transfers between devices: 4.05 us -> 6.33 us  [halos(): low = lax.ppermute(send_fwd, ('scale', 'rt'), forward)]
    convert_element_type x1, other arithmetic: 6.05 us -> 3.79 us  [scan_blocks(): return mexican(offsets[None], spread).astype(jnp.bfloat16)]
    pallas_call x1, Pallas kernels: 15.3 us -> 14.9 us  [wavelet_core(): pl.pallas_call(wavelet_kernel, grid_spec=grid_spec, out_shape=[jax.ShapeD...]
  transfers between devices with their start and end apart: 2 -> 2, of which waited for: 1 -> 1; matrix products, arithmetic and copies ran while one was open for 23% -> 18% of each run, Pallas kernels for 0% -> 0%
where the time goes in v11:
time: 36.8 us; the launch traced here: 36.6 us
  Pallas kernels  14.9 us (40%)
  waiting for transfers between devices  6.34 us (17%)
  starting transfers between devices  6.13 us (17%)
  other arithmetic  6.1 us (17%)
  local copies, waits for them, and re-layouts  2.45 us (7%)
  between operations  0.73 us (2%)
    pallas_call x1, Pallas kernels, wavelet_core(): pl.pallas_call(wavelet_kernel, grid_spec=grid_spec, out_shape=[jax.ShapeD...  14.9 us
    ppermute x1, waiting for transfers between devices, halos(): low = lax.ppermute(send_fwd, ('scale', 'rt'), forward)  6.33 us
    ppermute x1, starting transfers between devices, halos(): high = lax.ppermute(send_bwd, ('scale', 'rt'), backward)  4.21 us
    convert_element_type x1, other arithmetic, scan_blocks(): return mexican(offsets[None], spread).astype(jnp.bfloat16)  3.79 us
    ppermute x1, starting transfers between devices, halos(): low = lax.ppermute(send_fwd, ('scale', 'rt'), forward)  1.92 us
    convert_element_type x1, local copies, waits for them, and re-layouts, piece(): return part.astype(jnp.bfloat16)  1.39 us
    convert_element_type x1, other arithmetic, frame_tables(): return values.astype(jnp.bfloat16).reshape(-1, depth)  0.81 us
    unnamed x4, local copies, waits for them, and re-layouts  0.74 us
  transfers between devices with their start and end apart: 2, of which 1 were waited for; matrix products, arithmetic and copies ran while one was open for 18% of the time, Pallas kernels for 0%

profile of v11, /device:TPU:136, one launch (start us, length us, event | category | flops | bytes accessed | tf_op | source)
XLA Modules:
  0.0 36.6 jit_solution(16179849199892639610)
XLA Ops:
  0.7 1.4 %dynamic-slice_convert_fusion = (bf16[24,8,896]{2,1,0:T(8,128)(2,1)S(1)}, bf16[24,8,896]{2,1,0:T(8,128)(2,1)S(1)}) fusion(f32[24,128,896]{2,1,0:T(8,128)} %own_ref.1, s32[]{:T(128)S(6)} %select_n.36, s32[]{:T(128)S(6)} %select_n.34), kind=kLoop, calls=%fused_computation.5 | loop fusion | bytes 1376264 | tf_op jit(solution)/shard_map/convert_element_type | solution.py:36
  2.1 4.2 %collective-permute-start.1 = (bf16[24,8,896]{2,1,0:T(8,128)(2,1)S(1)}, bf16[24,8,896]{2,1,0:T(8,128)(2,1)S(1)}, u32[]{:S(2)}, u32[]{:S(2)}) collective-permute-start(bf16[24,8,896]{2,1,0:T(8,128)(2,1)S(1)} %get-tuple-element.2), channel_id=1, source_target_pairs={{1,0},{2,129},{3,2},{4,131},{5,4},{6,133},{7,6},{8,135},{9,8},{10,... | collective-permute-start | bytes 1032200 | tf_op jit(solution)/shard_map/ppermute | solution.py:41
  6.3 1.9 %collective-permute-start = (bf16[24,8,896]{2,1,0:T(8,128)(2,1)S(1)}, bf16[24,8,896]{2,1,0:T(8,128)(2,1)S(1)}, u32[]{:S(2)}, u32[]{:S(2)}) collective-permute-start(bf16[24,8,896]{2,1,0:T(8,128)(2,1)S(1)} %get-tuple-element.3), channel_id=1, source_target_pairs={{0,1},{1,130},{2,3},{3,132},{4,5},{5,134},{6,7},{7,136},{8,9},{9,1... | collective-permute-start | bytes 1032200 | tf_op jit(solution)/shard_map/ppermute | solution.py:40
  8.2 0.7 %convert_element_type.16 = f32[16]{0:T(128)S(1)} convert(s32[16]{0:T(128)} %param.3) | non-fusion elementwise | flops 16 | bytes 128 | tf_op jit(solution)/shard_map/convert_element_type | solution.py:153
  8.9 0.7 %broadcast_multiply_fusion = (f32[16]{0:T(128)S(1)}, f32[16]{0:T(128)S(1)}, f32[16]{0:T(128)S(1)}) fusion(s32[16]{0:T(128)} %param.3), kind=kLoop, calls=%fused_computation.21 | loop fusion | flops 32 | bytes 256 | tf_op jit(solution)/shard_map/mul | solution.py:60
  9.6 0.1 div.56
  9.7 0.1 div.57
  9.8 0.1 div.60
  9.8 0.1 div.61
  9.9 0.1 broadcast_add_fusion
  10.0 3.8 %fusion.3.b_ref = bf16[16,7,128,128]{3,2,1,0:T(8,128)(2,1)} fusion(f32[16]{0:T(128)S(1)} %get-tuple-element.5, f32[16]{0:T(128)S(1)} %get-tuple-element.4, f32[7,128,128]{2,1,0:T(8,128)S(1)} %broadcast_add_fusion), kind=kLoop, calls=%fused_computation.4 | loop fusion | flops 14680064 | bytes 4128896 | tf_op jit(solution)/shard_map/convert_element_type | solution.py:61
  13.9 0.8 %fusion.8.f_ref = bf16[384,128]{1,0:T(8,128)(2,1)} fusion(f32[384]{0:T(512)S(1)} %div.61, f32[384]{0:T(512)S(1)} %div.57, f32[24,128]{1,0:T(8,128)S(1)} %iota_subtract_fusion.1, pred[24,128]{1,0:T(8,128)(4,1)S(1)} %fusion.9), kind=kLoop, calls=%fused_computation.14 | loop fusion | flops 442368 | bytes 116736 | tf_op jit(solution)/shard_map/convert_element_type | solution.py:52
  14.7 0.0 collective-permute-done.1.hi_ref
  14.7 0.0 copy-start
  14.7 6.3 %collective-permute-done.lo_ref = bf16[24,8,896]{2,1,0:T(8,128)(2,1)S(1)} collective-permute-done((bf16[24,8,896]{2,1,0:T(8,128)(2,1)S(1)}, bf16[24,8,896]{2,1,0:T(8,128)(2,1)S(1)}, u32[]{:S(2)}, u32[]{:S(2)}) %collective-permute-start) | collective-permute-done | bytes 344096 | tf_op jit(solution)/shard_map/ppermute | solution.py:40
  21.0 0.0 copy-start.1
  21.0 0.0 copy-done
  21.0 0.7 %copy-done.1 = bf16[24,8,896]{2,1,0:T(8,128)(2,1)} copy-done((bf16[24,8,896]{2,1,0:T(8,128)(2,1)}, bf16[24,8,896]{2,1,0:T(8,128)(2,1)S(1)}, u32[]{:S(2)}) %copy-start.1) | copy-done | bytes 344088
  21.8 14.9 %shard_map.41 = (bf16[24,8,896]{2,1,0:T(8,128)(2,1)}, f32[24,8,896]{2,1,0:T(8,128)}) custom-call(s32[1]{0:T(128)} %bitcast.strip_ref, bf16[384,128]{1,0:T(8,128)(2,1)} %fusion.8.f_ref, bf16[24,8,896]{2,1,0:T(8,128)(2,1)} %copy-done.1, f32[24,128,896]{2,1,0:T(8,128)} %own_ref.1, bf16[24,8,896]{2,1,0:T(8,128)(2,1)} %copy-done, ...), custom_call_target="tpu_custom_call" | custom-call | tf_op jit(solution)/shard_map/pallas_call | solution.py:136
  (6 shorter events, 0.1 us)
Async XLA Ops:
  2.1 12.6 %collective-permute-start.1 = (bf16[24,8,896]{2,1,0:T(8,128)(2,1)S(1)}, bf16[24,8,896]{2,1,0:T(8,128)(2,1)S(1)}, u32[]{:S(2)}, u32[]{:S(2)}) collective-permute-start(bf16[24,8,896]{2,1,0:T(8,128)(2,1)S(1)} %get-tuple-element.2), channel_id=1, source_target_pairs={{1,0},{2,129},{3,2},{4,131},{5,4},{6,133},{7,6},{8,135},{9,8},{10,... | collective-permute-start | bytes 1032200 | tf_op jit(solution)/shard_map/ppermute | solution.py:41
  6.3 14.7 %collective-permute-start = (bf16[24,8,896]{2,1,0:T(8,128)(2,1)S(1)}, bf16[24,8,896]{2,1,0:T(8,128)(2,1)S(1)}, u32[]{:S(2)}, u32[]{:S(2)}) collective-permute-start(bf16[24,8,896]{2,1,0:T(8,128)(2,1)S(1)} %get-tuple-element.3), channel_id=1, source_target_pairs={{0,1},{1,130},{2,3},{3,132},{4,5},{5,134},{6,7},{7,136},{8,9},{9,1... | collective-permute-start | bytes 1032200 | tf_op jit(solution)/shard_map/ppermute | solution.py:40
  14.7 6.3 %copy-start = (bf16[24,8,896]{2,1,0:T(8,128)(2,1)}, bf16[24,8,896]{2,1,0:T(8,128)(2,1)S(1)}, u32[]{:S(2)}) copy-start(bf16[24,8,896]{2,1,0:T(8,128)(2,1)S(1)} %collective-permute-done.1.hi_ref) | copy-start | bytes 1032196
  21.0 0.7 %copy-start.1 = (bf16[24,8,896]{2,1,0:T(8,128)(2,1)}, bf16[24,8,896]{2,1,0:T(8,128)(2,1)S(1)}, u32[]{:S(2)}) copy-start(bf16[24,8,896]{2,1,0:T(8,128)(2,1)S(1)} %collective-permute-done.lo_ref) | copy-start | bytes 1032196

commit v12 on v11

--- a/solution.py
+++ b/solution.py
@@ -71,9 +71,9 @@
     p_scr[used:, :] = jnp.zeros((p_scr.shape[0] - used, p_scr.shape[1]), p_scr.dtype)
     for m in range(strip):
         cols = slice(m * scans, (m + 1) * scans)
-        p_scr[0:HALO, cols] = lo_ref[:, m, :].astype(jnp.float32)
+        p_scr[0:HALO, cols] = lo_ref[:, m, :]
         p_scr[HALO:HALO + frames, cols] = own_ref[:, m, :]
-        p_scr[HALO + frames:used, cols] = hi_ref[:, m, :].astype(jnp.float32)
+        p_scr[HALO + frames:used, cols] = hi_ref[:, m, :]
     fall = f_ref[...]
     for m in range(strip):
         part = p_scr[:, m * scans:(m + 1) * scans].astype(jnp.bfloat16)
@@ -154,6 +154,7 @@
     ftab = frame_tables(frames, scale_widths, depth)
     blocks = scan_blocks(scans, scale_widths)
     first = jnp.reshape(block_index, (1,)).astype(jnp.int32)
+    low, high = low.astype(jnp.float32), high.astype(jnp.float32)
     return wavelet_core(first, ftab, low, slab, high, blocks, interpret)
 
 

time: 36.8 us -> 37.3 us (1.014)
  other arithmetic: 6.1 us -> 7.89 us
  waiting for transfers between devices: 6.34 us -> 5.44 us
  local copies, waits for them, and re-layouts: 2.45 us -> 1.71 us
    convert_element_type x0 -> x2, other arithmetic: none -> 1.79 us  [compute(): low, high = (low.astype(jnp.float32), high.astype(jnp.float32))]
    ppermute x1, waiting for transfers between devices: 6.33 us -> 5.44 us  [halos(): low = lax.ppermute(send_fwd, ('scale', 'rt'), forward)]
    unnamed x4 -> x0, local copies, waits for them, and re-layouts: 0.74 us -> none
  transfers between devices with their start and end apart: 2 -> 2, of which waited for: 1 -> 1; matrix products, arithmetic and copies ran while one was open for 18% -> 20% of each run, Pallas kernels for 0% -> 0%
where the time goes in v12:
time: 37.3 us; the launch traced here: 37.1 us
  Pallas kernels  15.2 us (41%)
  other arithmetic  7.89 us (21%)
  starting transfers between devices  6.13 us (16%)
  waiting for transfers between devices  5.44 us (15%)
  local copies, waits for them, and re-layouts  1.71 us (5%)
  between operations  0.73 us (2%)
    pallas_call x1, Pallas kernels, wavelet_core(): pl.pallas_call(wavelet_kernel, grid_spec=grid_spec, out_shape=[jax.ShapeD...  15.2 us
    ppermute x1, waiting for transfers between devices, halos(): low = lax.ppermute(send_fwd, ('scale', 'rt'), forward)  5.44 us
    ppermute x1, starting transfers between devices, halos(): high = lax.ppermute(send_bwd, ('scale', 'rt'), backward)  4.21 us
    convert_element_type x1, other arithmetic, scan_blocks(): return mexican(offsets[None], spread).astype(jnp.bfloat16)  3.79 us
    ppermute x1, starting transfers between devices, halos(): low = lax.ppermute(send_fwd, ('scale', 'rt'), forward)  1.92 us
    convert_element_type x2, other arithmetic, compute(): low, high = (low.astype(jnp.float32), high.astype(jnp.float32))  1.79 us
    convert_element_type x1, local copies, waits for them, and re-layouts, piece(): return part.astype(jnp.bfloat16)  1.39 us
    convert_element_type x1, other arithmetic, frame_tables(): return values.astype(jnp.bfloat16).reshape(-1, depth)  0.81 us
  transfers between devices with their start and end apart: 2, of which 1 were waited for; matrix products, arithmetic and copies ran while one was open for 20% of the time, Pallas kernels for 0%

profile of v12, /device:TPU:136, one launch (start us, length us, event | category | flops | bytes accessed | tf_op | source)
XLA Modules:
  0.0 37.1 jit_solution(10342403007211870010)
XLA Ops:
  0.7 1.4 %dynamic-slice_convert_fusion = (bf16[24,8,896]{2,1,0:T(8,128)(2,1)S(1)}, bf16[24,8,896]{2,1,0:T(8,128)(2,1)S(1)}) fusion(f32[24,128,896]{2,1,0:T(8,128)} %own_ref.1, s32[]{:T(128)S(6)} %select_n.36, s32[]{:T(128)S(6)} %select_n.34), kind=kLoop, calls=%fused_computation.5 | loop fusion | bytes 1376264 | tf_op jit(solution)/shard_map/convert_element_type | solution.py:36
  2.1 4.2 %collective-permute-start.1 = (bf16[24,8,896]{2,1,0:T(8,128)(2,1)S(1)}, bf16[24,8,896]{2,1,0:T(8,128)(2,1)S(1)}, u32[]{:S(2)}, u32[]{:S(2)}) collective-permute-start(bf16[24,8,896]{2,1,0:T(8,128)(2,1)S(1)} %get-tuple-element.2), channel_id=1, source_target_pairs={{1,0},{2,129},{3,2},{4,131},{5,4},{6,133},{7,6},{8,135},{9,8},{10,... | collective-permute-start | bytes 1032200 | tf_op jit(solution)/shard_map/ppermute | solution.py:41
  6.3 1.9 %collective-permute-start = (bf16[24,8,896]{2,1,0:T(8,128)(2,1)S(1)}, bf16[24,8,896]{2,1,0:T(8,128)(2,1)S(1)}, u32[]{:S(2)}, u32[]{:S(2)}) collective-permute-start(bf16[24,8,896]{2,1,0:T(8,128)(2,1)S(1)} %get-tuple-element.3), channel_id=1, source_target_pairs={{0,1},{1,130},{2,3},{3,132},{4,5},{5,134},{6,7},{7,136},{8,9},{9,1... | collective-permute-start | bytes 1032200 | tf_op jit(solution)/shard_map/ppermute | solution.py:40
  8.2 0.7 %convert_element_type.22 = f32[16]{0:T(128)S(1)} convert(s32[16]{0:T(128)} %param.3) | non-fusion elementwise | flops 16 | bytes 128 | tf_op jit(solution)/shard_map/convert_element_type | solution.py:153
  8.9 0.7 %broadcast_multiply_fusion = (f32[16]{0:T(128)S(1)}, f32[16]{0:T(128)S(1)}, f32[16]{0:T(128)S(1)}) fusion(s32[16]{0:T(128)} %param.3), kind=kLoop, calls=%fused_computation.21 | loop fusion | flops 32 | bytes 256 | tf_op jit(solution)/shard_map/mul | solution.py:60
  9.6 0.1 div.56
  9.7 0.1 div.57
  9.8 0.1 div.60
  9.8 0.1 div.61
  9.9 0.1 broadcast_add_fusion
  10.0 3.8 %fusion.3.b_ref = bf16[16,7,128,128]{3,2,1,0:T(8,128)(2,1)} fusion(f32[16]{0:T(128)S(1)} %get-tuple-element.5, f32[16]{0:T(128)S(1)} %get-tuple-element.4, f32[7,128,128]{2,1,0:T(8,128)S(1)} %broadcast_add_fusion), kind=kLoop, calls=%fused_computation.4 | loop fusion | flops 14680064 | bytes 4128896 | tf_op jit(solution)/shard_map/convert_element_type | solution.py:61
  13.9 0.8 %fusion.8.f_ref = bf16[384,128]{1,0:T(8,128)(2,1)} fusion(f32[384]{0:T(512)S(1)} %div.61, f32[384]{0:T(512)S(1)} %div.57, f32[24,128]{1,0:T(8,128)S(1)} %iota_subtract_fusion.1, pred[24,128]{1,0:T(8,128)(4,1)S(1)} %fusion.9), kind=kLoop, calls=%fused_computation.14 | loop fusion | flops 442368 | bytes 116736 | tf_op jit(solution)/shard_map/convert_element_type | solution.py:52
  14.7 0.0 collective-permute-done.1
  14.7 0.9 %convert_element_type.27.hi_ref = f32[24,8,896]{2,1,0:T(8,128)} convert(bf16[24,8,896]{2,1,0:T(8,128)(2,1)S(1)} %collective-permute-done.1) | non-fusion elementwise | flops 172032 | bytes 1032192 | tf_op jit(solution)/shard_map/convert_element_type | solution.py:157
  15.6 5.4 %collective-permute-done = bf16[24,8,896]{2,1,0:T(8,128)(2,1)S(1)} collective-permute-done((bf16[24,8,896]{2,1,0:T(8,128)(2,1)S(1)}, bf16[24,8,896]{2,1,0:T(8,128)(2,1)S(1)}, u32[]{:S(2)}, u32[]{:S(2)}) %collective-permute-start) | collective-permute-done | bytes 344096 | tf_op jit(solution)/shard_map/ppermute | solution.py:40
  21.0 0.9 %convert_element_type.25.lo_ref = f32[24,8,896]{2,1,0:T(8,128)} convert(bf16[24,8,896]{2,1,0:T(8,128)(2,1)S(1)} %collective-permute-done) | non-fusion elementwise | flops 172032 | bytes 1032192 | tf_op jit(solution)/shard_map/convert_element_type | solution.py:157
  21.9 15.2 %shard_map.41 = (bf16[24,8,896]{2,1,0:T(8,128)(2,1)}, f32[24,8,896]{2,1,0:T(8,128)}) custom-call(s32[1]{0:T(128)} %bitcast.strip_ref, bf16[384,128]{1,0:T(8,128)(2,1)} %fusion.8.f_ref, f32[24,8,896]{2,1,0:T(8,128)} %convert_element_type.25.lo_ref, f32[24,128,896]{2,1,0:T(8,128)} %own_ref.1, f32[24,8,896]{2,1,0:T(8,128)} %convert_element_type.27.hi_ref, ...), custom_call_target="tpu_custom_call" | custom-call | tf_op jit(solution)/shard_map/pallas_call | solution.py:136
  (6 shorter events, 0.1 us)
Async XLA Ops:
  2.1 12.6 %collective-permute-start.1 = (bf16[24,8,896]{2,1,0:T(8,128)(2,1)S(1)}, bf16[24,8,896]{2,1,0:T(8,128)(2,1)S(1)}, u32[]{:S(2)}, u32[]{:S(2)}) collective-permute-start(bf16[24,8,896]{2,1,0:T(8,128)(2,1)S(1)} %get-tuple-element.2), channel_id=1, source_target_pairs={{1,0},{2,129},{3,2},{4,131},{5,4},{6,133},{7,6},{8,135},{9,8},{10,... | collective-permute-start | bytes 1032200 | tf_op jit(solution)/shard_map/ppermute | solution.py:41
  6.3 14.7 %collective-permute-start = (bf16[24,8,896]{2,1,0:T(8,128)(2,1)S(1)}, bf16[24,8,896]{2,1,0:T(8,128)(2,1)S(1)}, u32[]{:S(2)}, u32[]{:S(2)}) collective-permute-start(bf16[24,8,896]{2,1,0:T(8,128)(2,1)S(1)} %get-tuple-element.3), channel_id=1, source_target_pairs={{0,1},{1,130},{2,3},{3,132},{4,5},{5,134},{6,7},{7,136},{8,9},{9,1... | collective-permute-start | bytes 1032200 | tf_op jit(solution)/shard_map/ppermute | solution.py:40

commit v13 on v11

--- a/solution.py
+++ b/solution.py
@@ -91,12 +91,20 @@
         lhs = g_scr[c].astype(jnp.bfloat16)
         answer = jnp.dot(lhs, table[...], preferred_element_type=jnp.float32).astype(jnp.bfloat16)
         answer = answer.astype(jnp.float32)
-        if c == 0:
-            best_scr[...] = answer
-            total_scr[...] = answer * answer
+        if c % 2 == 0 and c + 1 < count:
+            held = answer
+            continue
+        if c % 2 == 1:
+            best = jnp.maximum(held, answer)
+            square = held * held + answer * answer
         else:
-            best_scr[...] = jnp.maximum(best_scr[...], answer)
-            total_scr[...] = total_scr[...] + answer * answer
+            best, square = answer, answer * answer
+        if c < 2:
+            best_scr[...] = best
+            total_scr[...] = square
+        else:
+            best_scr[...] = jnp.maximum(best_scr[...], best)
+            total_scr[...] = total_scr[...] + square
 
     for m in range(strip):
         peak_ref[:, m, :] = best_scr[m * frames:(m + 1) * frames, :].astype(peak_ref.dtype)

time: 36.8 us -> 36.9 us (level)
  transfers between devices with their start and end apart: 2 -> 2, of which waited for: 1 -> 1; matrix products, arithmetic and copies ran while one was open for 18% -> 17% of each run, Pallas kernels for 0% -> 0%
where the time goes in v13:
time: 36.9 us; the launch traced here: 36.7 us
  Pallas kernels  15 us (41%)
  waiting for transfers between devices  6.34 us (17%)
  starting transfers between devices  6.13 us (17%)
  other arithmetic  6.1 us (17%)
  local copies, waits for them, and re-layouts  2.45 us (7%)
  between operations  0.73 us (2%)
    pallas_call x1, Pallas kernels, wavelet_core(): pl.pallas_call(wavelet_kernel, grid_spec=grid_spec, out_shape=[jax.ShapeD...  15 us
    ppermute x1, waiting for transfers between devices, halos(): low = lax.ppermute(send_fwd, ('scale', 'rt'), forward)  6.33 us
    ppermute x1, starting transfers between devices, halos(): high = lax.ppermute(send_bwd, ('scale', 'rt'), backward)  4.21 us
    convert_element_type x1, other arithmetic, scan_blocks(): return mexican(offsets[None], spread).astype(jnp.bfloat16)  3.79 us
    ppermute x1, starting transfers between devices, halos(): low = lax.ppermute(send_fwd, ('scale', 'rt'), forward)  1.92 us
    convert_element_type x1, local copies, waits for them, and re-layouts, piece(): return part.astype(jnp.bfloat16)  1.39 us
    convert_element_type x1, other arithmetic, frame_tables(): return values.astype(jnp.bfloat16).reshape(-1, depth)  0.81 us
    unnamed x4, local copies, waits for them, and re-layouts  0.74 us
  transfers between devices with their start and end apart: 2, of which 1 were waited for; matrix products, arithmetic and copies ran while one was open for 17% of the time, Pallas kernels for 0%

profile of v13, /device:TPU:136, one launch (start us, length us, event | category | flops | bytes accessed | tf_op | source)
XLA Modules:
  0.0 36.7 jit_solution(8854674068468137068)
XLA Ops:
  0.7 1.4 %dynamic-slice_convert_fusion = (bf16[24,8,896]{2,1,0:T(8,128)(2,1)S(1)}, bf16[24,8,896]{2,1,0:T(8,128)(2,1)S(1)}) fusion(f32[24,128,896]{2,1,0:T(8,128)} %own_ref.1, s32[]{:T(128)S(6)} %select_n.36, s32[]{:T(128)S(6)} %select_n.34), kind=kLoop, calls=%fused_computation.5 | loop fusion | bytes 1376264 | tf_op jit(solution)/shard_map/convert_element_type | solution.py:36
  2.1 4.2 %collective-permute-start.1 = (bf16[24,8,896]{2,1,0:T(8,128)(2,1)S(1)}, bf16[24,8,896]{2,1,0:T(8,128)(2,1)S(1)}, u32[]{:S(2)}, u32[]{:S(2)}) collective-permute-start(bf16[24,8,896]{2,1,0:T(8,128)(2,1)S(1)} %get-tuple-element.2), channel_id=1, source_target_pairs={{1,0},{2,129},{3,2},{4,131},{5,4},{6,133},{7,6},{8,135},{9,8},{10,... | collective-permute-start | bytes 1032200 | tf_op jit(solution)/shard_map/ppermute | solution.py:41
  6.3 1.9 %collective-permute-start = (bf16[24,8,896]{2,1,0:T(8,128)(2,1)S(1)}, bf16[24,8,896]{2,1,0:T(8,128)(2,1)S(1)}, u32[]{:S(2)}, u32[]{:S(2)}) collective-permute-start(bf16[24,8,896]{2,1,0:T(8,128)(2,1)S(1)} %get-tuple-element.3), channel_id=1, source_target_pairs={{0,1},{1,130},{2,3},{3,132},{4,5},{5,134},{6,7},{7,136},{8,9},{9,1... | collective-permute-start | bytes 1032200 | tf_op jit(solution)/shard_map/ppermute | solution.py:40
  8.2 0.7 %convert_element_type.16 = f32[16]{0:T(128)S(1)} convert(s32[16]{0:T(128)} %param.3) | non-fusion elementwise | flops 16 | bytes 128 | tf_op jit(solution)/shard_map/convert_element_type | solution.py:161
  8.9 0.7 %broadcast_multiply_fusion = (f32[16]{0:T(128)S(1)}, f32[16]{0:T(128)S(1)}, f32[16]{0:T(128)S(1)}) fusion(s32[16]{0:T(128)} %param.3), kind=kLoop, calls=%fused_computation.21 | loop fusion | flops 32 | bytes 256 | tf_op jit(solution)/shard_map/mul | solution.py:60
  9.6 0.1 div.56
  9.7 0.1 div.57
  9.8 0.1 div.60
  9.8 0.1 div.61
  9.9 0.1 broadcast_add_fusion
  10.0 3.8 %fusion.3.b_ref = bf16[16,7,128,128]{3,2,1,0:T(8,128)(2,1)} fusion(f32[16]{0:T(128)S(1)} %get-tuple-element.5, f32[16]{0:T(128)S(1)} %get-tuple-element.4, f32[7,128,128]{2,1,0:T(8,128)S(1)} %broadcast_add_fusion), kind=kLoop, calls=%fused_computation.4 | loop fusion | flops 14680064 | bytes 4128896 | tf_op jit(solution)/shard_map/convert_element_type | solution.py:61
  13.9 0.8 %fusion.8.f_ref = bf16[384,128]{1,0:T(8,128)(2,1)} fusion(f32[384]{0:T(512)S(1)} %div.61, f32[384]{0:T(512)S(1)} %div.57, f32[24,128]{1,0:T(8,128)S(1)} %iota_subtract_fusion.1, pred[24,128]{1,0:T(8,128)(4,1)S(1)} %fusion.9), kind=kLoop, calls=%fused_computation.14 | loop fusion | flops 442368 | bytes 116736 | tf_op jit(solution)/shard_map/convert_element_type | solution.py:52
  14.7 0.0 collective-permute-done.1.hi_ref
  14.7 0.0 copy-start
  14.7 6.3 %collective-permute-done.lo_ref = bf16[24,8,896]{2,1,0:T(8,128)(2,1)S(1)} collective-permute-done((bf16[24,8,896]{2,1,0:T(8,128)(2,1)S(1)}, bf16[24,8,896]{2,1,0:T(8,128)(2,1)S(1)}, u32[]{:S(2)}, u32[]{:S(2)}) %collective-permute-start) | collective-permute-done | bytes 344096 | tf_op jit(solution)/shard_map/ppermute | solution.py:40
  21.0 0.0 copy-start.1
  21.0 0.0 copy-done
  21.0 0.7 %copy-done.1 = bf16[24,8,896]{2,1,0:T(8,128)(2,1)} copy-done((bf16[24,8,896]{2,1,0:T(8,128)(2,1)}, bf16[24,8,896]{2,1,0:T(8,128)(2,1)S(1)}, u32[]{:S(2)}) %copy-start.1) | copy-done | bytes 344088
  21.8 15.0 %shard_map.41 = (bf16[24,8,896]{2,1,0:T(8,128)(2,1)}, f32[24,8,896]{2,1,0:T(8,128)}) custom-call(s32[1]{0:T(128)} %bitcast.strip_ref, bf16[384,128]{1,0:T(8,128)(2,1)} %fusion.8.f_ref, bf16[24,8,896]{2,1,0:T(8,128)(2,1)} %copy-done.1, f32[24,128,896]{2,1,0:T(8,128)} %own_ref.1, bf16[24,8,896]{2,1,0:T(8,128)(2,1)} %copy-done, ...), custom_call_target="tpu_custom_call" | custom-call | tf_op jit(solution)/shard_map/pallas_call | solution.py:144
  (6 shorter events, 0.1 us)
Async XLA Ops:
  2.1 12.6 %collective-permute-start.1 = (bf16[24,8,896]{2,1,0:T(8,128)(2,1)S(1)}, bf16[24,8,896]{2,1,0:T(8,128)(2,1)S(1)}, u32[]{:S(2)}, u32[]{:S(2)}) collective-permute-start(bf16[24,8,896]{2,1,0:T(8,128)(2,1)S(1)} %get-tuple-element.2), channel_id=1, source_target_pairs={{1,0},{2,129},{3,2},{4,131},{5,4},{6,133},{7,6},{8,135},{9,8},{10,... | collective-permute-start | bytes 1032200 | tf_op jit(solution)/shard_map/ppermute | solution.py:41
  6.3 14.7 %collective-permute-start = (bf16[24,8,896]{2,1,0:T(8,128)(2,1)S(1)}, bf16[24,8,896]{2,1,0:T(8,128)(2,1)S(1)}, u32[]{:S(2)}, u32[]{:S(2)}) collective-permute-start(bf16[24,8,896]{2,1,0:T(8,128)(2,1)S(1)} %get-tuple-element.3), channel_id=1, source_target_pairs={{0,1},{1,130},{2,3},{3,132},{4,5},{5,134},{6,7},{7,136},{8,9},{9,1... | collective-permute-start | bytes 1032200 | tf_op jit(solution)/shard_map/ppermute | solution.py:40
  14.7 6.3 %copy-start = (bf16[24,8,896]{2,1,0:T(8,128)(2,1)}, bf16[24,8,896]{2,1,0:T(8,128)(2,1)S(1)}, u32[]{:S(2)}) copy-start(bf16[24,8,896]{2,1,0:T(8,128)(2,1)S(1)} %collective-permute-done.1.hi_ref) | copy-start | bytes 1032196
  21.0 0.7 %copy-start.1 = (bf16[24,8,896]{2,1,0:T(8,128)(2,1)}, bf16[24,8,896]{2,1,0:T(8,128)(2,1)S(1)}, u32[]{:S(2)}) copy-start(bf16[24,8,896]{2,1,0:T(8,128)(2,1)S(1)} %collective-permute-done.lo_ref) | copy-start | bytes 1032196

commit v14 on v11

--- a/solution.py
+++ b/solution.py
@@ -149,7 +149,7 @@
 
 def compute(slab, block_index, low, high, widths, interpret=False):
     frames, strip, scans = low.shape
-    depth = -(-(frames + 2 * HALO) // TILE) * TILE
+    depth = -(-(frames + 2 * HALO) // 16) * 16
     scale_widths = widths.astype(jnp.float32)
     ftab = frame_tables(frames, scale_widths, depth)
     blocks = scan_blocks(scans, scale_widths)

time: 36.8 us -> 36.8 us (level)
  no operation moved by 1% of the time
where the time goes in v14:
time: 36.8 us; the launch traced here: 36.6 us
  Pallas kernels  14.9 us (40%)
  waiting for transfers between devices  6.34 us (17%)
  starting transfers between devices  6.13 us (17%)
  other arithmetic  6.1 us (17%)
  local copies, waits for them, and re-layouts  2.45 us (7%)
  between operations  0.73 us (2%)
    pallas_call x1, Pallas kernels, wavelet_core(): pl.pallas_call(wavelet_kernel, grid_spec=grid_spec, out_shape=[jax.ShapeD...  14.9 us
    ppermute x1, waiting for transfers between devices, halos(): low = lax.ppermute(send_fwd, ('scale', 'rt'), forward)  6.33 us
    ppermute x1, starting transfers between devices, halos(): high = lax.ppermute(send_bwd, ('scale', 'rt'), backward)  4.21 us
    convert_element_type x1, other arithmetic, scan_blocks(): return mexican(offsets[None], spread).astype(jnp.bfloat16)  3.79 us
    ppermute x1, starting transfers between devices, halos(): low = lax.ppermute(send_fwd, ('scale', 'rt'), forward)  1.92 us
    convert_element_type x1, local copies, waits for them, and re-layouts, piece(): return part.astype(jnp.bfloat16)  1.39 us
    convert_element_type x1, other arithmetic, frame_tables(): return values.astype(jnp.bfloat16).reshape(-1, depth)  0.81 us
    unnamed x4, local copies, waits for them, and re-layouts  0.74 us
  transfers between devices with their start and end apart: 2, of which 1 were waited for; matrix products, arithmetic and copies ran while one was open for 18% of the time, Pallas kernels for 0%

profile of v14, /device:TPU:136, one launch (start us, length us, event | category | flops | bytes accessed | tf_op | source)
XLA Modules:
  0.0 36.6 jit_solution(5121942151159145529)
XLA Ops:
  0.7 1.4 %dynamic-slice_convert_fusion = (bf16[24,8,896]{2,1,0:T(8,128)(2,1)S(1)}, bf16[24,8,896]{2,1,0:T(8,128)(2,1)S(1)}) fusion(f32[24,128,896]{2,1,0:T(8,128)} %own_ref.1, s32[]{:T(128)S(6)} %select_n.36, s32[]{:T(128)S(6)} %select_n.34), kind=kLoop, calls=%fused_computation.5 | loop fusion | bytes 1376264 | tf_op jit(solution)/shard_map/convert_element_type | solution.py:36
  2.1 4.2 %collective-permute-start.1 = (bf16[24,8,896]{2,1,0:T(8,128)(2,1)S(1)}, bf16[24,8,896]{2,1,0:T(8,128)(2,1)S(1)}, u32[]{:S(2)}, u32[]{:S(2)}) collective-permute-start(bf16[24,8,896]{2,1,0:T(8,128)(2,1)S(1)} %get-tuple-element.2), channel_id=1, source_target_pairs={{1,0},{2,129},{3,2},{4,131},{5,4},{6,133},{7,6},{8,135},{9,8},{10,... | collective-permute-start | bytes 1032200 | tf_op jit(solution)/shard_map/ppermute | solution.py:41
  6.3 1.9 %collective-permute-start = (bf16[24,8,896]{2,1,0:T(8,128)(2,1)S(1)}, bf16[24,8,896]{2,1,0:T(8,128)(2,1)S(1)}, u32[]{:S(2)}, u32[]{:S(2)}) collective-permute-start(bf16[24,8,896]{2,1,0:T(8,128)(2,1)S(1)} %get-tuple-element.3), channel_id=1, source_target_pairs={{0,1},{1,130},{2,3},{3,132},{4,5},{5,134},{6,7},{7,136},{8,9},{9,1... | collective-permute-start | bytes 1032200 | tf_op jit(solution)/shard_map/ppermute | solution.py:40
  8.2 0.7 %convert_element_type.16 = f32[16]{0:T(128)S(1)} convert(s32[16]{0:T(128)} %param.3) | non-fusion elementwise | flops 16 | bytes 128 | tf_op jit(solution)/shard_map/convert_element_type | solution.py:153
  8.9 0.7 %broadcast_multiply_fusion = (f32[16]{0:T(128)S(1)}, f32[16]{0:T(128)S(1)}, f32[16]{0:T(128)S(1)}) fusion(s32[16]{0:T(128)} %param.3), kind=kLoop, calls=%fused_computation.21 | loop fusion | flops 32 | bytes 256 | tf_op jit(solution)/shard_map/mul | solution.py:60
  9.6 0.1 div.56
  9.7 0.1 div.57
  9.8 0.1 div.60
  9.8 0.1 div.61
  9.9 0.1 broadcast_add_fusion
  10.0 3.8 %fusion.3.b_ref = bf16[16,7,128,128]{3,2,1,0:T(8,128)(2,1)} fusion(f32[16]{0:T(128)S(1)} %get-tuple-element.5, f32[16]{0:T(128)S(1)} %get-tuple-element.4, f32[7,128,128]{2,1,0:T(8,128)S(1)} %broadcast_add_fusion), kind=kLoop, calls=%fused_computation.4 | loop fusion | flops 14680064 | bytes 4128896 | tf_op jit(solution)/shard_map/convert_element_type | solution.py:61
  13.9 0.8 %fusion.8.f_ref = bf16[384,80]{1,0:T(8,128)(2,1)} fusion(f32[384]{0:T(512)S(1)} %div.61, f32[384]{0:T(512)S(1)} %div.57, f32[24,80]{1,0:T(8,128)S(1)} %iota_subtract_fusion.1, pred[24,80]{1,0:T(8,128)(4,1)S(1)} %fusion.9), kind=kLoop, calls=%fused_computation.14 | loop fusion | flops 276480 | bytes 74112 | tf_op jit(solution)/shard_map/convert_element_type | solution.py:52
  14.7 0.0 collective-permute-done.1.hi_ref
  14.7 0.0 copy-start
  14.7 6.3 %collective-permute-done.lo_ref = bf16[24,8,896]{2,1,0:T(8,128)(2,1)S(1)} collective-permute-done((bf16[24,8,896]{2,1,0:T(8,128)(2,1)S(1)}, bf16[24,8,896]{2,1,0:T(8,128)(2,1)S(1)}, u32[]{:S(2)}, u32[]{:S(2)}) %collective-permute-start) | collective-permute-done | bytes 344096 | tf_op jit(solution)/shard_map/ppermute | solution.py:40
  21.0 0.0 copy-start.1
  21.0 0.0 copy-done
  21.0 0.7 %copy-done.1 = bf16[24,8,896]{2,1,0:T(8,128)(2,1)} copy-done((bf16[24,8,896]{2,1,0:T(8,128)(2,1)}, bf16[24,8,896]{2,1,0:T(8,128)(2,1)S(1)}, u32[]{:S(2)}) %copy-start.1) | copy-done | bytes 344088
  21.8 14.9 %shard_map.41 = (bf16[24,8,896]{2,1,0:T(8,128)(2,1)}, f32[24,8,896]{2,1,0:T(8,128)}) custom-call(s32[1]{0:T(128)} %bitcast.strip_ref, bf16[384,80]{1,0:T(8,128)(2,1)} %fusion.8.f_ref, bf16[24,8,896]{2,1,0:T(8,128)(2,1)} %copy-done.1, f32[24,128,896]{2,1,0:T(8,128)} %own_ref.1, bf16[24,8,896]{2,1,0:T(8,128)(2,1)} %copy-done, ...), custom_call_target="tpu_custom_call" | custom-call | tf_op jit(solution)/shard_map/pallas_call | solution.py:136
  (6 shorter events, 0.1 us)
Async XLA Ops:
  2.1 12.6 %collective-permute-start.1 = (bf16[24,8,896]{2,1,0:T(8,128)(2,1)S(1)}, bf16[24,8,896]{2,1,0:T(8,128)(2,1)S(1)}, u32[]{:S(2)}, u32[]{:S(2)}) collective-permute-start(bf16[24,8,896]{2,1,0:T(8,128)(2,1)S(1)} %get-tuple-element.2), channel_id=1, source_target_pairs={{1,0},{2,129},{3,2},{4,131},{5,4},{6,133},{7,6},{8,135},{9,8},{10,... | collective-permute-start | bytes 1032200 | tf_op jit(solution)/shard_map/ppermute | solution.py:41
  6.3 14.7 %collective-permute-start = (bf16[24,8,896]{2,1,0:T(8,128)(2,1)S(1)}, bf16[24,8,896]{2,1,0:T(8,128)(2,1)S(1)}, u32[]{:S(2)}, u32[]{:S(2)}) collective-permute-start(bf16[24,8,896]{2,1,0:T(8,128)(2,1)S(1)} %get-tuple-element.3), channel_id=1, source_target_pairs={{0,1},{1,130},{2,3},{3,132},{4,5},{5,134},{6,7},{7,136},{8,9},{9,1... | collective-permute-start | bytes 1032200 | tf_op jit(solution)/shard_map/ppermute | solution.py:40
  14.7 6.3 %copy-start = (bf16[24,8,896]{2,1,0:T(8,128)(2,1)}, bf16[24,8,896]{2,1,0:T(8,128)(2,1)S(1)}, u32[]{:S(2)}) copy-start(bf16[24,8,896]{2,1,0:T(8,128)(2,1)S(1)} %collective-permute-done.1.hi_ref) | copy-start | bytes 1032196
  21.0 0.7 %copy-start.1 = (bf16[24,8,896]{2,1,0:T(8,128)(2,1)}, bf16[24,8,896]{2,1,0:T(8,128)(2,1)S(1)}, u32[]{:S(2)}) copy-start(bf16[24,8,896]{2,1,0:T(8,128)(2,1)S(1)} %collective-permute-done.lo_ref) | copy-start | bytes 1032196

commit v15 on v14

--- a/solution.py
+++ b/solution.py
@@ -74,12 +74,10 @@
         p_scr[0:HALO, cols] = lo_ref[:, m, :].astype(jnp.float32)
         p_scr[HALO:HALO + frames, cols] = own_ref[:, m, :]
         p_scr[HALO + frames:used, cols] = hi_ref[:, m, :].astype(jnp.float32)
-    fall = f_ref[...]
+    g_all = jnp.dot(f_ref[...], p_scr[...].astype(jnp.bfloat16), preferred_element_type=jnp.float32)
     for m in range(strip):
-        part = p_scr[:, m * scans:(m + 1) * scans].astype(jnp.bfloat16)
-        gm = jnp.dot(fall, part, preferred_element_type=jnp.float32)
         for cc in range(count):
-            g_scr[cc, m * frames:(m + 1) * frames, :] = gm[cc * frames:(cc + 1) * frames, :]
+            g_scr[cc, m * frames:(m + 1) * frames, :] = g_all[cc * frames:(cc + 1) * frames, m * scans:(m + 1) * scans]
 
     for c in range(count):
         table = s_scr.at[c % 2]

time: 36.8 us -> 36.9 us (level)
  transfers between devices with their start and end apart: 2 -> 2, of which waited for: 1 -> 1; matrix products, arithmetic and copies ran while one was open for 18% -> 17% of each run, Pallas kernels for 0% -> 0%
where the time goes in v15:
time: 36.9 us; the launch traced here: 36.7 us
  Pallas kernels  14.9 us (40%)
  waiting for transfers between devices  6.34 us (17%)
  starting transfers between devices  6.13 us (17%)
  other arithmetic  6.1 us (17%)
  local copies, waits for them, and re-layouts  2.45 us (7%)
  between operations  0.73 us (2%)
    pallas_call x1, Pallas kernels, wavelet_core(): pl.pallas_call(wavelet_kernel, grid_spec=grid_spec, out_shape=[jax.ShapeD...  14.9 us
    ppermute x1, waiting for transfers between devices, halos(): low = lax.ppermute(send_fwd, ('scale', 'rt'), forward)  6.33 us
    ppermute x1, starting transfers between devices, halos(): high = lax.ppermute(send_bwd, ('scale', 'rt'), backward)  4.21 us
    convert_element_type x1, other arithmetic, scan_blocks(): return mexican(offsets[None], spread).astype(jnp.bfloat16)  3.79 us
    ppermute x1, starting transfers between devices, halos(): low = lax.ppermute(send_fwd, ('scale', 'rt'), forward)  1.92 us
    convert_element_type x1, local copies, waits for them, and re-layouts, piece(): return part.astype(jnp.bfloat16)  1.39 us
    convert_element_type x1, other arithmetic, frame_tables(): return values.astype(jnp.bfloat16).reshape(-1, depth)  0.81 us
    unnamed x4, local copies, waits for them, and re-layouts  0.74 us
  transfers between devices with their start and end apart: 2, of which 1 were waited for; matrix products, arithmetic and copies ran while one was open for 17% of the time, Pallas kernels for 0%

profile of v15, /device:TPU:136, one launch (start us, length us, event | category | flops | bytes accessed | tf_op | source)
XLA Modules:
  0.0 36.7 jit_solution(625573400363576685)
XLA Ops:
  0.7 1.4 %dynamic-slice_convert_fusion = (bf16[24,8,896]{2,1,0:T(8,128)(2,1)S(1)}, bf16[24,8,896]{2,1,0:T(8,128)(2,1)S(1)}) fusion(f32[24,128,896]{2,1,0:T(8,128)} %own_ref.1, s32[]{:T(128)S(6)} %select_n.36, s32[]{:T(128)S(6)} %select_n.34), kind=kLoop, calls=%fused_computation.5 | loop fusion | bytes 1376264 | tf_op jit(solution)/shard_map/convert_element_type | solution.py:36
  2.1 4.2 %collective-permute-start.1 = (bf16[24,8,896]{2,1,0:T(8,128)(2,1)S(1)}, bf16[24,8,896]{2,1,0:T(8,128)(2,1)S(1)}, u32[]{:S(2)}, u32[]{:S(2)}) collective-permute-start(bf16[24,8,896]{2,1,0:T(8,128)(2,1)S(1)} %get-tuple-element.2), channel_id=1, source_target_pairs={{1,0},{2,129},{3,2},{4,131},{5,4},{6,133},{7,6},{8,135},{9,8},{10,... | collective-permute-start | bytes 1032200 | tf_op jit(solution)/shard_map/ppermute | solution.py:41
  6.3 1.9 %collective-permute-start = (bf16[24,8,896]{2,1,0:T(8,128)(2,1)S(1)}, bf16[24,8,896]{2,1,0:T(8,128)(2,1)S(1)}, u32[]{:S(2)}, u32[]{:S(2)}) collective-permute-start(bf16[24,8,896]{2,1,0:T(8,128)(2,1)S(1)} %get-tuple-element.3), channel_id=1, source_target_pairs={{0,1},{1,130},{2,3},{3,132},{4,5},{5,134},{6,7},{7,136},{8,9},{9,1... | collective-permute-start | bytes 1032200 | tf_op jit(solution)/shard_map/ppermute | solution.py:40
  8.2 0.7 %convert_element_type.16 = f32[16]{0:T(128)S(1)} convert(s32[16]{0:T(128)} %param.3) | non-fusion elementwise | flops 16 | bytes 128 | tf_op jit(solution)/shard_map/convert_element_type | solution.py:151
  8.9 0.7 %broadcast_multiply_fusion = (f32[16]{0:T(128)S(1)}, f32[16]{0:T(128)S(1)}, f32[16]{0:T(128)S(1)}) fusion(s32[16]{0:T(128)} %param.3), kind=kLoop, calls=%fused_computation.21 | loop fusion | flops 32 | bytes 256 | tf_op jit(solution)/shard_map/mul | solution.py:60
  9.6 0.1 div.56
  9.7 0.1 div.57
  9.8 0.1 div.60
  9.8 0.1 div.61
  9.9 0.1 broadcast_add_fusion
  10.0 3.8 %fusion.3.b_ref = bf16[16,7,128,128]{3,2,1,0:T(8,128)(2,1)} fusion(f32[16]{0:T(128)S(1)} %get-tuple-element.5, f32[16]{0:T(128)S(1)} %get-tuple-element.4, f32[7,128,128]{2,1,0:T(8,128)S(1)} %broadcast_add_fusion), kind=kLoop, calls=%fused_computation.4 | loop fusion | flops 14680064 | bytes 4128896 | tf_op jit(solution)/shard_map/convert_element_type | solution.py:61
  13.9 0.8 %fusion.8.f_ref = bf16[384,80]{1,0:T(8,128)(2,1)} fusion(f32[384]{0:T(512)S(1)} %div.61, f32[384]{0:T(512)S(1)} %div.57, f32[24,80]{1,0:T(8,128)S(1)} %iota_subtract_fusion.1, pred[24,80]{1,0:T(8,128)(4,1)S(1)} %fusion.9), kind=kLoop, calls=%fused_computation.14 | loop fusion | flops 276480 | bytes 74112 | tf_op jit(solution)/shard_map/convert_element_type | solution.py:52
  14.7 0.0 collective-permute-done.1.hi_ref
  14.7 0.0 copy-start
  14.7 6.3 %collective-permute-done.lo_ref = bf16[24,8,896]{2,1,0:T(8,128)(2,1)S(1)} collective-permute-done((bf16[24,8,896]{2,1,0:T(8,128)(2,1)S(1)}, bf16[24,8,896]{2,1,0:T(8,128)(2,1)S(1)}, u32[]{:S(2)}, u32[]{:S(2)}) %collective-permute-start) | collective-permute-done | bytes 344096 | tf_op jit(solution)/shard_map/ppermute | solution.py:40
  21.0 0.0 copy-start.1
  21.0 0.0 copy-done
  21.0 0.7 %copy-done.1 = bf16[24,8,896]{2,1,0:T(8,128)(2,1)} copy-done((bf16[24,8,896]{2,1,0:T(8,128)(2,1)}, bf16[24,8,896]{2,1,0:T(8,128)(2,1)S(1)}, u32[]{:S(2)}) %copy-start.1) | copy-done | bytes 344088
  21.8 14.9 %shard_map.41 = (bf16[24,8,896]{2,1,0:T(8,128)(2,1)}, f32[24,8,896]{2,1,0:T(8,128)}) custom-call(s32[1]{0:T(128)} %bitcast.strip_ref, bf16[384,80]{1,0:T(8,128)(2,1)} %fusion.8.f_ref, bf16[24,8,896]{2,1,0:T(8,128)(2,1)} %copy-done.1, f32[24,128,896]{2,1,0:T(8,128)} %own_ref.1, bf16[24,8,896]{2,1,0:T(8,128)(2,1)} %copy-done, ...), custom_call_target="tpu_custom_call" | custom-call | tf_op jit(solution)/shard_map/pallas_call | solution.py:134
  (6 shorter events, 0.1 us)
Async XLA Ops:
  2.1 12.6 %collective-permute-start.1 = (bf16[24,8,896]{2,1,0:T(8,128)(2,1)S(1)}, bf16[24,8,896]{2,1,0:T(8,128)(2,1)S(1)}, u32[]{:S(2)}, u32[]{:S(2)}) collective-permute-start(bf16[24,8,896]{2,1,0:T(8,128)(2,1)S(1)} %get-tuple-element.2), channel_id=1, source_target_pairs={{1,0},{2,129},{3,2},{4,131},{5,4},{6,133},{7,6},{8,135},{9,8},{10,... | collective-permute-start | bytes 1032200 | tf_op jit(solution)/shard_map/ppermute | solution.py:41
  6.3 14.7 %collective-permute-start = (bf16[24,8,896]{2,1,0:T(8,128)(2,1)S(1)}, bf16[24,8,896]{2,1,0:T(8,128)(2,1)S(1)}, u32[]{:S(2)}, u32[]{:S(2)}) collective-permute-start(bf16[24,8,896]{2,1,0:T(8,128)(2,1)S(1)} %get-tuple-element.3), channel_id=1, source_target_pairs={{0,1},{1,130},{2,3},{3,132},{4,5},{5,134},{6,7},{7,136},{8,9},{9,1... | collective-permute-start | bytes 1032200 | tf_op jit(solution)/shard_map/ppermute | solution.py:40
  14.7 6.3 %copy-start = (bf16[24,8,896]{2,1,0:T(8,128)(2,1)}, bf16[24,8,896]{2,1,0:T(8,128)(2,1)S(1)}, u32[]{:S(2)}) copy-start(bf16[24,8,896]{2,1,0:T(8,128)(2,1)S(1)} %collective-permute-done.1.hi_ref) | copy-start | bytes 1032196
  21.0 0.7 %copy-start.1 = (bf16[24,8,896]{2,1,0:T(8,128)(2,1)}, bf16[24,8,896]{2,1,0:T(8,128)(2,1)S(1)}, u32[]{:S(2)}) copy-start(bf16[24,8,896]{2,1,0:T(8,128)(2,1)S(1)} %collective-permute-done.lo_ref) | copy-start | bytes 1032196

commit v16 on v11

--- a/solution.py
+++ b/solution.py
@@ -61,12 +61,14 @@
     return mexican(offsets[None], spread).astype(jnp.bfloat16)
 
 
-def wavelet_kernel(strip_ref, f_ref, lo_ref, own_ref, hi_ref, b_ref, peak_ref, energy_ref,
-                   p_scr, g_scr, s_scr, best_scr, total_scr):
+def wavelet_kernel(strip_ref, f_ref, lo_ref, own_ref, hi_ref, b_hbm, peak_ref, energy_ref,
+                   b_ref, sem, p_scr, g_scr, s_scr, best_scr, total_scr):
     count, rows, scans = g_scr.shape
     frames, strip, _ = own_ref.shape
     nb = scans // TILE
     used = 2 * HALO + frames
+    tables = pltpu.make_async_copy(b_hbm, b_ref, sem.at[0])
+    tables.start()
 
     p_scr[used:, :] = jnp.zeros((p_scr.shape[0] - used, p_scr.shape[1]), p_scr.dtype)
     for m in range(strip):
@@ -81,6 +83,7 @@
         for cc in range(count):
             g_scr[cc, m * frames:(m + 1) * frames, :] = gm[cc * frames:(cc + 1) * frames, :]
 
+    tables.wait()
     for c in range(count):
         table = s_scr.at[c % 2]
         flipped = {d: b_ref[c, d].T for d in range(1, nb)}
@@ -119,13 +122,15 @@
             pl.BlockSpec((HALO, strip, scans), whole3),
             pl.BlockSpec((frames, strip, scans), lambda c, i: (0, i[0], 0)),
             pl.BlockSpec((HALO, strip, scans), whole3),
-            pl.BlockSpec((count, nblk, TILE, TILE), lambda c, i: (0, 0, 0, 0)),
+            pl.BlockSpec(memory_space=pl.ANY),
         ],
         out_specs=[
             pl.BlockSpec((frames, strip, scans), whole3),
             pl.BlockSpec((frames, strip, scans), whole3),
         ],
         scratch_shapes=[
+            pltpu.VMEM(blocks.shape, blocks.dtype),
+            pltpu.SemaphoreType.DMA((1,)),
             pltpu.VMEM((depth, strip * scans), jnp.float32),
             pltpu.VMEM((count, rows, scans), jnp.float32),
             pltpu.VMEM((2, scans, scans), jnp.bfloat16),

time: 36.8 us -> 36.2 us (0.984)
  Pallas kernels: 14.9 us -> 14.2 us
    pallas_call x1, Pallas kernels: 14.9 us -> 14.2 us  [wavelet_core(): pl.pallas_call(wavelet_kernel, grid_spec=grid_spec, out_shape=[jax.ShapeD...]
where the time goes in v16:
time: 36.2 us; the launch traced here: 36 us
  Pallas kernels  14.2 us (39%)
  waiting for transfers between devices  6.34 us (18%)
  starting transfers between devices  6.13 us (17%)
  other arithmetic  6.1 us (17%)
  local copies, waits for them, and re-layouts  2.45 us (7%)
  between operations  0.73 us (2%)
    pallas_call x1, Pallas kernels, wavelet_core(): pl.pallas_call(wavelet_kernel, grid_spec=grid_spec, out_shape=[jax.ShapeD...  14.2 us
    ppermute x1, waiting for transfers between devices, halos(): low = lax.ppermute(send_fwd, ('scale', 'rt'), forward)  6.33 us
    ppermute x1, starting transfers between devices, halos(): high = lax.ppermute(send_bwd, ('scale', 'rt'), backward)  4.21 us
    convert_element_type x1, other arithmetic, scan_blocks(): return mexican(offsets[None], spread).astype(jnp.bfloat16)  3.79 us
    ppermute x1, starting transfers between devices, halos(): low = lax.ppermute(send_fwd, ('scale', 'rt'), forward)  1.92 us
    convert_element_type x1, local copies, waits for them, and re-layouts, piece(): return part.astype(jnp.bfloat16)  1.39 us
    convert_element_type x1, other arithmetic, frame_tables(): return values.astype(jnp.bfloat16).reshape(-1, depth)  0.81 us
    unnamed x4, local copies, waits for them, and re-layouts  0.74 us
  transfers between devices with their start and end apart: 2, of which 1 were waited for; matrix products, arithmetic and copies ran while one was open for 18% of the time, Pallas kernels for 0%

profile of v16, /device:TPU:136, one launch (start us, length us, event | category | flops | bytes accessed | tf_op | source)
XLA Modules:
  0.0 36.0 jit_solution(14913637765890140419)
XLA Ops:
  0.7 1.4 %dynamic-slice_convert_fusion = (bf16[24,8,896]{2,1,0:T(8,128)(2,1)S(1)}, bf16[24,8,896]{2,1,0:T(8,128)(2,1)S(1)}) fusion(f32[24,128,896]{2,1,0:T(8,128)} %own_ref.1, s32[]{:T(128)S(6)} %select_n.36, s32[]{:T(128)S(6)} %select_n.34), kind=kLoop, calls=%fused_computation.5 | loop fusion | bytes 1376264 | tf_op jit(solution)/shard_map/convert_element_type | solution.py:36
  2.1 4.2 %collective-permute-start.1 = (bf16[24,8,896]{2,1,0:T(8,128)(2,1)S(1)}, bf16[24,8,896]{2,1,0:T(8,128)(2,1)S(1)}, u32[]{:S(2)}, u32[]{:S(2)}) collective-permute-start(bf16[24,8,896]{2,1,0:T(8,128)(2,1)S(1)} %get-tuple-element.2), channel_id=1, source_target_pairs={{1,0},{2,129},{3,2},{4,131},{5,4},{6,133},{7,6},{8,135},{9,8},{10,... | collective-permute-start | bytes 1032200 | tf_op jit(solution)/shard_map/ppermute | solution.py:41
  6.3 1.9 %collective-permute-start = (bf16[24,8,896]{2,1,0:T(8,128)(2,1)S(1)}, bf16[24,8,896]{2,1,0:T(8,128)(2,1)S(1)}, u32[]{:S(2)}, u32[]{:S(2)}) collective-permute-start(bf16[24,8,896]{2,1,0:T(8,128)(2,1)S(1)} %get-tuple-element.3), channel_id=1, source_target_pairs={{0,1},{1,130},{2,3},{3,132},{4,5},{5,134},{6,7},{7,136},{8,9},{9,1... | collective-permute-start | bytes 1032200 | tf_op jit(solution)/shard_map/ppermute | solution.py:40
  8.2 0.7 %convert_element_type.16 = f32[16]{0:T(128)S(1)} convert(s32[16]{0:T(128)} %param.3) | non-fusion elementwise | flops 16 | bytes 128 | tf_op jit(solution)/shard_map/convert_element_type | solution.py:158
  8.9 0.7 %broadcast_multiply_fusion = (f32[16]{0:T(128)S(1)}, f32[16]{0:T(128)S(1)}, f32[16]{0:T(128)S(1)}) fusion(s32[16]{0:T(128)} %param.3), kind=kLoop, calls=%fused_computation.21 | loop fusion | flops 32 | bytes 256 | tf_op jit(solution)/shard_map/mul | solution.py:60
  9.6 0.1 div.56
  9.7 0.1 div.57
  9.8 0.1 div.60
  9.8 0.1 div.61
  9.9 0.1 broadcast_add_fusion
  10.0 3.8 %fusion.3.b_hbm = bf16[16,7,128,128]{3,2,1,0:T(8,128)(2,1)} fusion(f32[16]{0:T(128)S(1)} %get-tuple-element.5, f32[16]{0:T(128)S(1)} %get-tuple-element.4, f32[7,128,128]{2,1,0:T(8,128)S(1)} %broadcast_add_fusion), kind=kLoop, calls=%fused_computation.4 | loop fusion | flops 14680064 | bytes 4128896 | tf_op jit(solution)/shard_map/convert_element_type | solution.py:61
  13.9 0.8 %fusion.8.f_ref = bf16[384,128]{1,0:T(8,128)(2,1)} fusion(f32[384]{0:T(512)S(1)} %div.61, f32[384]{0:T(512)S(1)} %div.57, f32[24,128]{1,0:T(8,128)S(1)} %iota_subtract_fusion.1, pred[24,128]{1,0:T(8,128)(4,1)S(1)} %fusion.9), kind=kLoop, calls=%fused_computation.14 | loop fusion | flops 442368 | bytes 116736 | tf_op jit(solution)/shard_map/convert_element_type | solution.py:52
  14.7 0.0 collective-permute-done.1.hi_ref
  14.7 0.0 copy-start
  14.7 6.3 %collective-permute-done.lo_ref = bf16[24,8,896]{2,1,0:T(8,128)(2,1)S(1)} collective-permute-done((bf16[24,8,896]{2,1,0:T(8,128)(2,1)S(1)}, bf16[24,8,896]{2,1,0:T(8,128)(2,1)S(1)}, u32[]{:S(2)}, u32[]{:S(2)}) %collective-permute-start) | collective-permute-done | bytes 344096 | tf_op jit(solution)/shard_map/ppermute | solution.py:40
  21.0 0.0 copy-start.1
  21.0 0.0 copy-done
  21.0 0.7 %copy-done.1 = bf16[24,8,896]{2,1,0:T(8,128)(2,1)} copy-done((bf16[24,8,896]{2,1,0:T(8,128)(2,1)}, bf16[24,8,896]{2,1,0:T(8,128)(2,1)S(1)}, u32[]{:S(2)}) %copy-start.1) | copy-done | bytes 344088
  21.8 14.2 %shard_map.41 = (bf16[24,8,896]{2,1,0:T(8,128)(2,1)}, f32[24,8,896]{2,1,0:T(8,128)}) custom-call(s32[1]{0:T(128)} %bitcast.strip_ref, bf16[384,128]{1,0:T(8,128)(2,1)} %fusion.8.f_ref, bf16[24,8,896]{2,1,0:T(8,128)(2,1)} %copy-done.1, f32[24,128,896]{2,1,0:T(8,128)} %own_ref.1, bf16[24,8,896]{2,1,0:T(8,128)(2,1)} %copy-done, ...), custom_call_target="tpu_custom_call" | custom-call | tf_op jit(solution)/shard_map/pallas_call | solution.py:141
  (6 shorter events, 0.1 us)
Async XLA Ops:
  2.1 12.6 %collective-permute-start.1 = (bf16[24,8,896]{2,1,0:T(8,128)(2,1)S(1)}, bf16[24,8,896]{2,1,0:T(8,128)(2,1)S(1)}, u32[]{:S(2)}, u32[]{:S(2)}) collective-permute-start(bf16[24,8,896]{2,1,0:T(8,128)(2,1)S(1)} %get-tuple-element.2), channel_id=1, source_target_pairs={{1,0},{2,129},{3,2},{4,131},{5,4},{6,133},{7,6},{8,135},{9,8},{10,... | collective-permute-start | bytes 1032200 | tf_op jit(solution)/shard_map/ppermute | solution.py:41
  6.3 14.7 %collective-permute-start = (bf16[24,8,896]{2,1,0:T(8,128)(2,1)S(1)}, bf16[24,8,896]{2,1,0:T(8,128)(2,1)S(1)}, u32[]{:S(2)}, u32[]{:S(2)}) collective-permute-start(bf16[24,8,896]{2,1,0:T(8,128)(2,1)S(1)} %get-tuple-element.3), channel_id=1, source_target_pairs={{0,1},{1,130},{2,3},{3,132},{4,5},{5,134},{6,7},{7,136},{8,9},{9,1... | collective-permute-start | bytes 1032200 | tf_op jit(solution)/shard_map/ppermute | solution.py:40
  14.7 6.3 %copy-start = (bf16[24,8,896]{2,1,0:T(8,128)(2,1)}, bf16[24,8,896]{2,1,0:T(8,128)(2,1)S(1)}, u32[]{:S(2)}) copy-start(bf16[24,8,896]{2,1,0:T(8,128)(2,1)S(1)} %collective-permute-done.1.hi_ref) | copy-start | bytes 1032196
  21.0 0.7 %copy-start.1 = (bf16[24,8,896]{2,1,0:T(8,128)(2,1)}, bf16[24,8,896]{2,1,0:T(8,128)(2,1)S(1)}, u32[]{:S(2)}) copy-start(bf16[24,8,896]{2,1,0:T(8,128)(2,1)S(1)} %collective-permute-done.lo_ref) | copy-start | bytes 1032196
